TPU v7x, 512 devices: a whole 4x4x16 slice. The times are simulated.
512 devices in a mesh: node: 64 (over z, x), local: 8 (over y, core).
Axes of the slice: x: 4, y: 4, z: 16, core: 2. Of those that a mesh axis runs over, the one named last changes fastest.
Arguments:
- grad_out: bfloat16 [8192, 7168], P('node', 'local'), may hold values from -6 to 6
- probs: bfloat16 [8192, 8], P('node'), may hold values from 0.099609375 to 2.5
- node_list: int32 [8192, 4], P('node'), may hold values from 0 to 63, all different within a row; in each aligned block of 128 rows (0 to 127, 128 to 255, ...) at most 12 rows name the same one
- weight_down: bfloat16 [128, 1024, 7168], P('node', 'local'), may hold values from -0.1875 to 0.1875
- saved_hidden: bfloat16 [128, 768, 1024], P('node', None, 'local'), may hold values from -0.1875 to 0.1875
Outputs:
- grad_hidden: bfloat16 [128, 768, 1024], P('node', None, 'local')
- grad_probs: float32 [8192, 8], P('node')
Inputs may be any that keep to these rules, and one draw needn't show every extreme that they name: `node_list`: each token lists 4 different nodes. Among the 128 tokens of one index of node, at most 12 list any one node, and some node is listed by exactly 12 of them.
All inputs are finite; a program needn't handle non-finite values.
Results may differ from a plain program's by a relative error of at most 0.001.
Values may be sent and summed in bfloat16 or wider, within the bound.
No kernel may reach another device: no remote copies, remote signals or barrier semaphores. Data moves between devices by JAX's collectives and lax.ppermute only.
A program may use at most 128 MiB of HBM per device.

v0:
```python
import jax
import jax.numpy as jnp
from jax import lax
from jax.sharding import PartitionSpec as P


def gather_slots(source, source_row, slot_valid):
    padded = jnp.concatenate([source, jnp.zeros((1, source.shape[1]), source.dtype)], axis=0)
    index = jnp.where(slot_valid, source_row, source.shape[0])
    return jnp.take(padded, index, axis=0)


def on_device(grad_out, probs, node_list, weight_down, saved_hidden):
    node_count = lax.axis_size("node")
    tok_rows = node_list.shape[0]
    route_count = node_list.shape[1]
    slot_rows = saved_hidden.shape[1]
    capacity = slot_rows // node_count
    expert_count = weight_down.shape[0]
    node_ids = lax.broadcasted_iota(jnp.int32, (tok_rows, route_count, node_count), 2)
    listed = (node_list[:, :, None] == node_ids).astype(jnp.float32)
    member = jnp.sum((node_list[:, :, None] == node_ids).astype(jnp.int32), axis=1)
    arrival = jnp.cumsum(member, axis=0) - member
    positions = lax.broadcasted_iota(jnp.int32, (tok_rows, node_count, capacity), 2)
    select_mask = (arrival[:, :, None] == positions) & (member[:, :, None] == 1)
    select_count = select_mask.astype(jnp.int32)
    token_iota = lax.broadcasted_iota(jnp.int32, (tok_rows, node_count, capacity), 0)
    source_row = jnp.sum(select_count * token_iota, axis=0)
    slot_valid = jnp.sum(select_count, axis=0) > 0
    select_full = select_mask.astype(jnp.float32)
    grouped = probs.reshape(tok_rows, route_count, expert_count).astype(jnp.float32)
    picked = jnp.einsum("tjm,tjc->tmc", listed, grouped, precision=lax.Precision.HIGHEST)
    prob_send = jnp.einsum(
        "tms,tmc->msc", select_full, picked, precision=lax.Precision.HIGHEST
    ).astype(jnp.bfloat16)
    full_rows = lax.all_gather(grad_out, "local", axis=1, tiled=True)
    rows_send = gather_slots(full_rows, source_row, slot_valid)
    rows_in, prob_in = (
        lax.all_to_all(rows_send, "node", split_axis=0, concat_axis=0, tiled=True),
        lax.all_to_all(prob_send, "node", split_axis=0, concat_axis=0, tiled=True),
    )
    hidden_grads = jnp.einsum(
        "rd,ehd->erh",
        rows_in.reshape(slot_rows, -1),
        weight_down,
        preferred_element_type=jnp.float32,
    )
    scales = jnp.transpose(prob_in.reshape(slot_rows, expert_count).astype(jnp.float32))
    grad_hidden = (scales[:, :, None] * hidden_grads).astype(jnp.bfloat16)
    partial_value = jnp.sum(saved_hidden.astype(jnp.float32) * hidden_grads, axis=2)
    partial_value = jnp.transpose(partial_value).reshape(node_count, capacity, expert_count)
    summed = lax.psum(partial_value, "local")
    returned = lax.all_to_all(summed, "node", split_axis=0, concat_axis=0, tiled=True)
    per_node = jnp.einsum("tms,msc->tmc", select_full, returned, precision=lax.Precision.HIGHEST)
    grad_probs = jnp.einsum("tjm,tmc->tjc", listed, per_node, precision=lax.Precision.HIGHEST)
    return (grad_hidden, grad_probs.reshape(tok_rows, route_count * expert_count))


def solution(mesh):
    return jax.shard_map(
        on_device,
        mesh=mesh,
        in_specs=(
            P("node", "local"),
            P("node", None),
            P("node", None),
            P("node", "local", None),
            P("node", None, "local"),
        ),
        out_specs=(P("node", None, "local"), P("node", None)),
        check_vma=False,
    )
```

profile of v0, /device:TPU:1, one launch (start us, length us, event | category | flops | bytes accessed | tf_op | source)
XLA Modules:
  0.0 820.6 jit_solution(14254876430797097274)
XLA Ops:
  7.2 0.0 all-gather.2.cloned.1.call-start
  7.2 0.7 all-gather.2.cloned.1.call-update
  7.9 0.8 copy.55
  8.7 0.3 convert_reduce_fusion.1
  9.0 0.1 copy.57
  9.0 0.2 reduce_window_sum.11
  9.2 0.1 copy.56
  9.3 0.8 copy.58
  10.1 0.3 fusion.6
  10.5 0.1 copy.59
  10.6 1.2 convolution_convert_fusion
  11.8 19.1 %all-to-all-start = ((bf16[64,12,2]{1,2,0:T(2,128)(2,1)}), bf16[64,12,2]{1,2,0:T(2,128)(2,1)S(1)}, u32[]{:S(2)}, u32[]{:S(2)}) async-start(bf16[64,12,2]{1,2,0:T(2,128)(2,1)} %convolution_convert_fusion), calls=%async_computation | async-start | bytes 65536 | tf_op jit(solution)/shard_map/all_to_all | solution.py:40
  30.9 2.2 convert_reduce_fusion
  33.1 0.1 reshape.74
  33.3 15.3 %all-gather.2.cloned.1.call-done = bf16[128,7168]{1,0:T(8,128)(2,1)} async-done(((bf16[128,896]{1,0:T(8,128)(2,1)}), bf16[128,7168]{1,0:T(8,128)(2,1)}) %all-gather.2.cloned.1.call-update) | async-done | bytes 1835024 | tf_op jit(solution)/shard_map/all_gather | solution.py:36
  48.5 1.7 concatenate.3
  50.2 9.5 %gather_fusion = bf16[768,7168]{1,0:T(8,128)(2,1)} fusion(bf16[129,7168]{1,0:T(8,128)(2,1)S(1)} %concatenate.3, s32[1024]{0:T(1024)S(1)} %pad_clamp_fusion), kind=kCustom, calls=%fused_computation | custom fusion | bytes 22023168 | tf_op jit(solution)/shard_map/jit(_take)/gather | solution.py:10
  59.7 15.4 %reshape.73 = bf16[64,12,7168]{2,1,0:T(8,128)(2,1)} reshape(bf16[768,7168]{1,0:T(8,128)(2,1)} %gather_fusion) | data formatting | bytes 22020096 | tf_op jit(solution)/shard_map/jit(_take)/gather | solution.py:10
  75.0 13.6 %broadcast_select_fusion = bf16[64,12,7168]{2,1,0:T(8,128)(2,1)} fusion(bf16[64,12,7168]{2,1,0:T(8,128)(2,1)} %reshape.73, pred[64,12]{1,0:T(8,128)(4,1)S(1)} %compare_and_fusion), kind=kLoop, calls=%fused_computation.1 | loop fusion | flops 5505024 | bytes 22020864 | tf_op jit(solution)/shard_map/jit(_take)/select_n | solution.py:10
  88.7 0.0 copy-start
  88.7 0.0 all-to-all-done
  88.7 15.8 %all-to-all-start.1 = ((bf16[64,12,7168]{2,1,0:T(8,128)(2,1)}), bf16[64,12,7168]{2,1,0:T(8,128)(2,1)}, u32[]{:S(2)}, u32[]{:S(2)}) async-start(bf16[64,12,7168]{2,1,0:T(8,128)(2,1)} %broadcast_select_fusion), calls=%async_computation.1 | async-start | bytes 29360128 | tf_op jit(solution)/shard_map/all_to_all | solution.py:39
  104.5 0.0 copy-done
  104.5 0.2 copy.62
  104.7 0.1 copy.60
  104.8 0.1 copy.61
  104.9 0.1 reshape.71
  105.0 627.0 %all-to-all-done.1 = bf16[64,12,7168]{2,1,0:T(8,128)(2,1)} async-done(((bf16[64,12,7168]{2,1,0:T(8,128)(2,1)}), bf16[64,12,7168]{2,1,0:T(8,128)(2,1)}, u32[]{:S(2)}, u32[]{:S(2)}) %all-to-all-start.1) | async-done | bytes 11010080 | tf_op jit(solution)/shard_map/all_to_all | solution.py:39
  732.0 15.9 %reshape.81 = bf16[768,7168,1]{1,0,2:T(8,128)(2,1)} reshape(bf16[64,12,7168]{2,1,0:T(8,128)(2,1)} %all-to-all-done.1) | data formatting | bytes 22020096 | tf_op jit(solution)/shard_map/reshape | solution.py:44
  747.9 8.2 %multiply_reduce_fusion = (f32[2,768]{1,0:T(2,128)S(1)}, bf16[2,768,128]{1,2,0:T(8,128)(2,1)S(1)}) fusion(bf16[2,768,128]{1,2,0:T(8,128)(2,1)S(1)} %copy.62, f32[2,768]{1,0:T(2,128)S(1)} %bitcast.22, bf16[768,7168,1]{1,0,2:T(8,128)(2,1)} %reshape.81, bf16[2,128,7168]{2,1,0:T(8,128)(2,1)} %param.8), kind=kOutput, calls=%fused_computation.5 | convolution fusion | flops 2819553792 | bytes 15478784 | tf_op jit(solution)/shard_map/rd,ehd->erh/dot_general | solution.py:42
  756.2 0.1 reshape.69
  756.3 26.2 %psum.7 = f32[64,12,2]{1,0,2:T(8,128)S(1)} all-reduce(f32[64,12,2]{1,0,2:T(8,128)S(1)} %reshape.69), channel_id=1, replica_groups=mesh['node'=64,'local'=8] {'local'}, use_global_device_ids=true, to_apply=%region_5.6 | all-reduce | flops 1536 | bytes 12288 | tf_op jit(solution)/shard_map/psum | solution.py:52
  782.5 0.7 copy.63
  783.2 14.7 %all-to-all-start.2 = ((f32[64,12,2]{1,2,0:T(2,128)}), f32[64,12,2]{1,2,0:T(2,128)S(1)}, u32[]{:S(2)}, u32[]{:S(2)}) async-start(f32[64,12,2]{1,2,0:T(2,128)} %copy.63), calls=%async_computation.2 | async-start | bytes 131072 | tf_op jit(solution)/shard_map/all_to_all | solution.py:53
  797.9 0.9 copy.66
  798.8 13.1 %all-to-all-done.2 = f32[64,12,2]{1,2,0:T(2,128)S(1)} async-done(((f32[64,12,2]{1,2,0:T(2,128)}), f32[64,12,2]{1,2,0:T(2,128)S(1)}, u32[]{:S(2)}, u32[]{:S(2)}) %all-to-all-start.2) | async-done | bytes 6176 | tf_op jit(solution)/shard_map/all_to_all | solution.py:53
  811.9 0.4 convolution_bitcast_fusion.1
  812.3 0.1 copy.64
  812.4 0.6 fusion.5
  813.1 0.7 copy.65
  (5 shorter events, 0.1 us)
Async XLA Ops:
  7.2 41.4 %all-gather.2.cloned.1.call-start = ((), (), s32[]{:S(2)}) async-start(), calls=%async_computation.3 | async-start | bytes 2064384 | tf_op jit(solution)/shard_map/all_gather | solution.py:36
  11.8 76.9 %all-to-all-start = ((bf16[64,12,2]{1,2,0:T(2,128)(2,1)}), bf16[64,12,2]{1,2,0:T(2,128)(2,1)S(1)}, u32[]{:S(2)}, u32[]{:S(2)}) async-start(bf16[64,12,2]{1,2,0:T(2,128)(2,1)} %convolution_convert_fusion), calls=%async_computation | async-start | bytes 65536 | tf_op jit(solution)/shard_map/all_to_all | solution.py:40
  88.7 15.8 %copy-start = (bf16[2,768,128]{2,1,0:T(8,128)(2,1)S(1)}, bf16[2,768,128]{2,1,0:T(8,128)(2,1)}, u32[]{:S(2)}) copy-start(bf16[2,768,128]{2,1,0:T(8,128)(2,1)} %param.9) | copy-start | bytes 1179652
  88.7 643.4 %all-to-all-start.1 = ((bf16[64,12,7168]{2,1,0:T(8,128)(2,1)}), bf16[64,12,7168]{2,1,0:T(8,128)(2,1)}, u32[]{:S(2)}, u32[]{:S(2)}) async-start(bf16[64,12,7168]{2,1,0:T(8,128)(2,1)} %broadcast_select_fusion), calls=%async_computation.1 | async-start | bytes 29360128 | tf_op jit(solution)/shard_map/all_to_all | solution.py:39
  783.2 28.7 %all-to-all-start.2 = ((f32[64,12,2]{1,2,0:T(2,128)}), f32[64,12,2]{1,2,0:T(2,128)S(1)}, u32[]{:S(2)}, u32[]{:S(2)}) async-start(f32[64,12,2]{1,2,0:T(2,128)} %copy.63), calls=%async_computation.2 | async-start | bytes 131072 | tf_op jit(solution)/shard_map/all_to_all | solution.py:53
Sparse Core Ops, SparseCore 0:
  10.1 38.3 all-gather.1
where the time goes:
time: 824 us; the launch traced here: 821 us
  waiting for transfers between devices  656 us (80%)
  starting transfers between devices  49.6 us (6%)
  local copies, waits for them, and re-layouts  47.3 us (6%)
  blocking collectives  26.2 us (3%)
  other arithmetic  16.3 us (2%)
  between operations  14.2 us (2%)
  matrix products  10.8 us (1%)
    all_to_all x1, waiting for transfers between devices, on_device(): lax.all_to_all(rows_send, 'node', split_axis=0, concat_axis=0, tiled=True)  627 us
    psum x1, blocking collectives, on_device(): summed = lax.psum(partial_value, 'local')  26.2 us
    gather x2, local copies, waits for them, and re-layouts, gather_slots(): return jnp.take(padded, index, axis=0)  24.8 us
    all_to_all x1, starting transfers between devices, on_device(): lax.all_to_all(prob_send, 'node', split_axis=0, concat_axis=0, tiled=True)  19.1 us
  transfers between devices with their start and end apart: 4, of which 3 were waited for; matrix products, arithmetic and copies ran while one was open for 6% of the time, Pallas kernels for 0%

commit v1 on v0

--- a/solution.py
+++ b/solution.py
@@ -33,16 +33,27 @@
     prob_send = jnp.einsum(
         "tms,tmc->msc", select_full, picked, precision=lax.Precision.HIGHEST
     ).astype(jnp.bfloat16)
-    full_rows = lax.all_gather(grad_out, "local", axis=1, tiled=True)
-    rows_send = gather_slots(full_rows, source_row, slot_valid)
-    rows_in, prob_in = (
-        lax.all_to_all(rows_send, "node", split_axis=0, concat_axis=0, tiled=True),
-        lax.all_to_all(prob_send, "node", split_axis=0, concat_axis=0, tiled=True),
+    rows_send = gather_slots(grad_out, source_row, slot_valid)
+    width = grad_out.shape[1]
+    payload = jnp.concatenate(
+        [
+            rows_send.reshape(node_count, capacity * width),
+            prob_send.reshape(node_count, capacity * expert_count),
+        ],
+        axis=1,
+    )
+    payload_in = lax.all_to_all(payload, "node", split_axis=0, concat_axis=0, tiled=True)
+    rows_in = payload_in[:, : capacity * width].reshape(slot_rows, width)
+    prob_in = payload_in[:, capacity * width :]
+    full_rows = lax.all_gather(rows_in, "local", axis=0, tiled=False)
+    local_count = full_rows.shape[0]
+    weight_split = weight_down.reshape(
+        expert_count, weight_down.shape[1], local_count, width
     )
     hidden_grads = jnp.einsum(
-        "rd,ehd->erh",
-        rows_in.reshape(slot_rows, -1),
-        weight_down,
+        "lrd,ehld->erh",
+        full_rows,
+        weight_split,
         preferred_element_type=jnp.float32,
     )
     scales = jnp.transpose(prob_in.reshape(slot_rows, expert_count).astype(jnp.float32))

time: 824 us -> 256 us (0.31)
  waiting for transfers between devices: 656 us -> 76.6 us
  blocking collectives: 26.2 us -> 107 us
  starting transfers between devices: 49.6 us -> 15.6 us
  local copies, waits for them, and re-layouts: 47.3 us -> 23.4 us
  other arithmetic: 16.3 us -> 5.51 us
    all_to_all x2 -> x0, waiting for transfers between devices: 627 us -> none  [the longest x1 627 us: on_device(): lax.all_to_all(rows_send, 'node', split_axis=0, concat_axis=0, tiled=True)]
    all_to_all x0 -> x1, blocking collectives: none -> 86 us  [on_device(): lax.all_to_all(payload, 'node', split_axis=0, concat_axis=0, tiled=True)]
    all_gather x1, waiting for transfers between devices: 15.3 us -> 63.5 us  [on_device(): full_rows = lax.all_gather(rows_in, 'local', axis=0, tiled=False)]
    all_to_all x2 -> x0, starting transfers between devices: 34.9 us -> none  [the longest x1 19.1 us: on_device(): lax.all_to_all(prob_send, 'node', split_axis=0, concat_axis=0, tiled=True)]
    gather x2, local copies, waits for them, and re-layouts: 24.8 us -> 3.16 us  [gather_slots(): return jnp.take(padded, index, axis=0)]
    reshape x1, local copies, waits for them, and re-layouts: 15.9 us -> 0.1 us  [on_device(): prob_send.reshape(node_count, capacity * expert_count)]
    select_n x2, other arithmetic: 13.6 us -> 0.31 us  [gather_slots(): return jnp.take(padded, index, axis=0)]
    unnamed x5 -> x13, local copies, waits for them, and re-layouts: 1.89 us -> 13.3 us
  transfers between devices with their start and end apart: 4 -> 2, of which waited for: 3 -> 2; matrix products, arithmetic and copies ran while one was open for 6% -> 1% of each run, Pallas kernels for 0% -> 0%
where the time goes in v1:
time: 256 us; the launch traced here: 253 us
  blocking collectives  107 us (42%)
  waiting for transfers between devices  76.6 us (30%)
  local copies, waits for them, and re-layouts  23.4 us (9%)
  starting transfers between devices  15.6 us (6%)
  between operations  14.3 us (6%)
  matrix products  10.2 us (4%)
  other arithmetic  5.51 us (2%)
    all_to_all x1, blocking collectives, on_device(): lax.all_to_all(payload, 'node', split_axis=0, concat_axis=0, tiled=True)  86 us
    all_gather x1, waiting for transfers between devices, on_device(): full_rows = lax.all_gather(rows_in, 'local', axis=0, tiled=False)  63.5 us
    psum x1, blocking collectives, on_device(): summed = lax.psum(partial_value, 'local')  21.3 us
    all_to_all x1, starting transfers between devices, on_device(): lax.all_to_all(summed, 'node', split_axis=0, concat_axis=0, tiled=True)  15.6 us
    unnamed x13, local copies, waits for them, and re-layouts  13.3 us
    all_to_all x1, waiting for transfers between devices, on_device(): lax.all_to_all(summed, 'node', split_axis=0, concat_axis=0, tiled=True)  13.1 us
    dot_general x1, matrix products, on_device(): jnp.einsum('lrd,ehld->erh', full_rows, weight_split, preferred_element_ty...  8.23 us
  transfers between devices with their start and end apart: 2, of which 2 were waited for; matrix products, arithmetic and copies ran while one was open for 1% of the time, Pallas kernels for 0%

profile of v1, /device:TPU:1, one launch (start us, length us, event | category | flops | bytes accessed | tf_op | source)
XLA Modules:
  0.0 252.9 jit_solution(3523019031387411221)
XLA Ops:
  7.2 0.0 copy-start.2
  7.2 0.0 all-gather.2.cloned.1.call-start
  7.2 0.8 copy.69
  8.1 0.3 convert_reduce_fusion.1
  8.3 0.1 copy.71
  8.4 0.2 reduce_window_sum.11
  8.6 0.1 copy.70
  8.7 2.2 convert_reduce_fusion
  11.0 0.8 copy.72
  11.8 0.3 fusion.15
  12.1 0.1 copy.73
  12.2 0.6 convolution_convert_fusion
  12.8 0.1 copy.74
  12.9 0.1 copy.75
  13.0 0.1 reshape.85
  13.1 0.0 copy-done.2
  13.2 2.8 %gather_fusion = bf16[768,896]{1,0:T(8,128)(2,1)S(1)} fusion(bf16[129,896]{1,0:T(8,128)(2,1)S(1)} %concatenate.6, s32[1024]{0:T(1024)S(1)} %pad_clamp_fusion), kind=kCustom, calls=%fused_computation | custom fusion | bytes 2755584 | tf_op jit(solution)/shard_map/jit(_take)/gather | solution.py:10
  16.0 0.3 reshape.84
  16.3 0.3 broadcast_select_fusion
  16.6 0.3 copy.87
  16.9 0.1 maximum_bitcast_fusion
  17.0 0.5 broadcast.68
  17.5 1.6 reduce
  19.2 1.5 reshape.94
  20.7 86.0 %all_to_all.17 = bf16[64,2,5388]{2,1,0:T(2,128)(2,1)} all-to-all(bf16[64,2,5388]{2,1,0:T(2,128)(2,1)S(1)} %reshape.94), channel_id=1, replica_groups=mesh['node'=64,'local'=8] {'node'}, dimensions={0} | all-to-all | bytes 2758656 | tf_op jit(solution)/shard_map/all_to_all | solution.py:45
  106.7 8.4 %reshape.95 = bf16[64,1,10776]{2,1,0:T(2,128)(2,1)S(1)} reshape(bf16[64,2,5388]{2,1,0:T(2,128)(2,1)} %all_to_all.17) | data formatting | bytes 2758656
  115.1 0.2 copy.97
  115.3 0.0 copy-start
  115.3 1.1 copy-done
  116.4 0.1 slice.11
  116.5 0.0 copy-start.1
  116.5 3.1 %all_gather_reshape.3 = bf16[1,768,896]{2,1,0:T(8,128)(2,1)} reshape(bf16[64,10752]{1,0:T(8,128)(2,1)S(1)} %slice.11) | data formatting | bytes 2752512 | tf_op jit(solution)/shard_map/all_gather;reshape | solution.py:48
  119.5 0.0 all-gather.2.cloned.1.call-update
  119.6 0.0 copy-done.1
  119.6 0.2 copy.79
  119.8 0.7 slice_convert_fusion
  120.5 0.2 reshape.82
  120.6 0.1 copy.77
  120.8 63.5 %all-gather.2.cloned.1.call-done = bf16[8,768,896]{2,1,0:T(8,128)(2,1)} async-done(((bf16[1,768,896]{2,1,0:T(8,128)(2,1)}), bf16[8,768,896]{2,1,0:T(8,128)(2,1)}) %all-gather.2.cloned.1.call-update) | async-done | bytes 11010064 | tf_op jit(solution)/shard_map/all_gather | solution.py:48
  184.3 8.2 %multiply_reduce_fusion = (f32[2,768]{1,0:T(2,128)S(1)}, bf16[2,768,128]{1,2,0:T(8,128)(2,1)S(1)}) fusion(bf16[2,768,128]{1,2,0:T(8,128)(2,1)S(1)} %copy.79, f32[2,768]{1,0:T(2,128)S(1)} %copy.77, bf16[2,16,8,8,896]{4,3,2,1,0:T(8,128)(2,1)} %bitcast.53, bf16[8,768,896]{2,1,0:T(8,128)(2,1)} %all-gather.2.cloned.1.call-done), kind=kOutput, calls=%fused_computation.11 | convolution fusion | flops 2819553792 | bytes 15478784 | tf_op jit(solution)/shard_map/lrd,ehld->erh/dot_general | solution.py:53
  192.5 0.1 reshape.80
  192.7 21.3 %psum.7 = f32[64,12,2]{1,0,2:T(8,128)S(1)} all-reduce(f32[64,12,2]{1,0,2:T(8,128)S(1)} %reshape.80), channel_id=1, replica_groups=mesh['node'=64,'local'=8] {'local'}, use_global_device_ids=true, to_apply=%region_5.6 | all-reduce | flops 1536 | bytes 12288 | tf_op jit(solution)/shard_map/psum | solution.py:63
  213.9 0.7 copy.80
  214.6 15.6 %all-to-all-start.1 = ((f32[64,12,2]{1,2,0:T(2,128)}), f32[64,12,2]{1,2,0:T(2,128)S(1)}, u32[]{:S(2)}, u32[]{:S(2)}) async-start(f32[64,12,2]{1,2,0:T(2,128)} %copy.80), calls=%async_computation.1 | async-start | bytes 131072 | tf_op jit(solution)/shard_map/all_to_all | solution.py:64
  230.2 0.9 copy.83
  231.1 13.1 %all-to-all-done.1 = f32[64,12,2]{1,2,0:T(2,128)S(1)} async-done(((f32[64,12,2]{1,2,0:T(2,128)}), f32[64,12,2]{1,2,0:T(2,128)S(1)}, u32[]{:S(2)}, u32[]{:S(2)}) %all-to-all-start.1) | async-done | bytes 6176 | tf_op jit(solution)/shard_map/all_to_all | solution.py:64
  244.2 0.4 convolution_bitcast_fusion
  244.6 0.1 copy.81
  244.7 0.6 fusion.14
  245.4 0.7 copy.82
  (6 shorter events, 0.1 us)
Async XLA Ops:
  7.2 6.0 %copy-start.2 = (bf16[128,896]{1,0:T(8,128)(2,1)S(1)}, bf16[128,896]{1,0:T(8,128)(2,1)}, u32[]{:S(2)}) copy-start(bf16[128,896]{1,0:T(8,128)(2,1)} %param.5) | copy-start | bytes 688132
  7.2 177.1 %all-gather.2.cloned.1.call-start = ((), (), s32[]{:S(2)}) async-start(), calls=%async_computation.2 | async-start | bytes 12386304 | tf_op jit(solution)/shard_map/all_gather | solution.py:48
  115.3 1.1 copy-start
  116.5 3.1 %copy-start.1 = (bf16[2,768,128]{2,1,0:T(8,128)(2,1)S(1)}, bf16[2,768,128]{2,1,0:T(8,128)(2,1)}, u32[]{:S(2)}) copy-start(bf16[2,768,128]{2,1,0:T(8,128)(2,1)} %param.9) | copy-start | bytes 1179652
  214.6 29.6 %all-to-all-start.1 = ((f32[64,12,2]{1,2,0:T(2,128)}), f32[64,12,2]{1,2,0:T(2,128)S(1)}, u32[]{:S(2)}, u32[]{:S(2)}) async-start(f32[64,12,2]{1,2,0:T(2,128)} %copy.80), calls=%async_computation.1 | async-start | bytes 131072 | tf_op jit(solution)/shard_map/all_to_all | solution.py:64
Sparse Core Ops, SparseCore 0:
  119.7 64.5 all-gather.1

commit v2 on v1

--- a/solution.py
+++ b/solution.py
@@ -60,8 +60,11 @@
     grad_hidden = (scales[:, :, None] * hidden_grads).astype(jnp.bfloat16)
     partial_value = jnp.sum(saved_hidden.astype(jnp.float32) * hidden_grads, axis=2)
     partial_value = jnp.transpose(partial_value).reshape(node_count, capacity, expert_count)
-    summed = lax.psum(partial_value, "local")
-    returned = lax.all_to_all(summed, "node", split_axis=0, concat_axis=0, tiled=True)
+    local_count = lax.axis_size("local")
+    gathered = lax.all_gather(partial_value, ("node", "local"), axis=0, tiled=False)
+    gathered = gathered.reshape(node_count, local_count, node_count, capacity, expert_count)
+    mine = lax.dynamic_index_in_dim(gathered, lax.axis_index("node"), axis=2, keepdims=False)
+    returned = jnp.sum(mine, axis=1)
     per_node = jnp.einsum("tms,msc->tmc", select_full, returned, precision=lax.Precision.HIGHEST)
     grad_probs = jnp.einsum("tjm,tmc->tjc", listed, per_node, precision=lax.Precision.HIGHEST)
     return (grad_hidden, grad_probs.reshape(tok_rows, route_count * expert_count))

time: 256 us -> 414 us (1.62)
  waiting for transfers between devices: 76.6 us -> 263 us
  blocking collectives: 107 us -> 86 us
  starting transfers between devices: 15.6 us -> 0.26 us
  other arithmetic: 5.51 us -> 16 us
    all_gather x0 -> x1, waiting for transfers between devices: none -> 200 us  [on_device(): lax.all_gather(partial_value, ('node', 'local'), axis=0, tiled=False)]
    psum x1 -> x0, blocking collectives: 21.3 us -> none  [on_device(): summed = lax.psum(partial_value, 'local')]
    all_to_all x1 -> x0, starting transfers between devices: 15.6 us -> none  [on_device(): lax.all_to_all(summed, 'node', split_axis=0, concat_axis=0, tiled=True)]
    all_to_all x1 -> x0, waiting for transfers between devices: 13.1 us -> none  [on_device(): lax.all_to_all(summed, 'node', split_axis=0, concat_axis=0, tiled=True)]
    unnamed x0 -> x1, other arithmetic: none -> 10.5 us
where the time goes in v2:
time: 414 us
  waiting for transfers between devices  263 us (64%)
  blocking collectives  86 us (21%)
  local copies, waits for them, and re-layouts  23.4 us (6%)
  other arithmetic  16 us (4%)
  between operations  14.3 us (3%)
  matrix products  10.4 us (3%)
    all_gather x1, waiting for transfers between devices, on_device(): lax.all_gather(partial_value, ('node', 'local'), axis=0, tiled=False)  200 us
    all_to_all x1, blocking collectives, on_device(): lax.all_to_all(payload, 'node', split_axis=0, concat_axis=0, tiled=True)  86 us
    all_gather x1, waiting for transfers between devices, on_device(): full_rows = lax.all_gather(rows_in, 'local', axis=0, tiled=False)  63.4 us
    unnamed x13, local copies, waits for them, and re-layouts  13.3 us
    unnamed x1, other arithmetic  10.5 us
  transfers between devices with their start and end apart: 2, of which 2 were waited for; matrix products, arithmetic and copies ran while one was open for 1% of the time, Pallas kernels for 0%

profile of v2, /device:TPU:1, one launch (start us, length us, event | category | flops | bytes accessed | tf_op | source)
XLA Modules:
  0.0 413.6 jit_solution(9159798869020528608)
XLA Ops:
  7.2 0.0 copy-start.2
  7.2 0.0 all-gather.3.cloned.1.call-start
  7.2 0.8 copy.72
  8.1 0.3 convert_reduce_fusion.1
  8.3 0.1 copy.74
  8.4 0.2 reduce_window_sum.11
  8.6 0.1 copy.73
  8.7 2.2 convert_reduce_fusion
  11.0 0.8 copy.75
  11.8 0.3 fusion.15
  12.1 0.1 copy.76
  12.2 0.6 convolution_convert_fusion
  12.8 0.1 copy.77
  12.9 0.1 copy.78
  13.0 0.1 reshape.85
  13.1 0.0 copy-done.2
  13.2 2.8 gather_fusion
  16.0 0.3 reshape.84
  16.3 0.3 broadcast_select_fusion
  16.6 0.3 copy.93
  16.9 0.1 maximum_bitcast_fusion
  17.0 0.5 broadcast.68
  17.5 1.6 reduce.1
  19.2 1.5 reshape.94
  20.7 86.0 %all_to_all.12 = bf16[64,2,5388]{2,1,0:T(2,128)(2,1)} all-to-all(bf16[64,2,5388]{2,1,0:T(2,128)(2,1)S(1)} %reshape.94), channel_id=1, replica_groups=mesh['node'=64,'local'=8] {'node'}, dimensions={0} | all-to-all | bytes 2758656 | tf_op jit(solution)/shard_map/all_to_all | solution.py:45
  106.6 8.4 %reshape.95 = bf16[64,1,10776]{2,1,0:T(2,128)(2,1)S(1)} reshape(bf16[64,2,5388]{2,1,0:T(2,128)(2,1)} %all_to_all.12) | data formatting | bytes 2758656
  115.0 0.2 copy.103
  115.2 0.0 copy-start
  115.2 1.1 copy-done
  116.3 0.1 slice.11
  116.4 0.0 copy-start.1
  116.4 3.1 all_gather_reshape.6
  119.4 0.0 all-gather.3.cloned.1.call-update
  119.5 0.2 all-gather.5.cloned.1.call-start
  119.7 0.0 copy-done.1
  119.7 0.2 copy.82
  119.9 0.7 slice_convert_fusion
  120.6 0.2 reshape.82
  120.8 0.1 copy.80
  120.9 63.4 %all-gather.3.cloned.1.call-done = bf16[8,768,896]{2,1,0:T(8,128)(2,1)} async-done(((bf16[1,768,896]{2,1,0:T(8,128)(2,1)}), bf16[8,768,896]{2,1,0:T(8,128)(2,1)}) %all-gather.3.cloned.1.call-update) | async-done | bytes 11010064 | tf_op jit(solution)/shard_map/all_gather | solution.py:48
  184.3 8.2 %multiply_reduce_fusion = (f32[2,768]{1,0:T(2,128)S(1)}, bf16[2,768,128]{1,2,0:T(8,128)(2,1)S(1)}) fusion(bf16[2,768,128]{1,2,0:T(8,128)(2,1)S(1)} %copy.82, f32[2,768]{1,0:T(2,128)S(1)} %copy.80, bf16[2,16,8,8,896]{4,3,2,1,0:T(8,128)(2,1)} %bitcast.55, bf16[8,768,896]{2,1,0:T(8,128)(2,1)} %all-gather.3.cloned.1.call-done), kind=kOutput, calls=%fused_computation.12 | convolution fusion | flops 2819553792 | bytes 15478784 | tf_op jit(solution)/shard_map/lrd,ehld->erh/dot_general | solution.py:53
  192.5 0.1 all_gather_reshape.7
  192.7 0.7 copy.83
  193.3 0.0 all-gather.5.cloned.1.call-update
  193.4 0.9 copy.87
  194.3 199.9 %all-gather.5.cloned.1.call-done = f32[512,64,12,2]{1,3,2,0:T(2,128)} async-done(((f32[1,64,12,2]{1,3,2,0:T(2,128)}), f32[512,64,12,2]{1,3,2,0:T(2,128)}) %all-gather.5.cloned.1.call-update) | async-done | bytes 3145744 | tf_op jit(solution)/shard_map/all_gather | solution.py:64
  394.2 10.5 %dynamic-slice_reduce_fusion = f32[64,12,2]{2,1,0:T(8,128)S(1)} fusion(f32[64,8,64,12,2]{2,4,3,1,0:T(2,128)} %bitcast.46, s32[]{:T(128)S(6)} %select_n.50), kind=kLoop, calls=%fused_computation.3 | loop fusion | flops 10752 | bytes 55300
  404.7 0.6 convolution_bitcast_fusion
  405.3 0.1 copy.85
  405.4 0.6 fusion.14
  406.1 0.7 copy.86
  (6 shorter events, 0.1 us)
Async XLA Ops:
  7.2 6.0 %copy-start.2 = (bf16[128,896]{1,0:T(8,128)(2,1)S(1)}, bf16[128,896]{1,0:T(8,128)(2,1)}, u32[]{:S(2)}) copy-start(bf16[128,896]{1,0:T(8,128)(2,1)} %param.5) | copy-start | bytes 688132
  7.2 177.1 %all-gather.3.cloned.1.call-start = ((), (), s32[]{:S(2)}) async-start(), calls=%async_computation.1 | async-start | bytes 12386304 | tf_op jit(solution)/shard_map/all_gather | solution.py:48
  115.2 1.1 copy-start
  116.4 3.3 copy-start.1
  119.5 274.8 %all-gather.5.cloned.1.call-start = ((), (), s32[]{:S(2)}) async-start(), calls=%async_computation.2 | async-start | bytes 6303744 | tf_op jit(solution)/shard_map/all_gather | solution.py:64
Sparse Core Ops, SparseCore 0:
  119.6 64.6 all-gather.2
  193.5 200.7 all-gather.4

commit v3 on v1

--- a/solution.py
+++ b/solution.py
@@ -60,7 +60,7 @@
     grad_hidden = (scales[:, :, None] * hidden_grads).astype(jnp.bfloat16)
     partial_value = jnp.sum(saved_hidden.astype(jnp.float32) * hidden_grads, axis=2)
     partial_value = jnp.transpose(partial_value).reshape(node_count, capacity, expert_count)
-    summed = lax.psum(partial_value, "local")
+    summed = jnp.sum(lax.all_gather(partial_value, "local", axis=0, tiled=False), axis=0)
     returned = lax.all_to_all(summed, "node", split_axis=0, concat_axis=0, tiled=True)
     per_node = jnp.einsum("tms,msc->tmc", select_full, returned, precision=lax.Precision.HIGHEST)
     grad_probs = jnp.einsum("tjm,tmc->tjc", listed, per_node, precision=lax.Precision.HIGHEST)

time: 256 us -> 245 us (0.957); the launches traced: 253 us -> 245 us
  blocking collectives: 107 us -> 98.8 us
    psum x1 -> x0, blocking collectives: 21.3 us -> none  [on_device(): summed = lax.psum(partial_value, 'local')]
    all_gather x0 -> x1, blocking collectives: none -> 12.8 us  [on_device(): lax.all_gather(partial_value, 'local', axis=0, tiled=False)]
where the time goes in v3:
time: 245 us
  blocking collectives  98.8 us (40%)
  waiting for transfers between devices  76.8 us (31%)
  local copies, waits for them, and re-layouts  23.5 us (10%)
  starting transfers between devices  15.4 us (6%)
  between operations  14.3 us (6%)
  matrix products  10.2 us (4%)
  other arithmetic  5.56 us (2%)
    all_to_all x1, blocking collectives, on_device(): lax.all_to_all(payload, 'node', split_axis=0, concat_axis=0, tiled=True)  86 us
    all_gather x1, waiting for transfers between devices, on_device(): full_rows = lax.all_gather(rows_in, 'local', axis=0, tiled=False)  63.5 us
    all_to_all x1, starting transfers between devices, on_device(): lax.all_to_all(summed, 'node', split_axis=0, concat_axis=0, tiled=True)  15.3 us
    unnamed x13, local copies, waits for them, and re-layouts  13.3 us
    all_to_all x1, waiting for transfers between devices, on_device(): lax.all_to_all(summed, 'node', split_axis=0, concat_axis=0, tiled=True)  13.2 us
    all_gather x1, blocking collectives, on_device(): lax.all_gather(partial_value, 'local', axis=0, tiled=False)  12.8 us
    dot_general x1, matrix products, on_device(): jnp.einsum('lrd,ehld->erh', full_rows, weight_split, preferred_element_ty...  8.23 us
  transfers between devices with their start and end apart: 2, of which 2 were waited for; matrix products, arithmetic and copies ran while one was open for 1% of the time, Pallas kernels for 0%

profile of v3, /device:TPU:1, one launch (start us, length us, event | category | flops | bytes accessed | tf_op | source)
XLA Modules:
  0.0 244.5 jit_solution(12758288892406756569)
XLA Ops:
  7.2 0.0 copy-start.2
  7.2 0.0 all-gather.2.cloned.1.call-start
  7.2 0.8 copy.75
  8.1 0.3 convert_reduce_fusion.1
  8.3 0.1 copy.77
  8.4 0.2 reduce_window_sum.11
  8.6 0.1 copy.76
  8.7 2.2 convert_reduce_fusion
  11.0 0.8 copy.78
  11.8 0.3 fusion.15
  12.1 0.1 copy.79
  12.2 0.6 convolution_convert_fusion
  12.8 0.1 copy.80
  12.9 0.1 copy.81
  13.0 0.1 reshape.81
  13.1 0.0 copy-done.2
  13.2 2.8 %gather_fusion = bf16[768,896]{1,0:T(8,128)(2,1)S(1)} fusion(bf16[129,896]{1,0:T(8,128)(2,1)S(1)} %concatenate.6, s32[1024]{0:T(1024)S(1)} %pad_clamp_fusion), kind=kCustom, calls=%fused_computation | custom fusion | bytes 2755584 | tf_op jit(solution)/shard_map/jit(_take)/gather | solution.py:10
  16.0 0.3 reshape.80
  16.3 0.3 broadcast_select_fusion
  16.6 0.3 copy.97
  16.9 0.1 maximum_bitcast_fusion
  17.0 0.5 broadcast.68
  17.5 1.6 reduce
  19.2 1.5 reshape.90
  20.7 86.0 %all_to_all.17 = bf16[64,2,5388]{2,1,0:T(2,128)(2,1)} all-to-all(bf16[64,2,5388]{2,1,0:T(2,128)(2,1)S(1)} %reshape.90), channel_id=1, replica_groups=mesh['node'=64,'local'=8] {'node'}, dimensions={0} | all-to-all | bytes 2758656 | tf_op jit(solution)/shard_map/all_to_all | solution.py:45
  106.7 8.4 %reshape.91 = bf16[64,1,10776]{2,1,0:T(2,128)(2,1)S(1)} reshape(bf16[64,2,5388]{2,1,0:T(2,128)(2,1)} %all_to_all.17) | data formatting | bytes 2758656
  115.1 0.2 copy.107
  115.3 0.0 copy-start
  115.3 1.1 copy-done
  116.4 0.1 slice.11
  116.5 0.0 copy-start.1
  116.5 3.1 %all_gather_reshape.6 = bf16[1,768,896]{2,1,0:T(8,128)(2,1)} reshape(bf16[64,10752]{1,0:T(8,128)(2,1)S(1)} %slice.11) | data formatting | bytes 2752512 | tf_op jit(solution)/shard_map/all_gather;reshape | solution.py:48
  119.5 0.0 all-gather.2.cloned.1.call-update
  119.6 0.0 copy-done.1
  119.6 0.2 copy.85
  119.8 0.7 slice_convert_fusion
  120.5 0.2 reshape.78
  120.6 0.1 copy.83
  120.8 63.5 %all-gather.2.cloned.1.call-done = bf16[8,768,896]{2,1,0:T(8,128)(2,1)} async-done(((bf16[1,768,896]{2,1,0:T(8,128)(2,1)}), bf16[8,768,896]{2,1,0:T(8,128)(2,1)}) %all-gather.2.cloned.1.call-update) | async-done | bytes 11010064 | tf_op jit(solution)/shard_map/all_gather | solution.py:48
  184.3 8.2 %multiply_reduce_fusion = (f32[2,768]{1,0:T(2,128)S(1)}, bf16[2,768,128]{1,2,0:T(8,128)(2,1)S(1)}) fusion(bf16[2,768,128]{1,2,0:T(8,128)(2,1)S(1)} %copy.85, f32[2,768]{1,0:T(2,128)S(1)} %copy.83, bf16[2,16,8,8,896]{4,3,2,1,0:T(8,128)(2,1)} %bitcast.53, bf16[8,768,896]{2,1,0:T(8,128)(2,1)} %all-gather.2.cloned.1.call-done), kind=kOutput, calls=%fused_computation.11 | convolution fusion | flops 2819553792 | bytes 15478784 | tf_op jit(solution)/shard_map/lrd,ehld->erh/dot_general | solution.py:53
  192.5 0.1 all_gather_reshape.7
  192.7 0.1 copy.86
  192.7 12.8 %all_gather.7 = f32[8,64,12,2]{1,3,2,0:T(2,128)S(1)} all-gather(f32[1,64,12,2]{1,3,2,0:T(2,128)S(1)} %copy.86), channel_id=1, replica_groups=mesh['node'=64,'local'=8] {'local'}, dimensions={0}, use_global_device_ids=true | all-gather | bytes 55296 | tf_op jit(solution)/shard_map/all_gather | solution.py:63
  205.5 0.1 reduce_sum.49
  205.6 0.7 copy.88
  206.3 15.3 %all-to-all-start.1 = ((f32[64,12,2]{1,2,0:T(2,128)}), f32[64,12,2]{1,2,0:T(2,128)S(1)}, u32[]{:S(2)}, u32[]{:S(2)}) async-start(f32[64,12,2]{1,2,0:T(2,128)} %copy.88), calls=%async_computation.1 | async-start | bytes 131072 | tf_op jit(solution)/shard_map/all_to_all | solution.py:64
  221.6 0.9 copy.91
  222.6 13.2 %all-to-all-done.1 = f32[64,12,2]{1,2,0:T(2,128)S(1)} async-done(((f32[64,12,2]{1,2,0:T(2,128)}), f32[64,12,2]{1,2,0:T(2,128)S(1)}, u32[]{:S(2)}, u32[]{:S(2)}) %all-to-all-start.1) | async-done | bytes 6176 | tf_op jit(solution)/shard_map/all_to_all | solution.py:64
  235.8 0.4 convolution_bitcast_fusion
  236.2 0.1 copy.89
  236.4 0.6 fusion.14
  237.0 0.7 copy.90
  (6 shorter events, 0.1 us)
Async XLA Ops:
  7.2 6.0 %copy-start.2 = (bf16[128,896]{1,0:T(8,128)(2,1)S(1)}, bf16[128,896]{1,0:T(8,128)(2,1)}, u32[]{:S(2)}) copy-start(bf16[128,896]{1,0:T(8,128)(2,1)} %param.5) | copy-start | bytes 688132
  7.2 177.1 %all-gather.2.cloned.1.call-start = ((), (), s32[]{:S(2)}) async-start(), calls=%async_computation.2 | async-start | bytes 12386304 | tf_op jit(solution)/shard_map/all_gather | solution.py:48
  115.3 1.1 copy-start
  116.5 3.1 %copy-start.1 = (bf16[2,768,128]{2,1,0:T(8,128)(2,1)S(1)}, bf16[2,768,128]{2,1,0:T(8,128)(2,1)}, u32[]{:S(2)}) copy-start(bf16[2,768,128]{2,1,0:T(8,128)(2,1)} %param.9) | copy-start | bytes 1179652
  206.3 29.5 %all-to-all-start.1 = ((f32[64,12,2]{1,2,0:T(2,128)}), f32[64,12,2]{1,2,0:T(2,128)S(1)}, u32[]{:S(2)}, u32[]{:S(2)}) async-start(f32[64,12,2]{1,2,0:T(2,128)} %copy.88), calls=%async_computation.1 | async-start | bytes 131072 | tf_op jit(solution)/shard_map/all_to_all | solution.py:64
Sparse Core Ops, SparseCore 0:
  119.7 64.5 all-gather.1

commit v4 on v3

--- a/solution.py
+++ b/solution.py
@@ -45,17 +45,18 @@
     payload_in = lax.all_to_all(payload, "node", split_axis=0, concat_axis=0, tiled=True)
     rows_in = payload_in[:, : capacity * width].reshape(slot_rows, width)
     prob_in = payload_in[:, capacity * width :]
-    full_rows = lax.all_gather(rows_in, "local", axis=0, tiled=False)
-    local_count = full_rows.shape[0]
-    weight_split = weight_down.reshape(
-        expert_count, weight_down.shape[1], local_count, width
-    )
-    hidden_grads = jnp.einsum(
-        "lrd,ehld->erh",
-        full_rows,
-        weight_split,
+    local_count = lax.axis_size("local")
+    hidden_local = weight_down.shape[1]
+    weight_split = weight_down.reshape(expert_count, hidden_local, local_count, width)
+    weight_cols = lax.all_to_all(weight_split, "local", split_axis=2, concat_axis=1, tiled=True)
+    weight_cols = weight_cols.reshape(expert_count, hidden_local * local_count, width)
+    partial_grads = jnp.einsum(
+        "rd,ehd->erh",
+        rows_in,
+        weight_cols,
         preferred_element_type=jnp.float32,
     )
+    hidden_grads = lax.psum_scatter(partial_grads, "local", scatter_dimension=2, tiled=True)
     scales = jnp.transpose(prob_in.reshape(slot_rows, expert_count).astype(jnp.float32))
     grad_hidden = (scales[:, :, None] * hidden_grads).astype(jnp.bfloat16)
     partial_value = jnp.sum(saved_hidden.astype(jnp.float32) * hidden_grads, axis=2)

time: 245 us -> 272 us (1.11)
  waiting for transfers between devices: 76.8 us -> 135 us
  blocking collectives: 98.8 us -> 43.1 us
  local copies, waits for them, and re-layouts: 23.5 us -> 36.8 us
  starting transfers between devices: 15.4 us -> 24.8 us
    all_to_all x1 -> x2, waiting for transfers between devices: 13.2 us -> 92.1 us  [the longest x1 61.7 us: on_device(): lax.all_to_all(payload, 'node', split_axis=0, concat_axis=0, tiled=True)]
    all_gather x1 -> x0, waiting for transfers between devices: 63.5 us -> none  [on_device(): full_rows = lax.all_gather(rows_in, 'local', axis=0, tiled=False)]
    all_to_all x1, blocking collectives: 86 us -> 29.3 us  [on_device(): lax.all_to_all(summed, 'node', split_axis=0, concat_axis=0, tiled=True)]
    reduce_scatter x0 -> x1, waiting for transfers between devices: none -> 43.1 us  [on_device(): lax.psum_scatter(partial_grads, 'local', scatter_dimension=2, tiled=True)]
    all_to_all x1 -> x2, starting transfers between devices: 15.3 us -> 24.6 us  [the longest x1 13.2 us: on_device(): lax.all_to_all(payload, 'node', split_axis=0, concat_axis=0, tiled=True)]
    reshape x0 -> x2, local copies, waits for them, and re-layouts: none -> 8.41 us  [the longest x1 6.23 us: on_device(): weight_down.reshape(expert_count, hidden_local, local_count, width)]
    unnamed x13 -> x16, local copies, waits for them, and re-layouts: 13.3 us -> 18.4 us
    all_to_all x0 -> x1, local copies, waits for them, and re-layouts: none -> 4.23 us  [on_device(): lax.all_to_all(weight_split, 'local', split_axis=2, concat_axis=1, tiled=...]
  transfers between devices with their start and end apart: 2 -> 3, of which waited for: 2 -> 3; matrix products, arithmetic and copies ran while one was open for 1% -> 7% of each run, Pallas kernels for 0% -> 0%
where the time goes in v4:
time: 272 us; the launch traced here: 271 us
  waiting for transfers between devices  135 us (50%)
  blocking collectives  43.1 us (16%)
  local copies, waits for them, and re-layouts  36.8 us (14%)
  starting transfers between devices  24.8 us (9%)
  between operations  14.3 us (5%)
  matrix products  9.37 us (3%)
  other arithmetic  7.89 us (3%)
    all_to_all x1, waiting for transfers between devices, on_device(): lax.all_to_all(payload, 'node', split_axis=0, concat_axis=0, tiled=True)  61.7 us
    reduce_scatter x1, waiting for transfers between devices, on_device(): lax.psum_scatter(partial_grads, 'local', scatter_dimension=2, tiled=True)  43.1 us
    all_to_all x1, waiting for transfers between devices, on_device(): lax.all_to_all(weight_split, 'local', split_axis=2, concat_axis=1, tiled=...  30.3 us
    all_to_all x1, blocking collectives, on_device(): lax.all_to_all(summed, 'node', split_axis=0, concat_axis=0, tiled=True)  29.3 us
    unnamed x16, local copies, waits for them, and re-layouts  18.4 us
    all_gather x1, blocking collectives, on_device(): lax.all_gather(partial_value, 'local', axis=0, tiled=False)  13.8 us
    all_to_all x1, starting transfers between devices, on_device(): lax.all_to_all(payload, 'node', split_axis=0, concat_axis=0, tiled=True)  13.2 us
    all_to_all x1, starting transfers between devices, on_device(): lax.all_to_all(weight_split, 'local', split_axis=2, concat_axis=1, tiled=...  11.4 us
  transfers between devices with their start and end apart: 3, of which 3 were waited for; matrix products, arithmetic and copies ran while one was open for 7% of the time, Pallas kernels for 0%

profile of v4, /device:TPU:1, one launch (start us, length us, event | category | flops | bytes accessed | tf_op | source)
XLA Modules:
  0.0 271.4 jit_solution(12409712123208933885)
XLA Ops:
  7.2 5.9 %copy.78 = bf16[2,128,7168]{1,2,0:T(8,128)(2,1)} copy(bf16[2,128,7168]{2,1,0:T(8,128)(2,1)} %param.8) | data formatting | bytes 7340032 | tf_op args[3]
  13.1 6.2 %copy.79 = bf16[2,128,8,896]{3,1,0,2:T(8,128)(2,1)} copy(bf16[2,128,8,896]{1,3,2,0:T(8,128)(2,1)} %bitcast.33) | data formatting | bytes 7340032 | tf_op jit(solution)/shard_map/reshape | solution.py:50
  19.3 0.0 copy-start.3
  19.3 0.0 copy-start.4
  19.3 11.4 %all-to-all-start.1 = ((bf16[2,128,8,896]{3,1,0,2:T(8,128)(2,1)}), bf16[2,128,8,896]{3,1,0,2:T(8,128)(2,1)}, u32[]{:S(2)}, u32[]{:S(2)}) async-start(bf16[2,128,8,896]{3,1,0,2:T(8,128)(2,1)} %copy.79), calls=%async_computation.1 | async-start | bytes 7340032 | tf_op jit(solution)/shard_map/all_to_all | solution.py:51
  30.7 0.0 copy-done.3
  30.7 0.0 copy-start.2
  30.7 0.1 copy.69
  30.8 0.3 convert_reduce_fusion.1
  31.1 0.1 copy.71
  31.2 0.2 reduce_window_sum.11
  31.4 0.1 copy.70
  31.4 0.0 copy-done.4
  31.5 0.1 copy.72
  31.6 0.3 fusion.6
  32.0 0.1 copy.73
  32.1 0.5 convolution_convert_fusion
  32.6 0.1 copy.74
  32.7 0.1 copy.75
  32.8 2.2 convert_reduce_fusion
  35.1 0.1 reshape.90
  35.2 0.0 copy-done.2
  35.2 2.8 %gather_fusion = bf16[768,896]{1,0:T(8,128)(2,1)S(1)} fusion(bf16[129,896]{1,0:T(8,128)(2,1)S(1)} %concatenate.6, s32[1024]{0:T(1024)S(1)} %pad_clamp_fusion), kind=kCustom, calls=%fused_computation | custom fusion | bytes 2755584 | tf_op jit(solution)/shard_map/jit(_take)/gather | solution.py:10
  38.1 0.3 reshape.89
  38.4 0.3 broadcast_select_fusion
  38.7 0.3 copy.89
  39.0 0.1 maximum_bitcast_fusion
  39.1 0.5 broadcast.68
  39.6 1.6 reduce
  41.3 2.4 reshape.99
  43.7 30.3 %all-to-all-done.1 = bf16[2,128,8,896]{3,1,0,2:T(8,128)(2,1)} async-done(((bf16[2,128,8,896]{3,1,0,2:T(8,128)(2,1)}), bf16[2,128,8,896]{3,1,0,2:T(8,128)(2,1)}, u32[]{:S(2)}, u32[]{:S(2)}) %all-to-all-start.1) | async-done | bytes 3670048 | tf_op jit(solution)/shard_map/all_to_all | solution.py:51
  74.0 13.2 %all-to-all-start = ((bf16[64,2,5388]{2,1,0:T(2,128)(2,1)}), bf16[64,2,5388]{2,1,0:T(2,128)(2,1)}, u32[]{:S(2)}, u32[]{:S(2)}) async-start(bf16[64,2,5388]{2,1,0:T(2,128)(2,1)} %reshape.99), calls=%async_computation | async-start | bytes 2818048 | tf_op jit(solution)/shard_map/all_to_all | solution.py:45
  87.2 0.2 reduce-scatter.2.cloned.1.call-start
  87.5 4.2 %copy.80 = bf16[2,8,128,1,896]{4,2,1,0,3:T(8,128)(2,1)} copy(bf16[2,8,128,1,896]{4,2,0,1,3:T(8,128)(2,1)} %bitcast.7) | data formatting | bytes 7340032 | tf_op jit(solution)/shard_map/all_to_all | solution.py:51
  91.7 61.7 %all-to-all-done = bf16[64,2,5388]{2,1,0:T(2,128)(2,1)} async-done(((bf16[64,2,5388]{2,1,0:T(2,128)(2,1)}), bf16[64,2,5388]{2,1,0:T(2,128)(2,1)}, u32[]{:S(2)}, u32[]{:S(2)}) %all-to-all-start) | async-done | bytes 1379360 | tf_op jit(solution)/shard_map/all_to_all | solution.py:45
  153.4 8.4 %reshape.100 = bf16[64,1,10776]{2,1,0:T(2,128)(2,1)S(1)} reshape(bf16[64,2,5388]{2,1,0:T(2,128)(2,1)} %all-to-all-done) | data formatting | bytes 2758656
  161.8 0.2 copy.91
  162.0 0.0 copy-start
  162.0 1.1 copy-done
  163.1 0.1 slice.11
  163.2 2.2 reshape.97
  165.4 7.4 %convolution_bitcast_fusion = f32[2,768,1024]{2,1,0:T(8,128)} fusion(bf16[768,896,1]{1,0,2:T(8,128)(2,1)S(1)} %reshape.97, bf16[2,1024,896]{2,1,0:T(8,128)(2,1)} %bitcast.38), kind=kOutput, calls=%fused_computation.1 | convolution fusion | flops 2818572288 | bytes 11337728 | tf_op jit(solution)/shard_map/rd,ehd->erh/dot_general | solution.py:53
  172.8 0.0 copy-start.1
  172.8 0.0 reduce-scatter.2.cloned.1.call-update
  172.8 0.8 slice_convert_fusion
  173.6 0.2 reshape.87
  173.7 0.1 copy.77
  173.9 43.1 %reduce-scatter.2.cloned.1.call-done = f32[2,768,128]{2,1,0:T(8,128)} async-done(((f32[2,768,1024]{2,1,0:T(8,128)}), f32[2,768,128]{2,1,0:T(8,128)}) %reduce-scatter.2.cloned.1.call-update) | async-done | bytes 786448 | tf_op jit(solution)/shard_map/reduce_scatter | solution.py:59
  217.0 0.0 copy-done.1
  217.0 2.3 multiply_reduce_fusion
  219.3 0.1 all_gather_reshape.3
  219.4 0.1 copy.81
  219.5 13.8 %all_gather.3 = f32[8,64,12,2]{1,3,2,0:T(2,128)S(1)} all-gather(f32[1,64,12,2]{1,3,2,0:T(2,128)S(1)} %copy.81), channel_id=1, replica_groups=mesh['node'=64,'local'=8] {'local'}, dimensions={0}, use_global_device_ids=true | all-gather | bytes 55296 | tf_op jit(solution)/shard_map/all_gather | solution.py:64
  233.3 0.1 reduce_sum.49
  233.3 0.1 copy.83
  233.4 29.3 %all_to_all.32 = f32[64,12,2]{1,2,0:T(2,128)S(1)} all-to-all(f32[64,12,2]{1,2,0:T(2,128)S(1)} %copy.83), channel_id=1, replica_groups=mesh['node'=64,'local'=8] {'node'}, dimensions={0} | all-to-all | bytes 12288 | tf_op jit(solution)/shard_map/all_to_all | solution.py:65
  262.7 0.4 convolution_bitcast_fusion.1
  263.2 0.1 copy.84
  263.3 0.6 fusion.5
  263.9 0.7 copy.85
  (6 shorter events, 0.1 us)
Async XLA Ops:
  19.3 11.4 %copy-start.3 = (s32[128,4]{0,1:T(4,128)S(1)}, s32[128,4]{0,1:T(4,128)}, u32[]{:S(2)}) copy-start(s32[128,4]{0,1:T(4,128)} %param.7) | copy-start | bytes 6148
  19.3 12.1 %copy-start.4 = (bf16[128,8]{0,1:T(8,128)(2,1)S(1)}, bf16[128,8]{0,1:T(8,128)(2,1)}, u32[]{:S(2)}) copy-start(bf16[128,8]{0,1:T(8,128)(2,1)} %param.6) | copy-start | bytes 6148
  19.3 54.7 %all-to-all-start.1 = ((bf16[2,128,8,896]{3,1,0,2:T(8,128)(2,1)}), bf16[2,128,8,896]{3,1,0,2:T(8,128)(2,1)}, u32[]{:S(2)}, u32[]{:S(2)}) async-start(bf16[2,128,8,896]{3,1,0,2:T(8,128)(2,1)} %copy.79), calls=%async_computation.1 | async-start | bytes 7340032 | tf_op jit(solution)/shard_map/all_to_all | solution.py:51
  30.7 4.5 %copy-start.2 = (bf16[128,896]{1,0:T(8,128)(2,1)S(1)}, bf16[128,896]{1,0:T(8,128)(2,1)}, u32[]{:S(2)}) copy-start(bf16[128,896]{1,0:T(8,128)(2,1)} %param.5) | copy-start | bytes 688132
  74.0 79.4 %all-to-all-start = ((bf16[64,2,5388]{2,1,0:T(2,128)(2,1)}), bf16[64,2,5388]{2,1,0:T(2,128)(2,1)}, u32[]{:S(2)}, u32[]{:S(2)}) async-start(bf16[64,2,5388]{2,1,0:T(2,128)(2,1)} %reshape.99), calls=%async_computation | async-start | bytes 2818048 | tf_op jit(solution)/shard_map/all_to_all | solution.py:45
  87.2 129.7 %reduce-scatter.2.cloned.1.call-start = ((), (), s32[]{:S(2)}) async-start(), calls=%async_computation.4 | async-start | bytes 7077888 | tf_op jit(solution)/shard_map/reduce_scatter | solution.py:59
  162.0 1.1 copy-start
  172.8 44.2 %copy-start.1 = (bf16[2,768,128]{2,1,0:T(8,128)(2,1)S(1)}, bf16[2,768,128]{2,1,0:T(8,128)(2,1)}, u32[]{:S(2)}) copy-start(bf16[2,768,128]{2,1,0:T(8,128)(2,1)} %param.9) | copy-start | bytes 1179652
Sparse Core Ops, SparseCore 0:
  172.9 44.0 reduce-scatter.1

commit v5 on v4

--- a/solution.py
+++ b/solution.py
@@ -46,16 +46,24 @@
     rows_in = payload_in[:, : capacity * width].reshape(slot_rows, width)
     prob_in = payload_in[:, capacity * width :]
     local_count = lax.axis_size("local")
-    hidden_local = weight_down.shape[1]
-    weight_split = weight_down.reshape(expert_count, hidden_local, local_count, width)
-    weight_cols = lax.all_to_all(weight_split, "local", split_axis=2, concat_axis=1, tiled=True)
-    weight_cols = weight_cols.reshape(expert_count, hidden_local * local_count, width)
+    local_index = lax.axis_index("local")
+    pieces = []
+    for step in range(local_count):
+        target = (local_index + step) % local_count
+        piece = lax.dynamic_slice_in_dim(weight_down, target * width, width, axis=2)
+        if step:
+            pairs = [(j, (j + step) % local_count) for j in range(local_count)]
+            piece = lax.ppermute(piece, "local", perm=pairs)
+        pieces.append(piece)
+    stacked = jnp.stack(pieces, axis=0)
+    block_order = (local_index - jnp.arange(local_count, dtype=jnp.int32)) % local_count
+    weight_blocks = jnp.take(stacked, block_order, axis=0)
     partial_grads = jnp.einsum(
-        "rd,ehd->erh",
+        "rd,behd->erbh",
         rows_in,
-        weight_cols,
+        weight_blocks,
         preferred_element_type=jnp.float32,
-    )
+    ).reshape(expert_count, slot_rows, -1)
     hidden_grads = lax.psum_scatter(partial_grads, "local", scatter_dimension=2, tiled=True)
     scales = jnp.transpose(prob_in.reshape(slot_rows, expert_count).astype(jnp.float32))
     grad_hidden = (scales[:, :, None] * hidden_grads).astype(jnp.bfloat16)

time: 272 us -> 236 us (0.87)
  waiting for transfers between devices: 135 us -> 91.3 us
  starting transfers between devices: 24.8 us -> 56.5 us
  blocking collectives: 43.1 us -> 13.8 us
  local copies, waits for them, and re-layouts: 36.8 us -> 44.3 us
    all_to_all x1, waiting for transfers between devices: 61.7 us -> 0.2 us  [on_device(): lax.all_to_all(payload, 'node', split_axis=0, concat_axis=0, tiled=True)]
    all_to_all x1 -> x0, blocking collectives: 29.3 us -> none  [on_device(): lax.all_to_all(summed, 'node', split_axis=0, concat_axis=0, tiled=True)]
    ppermute x0 -> x7, waiting for transfers between devices: none -> 28.9 us  [on_device(): piece = lax.ppermute(piece, 'local', perm=pairs)]
    ppermute x0 -> x7, starting transfers between devices: none -> 21.8 us  [on_device(): piece = lax.ppermute(piece, 'local', perm=pairs)]
    all_to_all x1, waiting for transfers between devices: 30.3 us -> 13.2 us  [on_device(): lax.all_to_all(summed, 'node', split_axis=0, concat_axis=0, tiled=True)]
    reshape x1 -> x0, local copies, waits for them, and re-layouts: 6.23 us -> none  [on_device(): weight_down.reshape(expert_count, hidden_local, local_count, width)]
    all_to_all x1, starting transfers between devices: 13.2 us -> 19.3 us  [on_device(): lax.all_to_all(payload, 'node', split_axis=0, concat_axis=0, tiled=True)]
    reduce_scatter x1, waiting for transfers between devices: 43.1 us -> 49 us  [on_device(): lax.psum_scatter(partial_grads, 'local', scatter_dimension=2, tiled=True)]
  transfers between devices with their start and end apart: 3 -> 10, of which waited for: 3 -> 6; matrix products, arithmetic and copies ran while one was open for 7% -> 8% of each run, Pallas kernels for 0% -> 0%
where the time goes in v5:
time: 236 us; the launch traced here: 235 us
  waiting for transfers between devices  91.3 us (39%)
  starting transfers between devices  56.5 us (24%)
  local copies, waits for them, and re-layouts  44.3 us (19%)
  between operations  14.4 us (6%)
  blocking collectives  13.8 us (6%)
  matrix products  7.52 us (3%)
  other arithmetic  6.87 us (3%)
    reduce_scatter x1, waiting for transfers between devices, on_device(): lax.psum_scatter(partial_grads, 'local', scatter_dimension=2, tiled=True)  49 us
    ppermute x7, waiting for transfers between devices, on_device(): piece = lax.ppermute(piece, 'local', perm=pairs)  28.9 us
    unnamed x18, local copies, waits for them, and re-layouts  21.8 us
    ppermute x7, starting transfers between devices, on_device(): piece = lax.ppermute(piece, 'local', perm=pairs)  21.8 us
    all_to_all x1, starting transfers between devices, on_device(): lax.all_to_all(payload, 'node', split_axis=0, concat_axis=0, tiled=True)  19.3 us
    all_to_all x1, starting transfers between devices, on_device(): lax.all_to_all(summed, 'node', split_axis=0, concat_axis=0, tiled=True)  15.3 us
    all_gather x1, blocking collectives, on_device(): lax.all_gather(partial_value, 'local', axis=0, tiled=False)  13.8 us
    all_to_all x1, waiting for transfers between devices, on_device(): lax.all_to_all(summed, 'node', split_axis=0, concat_axis=0, tiled=True)  13.2 us
  transfers between devices with their start and end apart: 10, of which 6 were waited for; matrix products, arithmetic and copies ran while one was open for 8% of the time, Pallas kernels for 0%

profile of v5, /device:TPU:1, one launch (start us, length us, event | category | flops | bytes accessed | tf_op | source)
XLA Modules:
  0.0 234.7 jit_solution(15492797296723181403)
XLA Ops:
  7.2 0.8 copy.72
  8.0 0.3 convert_reduce_fusion.1
  8.3 0.2 reduce_window_sum.11
  8.6 2.3 convert_reduce_fusion
  10.9 0.8 copy.75
  11.7 0.3 fusion.14
  12.1 0.6 convolution_convert_fusion
  12.7 0.1 copy.77
  12.8 0.1 copy.78
  12.9 0.1 reshape.139
  13.0 1.0 concatenate.6
  14.0 2.8 %gather_fusion = bf16[768,896]{1,0:T(8,128)(2,1)S(1)} fusion(bf16[129,896]{1,0:T(8,128)(2,1)S(1)} %concatenate.6, s32[1024]{0:T(1024)S(1)} %pad_clamp_fusion.1), kind=kCustom, calls=%fused_computation | custom fusion | bytes 2755584 | tf_op jit(solution)/shard_map/jit(_take)/gather | solution.py:10
  16.8 0.3 reshape.138
  17.2 0.3 broadcast_select_fusion
  17.5 0.3 copy.93
  17.7 0.1 maximum_bitcast_fusion
  17.8 0.5 broadcast.177
  18.4 1.6 reduce
  20.0 2.3 reshape.156
  22.3 19.3 %all-to-all-start = ((bf16[64,2,5388]{2,1,0:T(2,128)(2,1)}), bf16[64,2,5388]{2,1,0:T(2,128)(2,1)}, u32[]{:S(2)}, u32[]{:S(2)}) async-start(bf16[64,2,5388]{2,1,0:T(2,128)(2,1)} %reshape.156), calls=%async_computation | async-start | bytes 2818048 | tf_op jit(solution)/shard_map/all_to_all | solution.py:45
  41.8 3.3 %constant_dynamic-slice_fusion = (bf16[2,128,896]{2,1,0:T(8,128)(2,1)S(1)}, bf16[2,128,896]{2,1,0:T(8,128)(2,1)}, bf16[2,128,896]{2,1,0:T(8,128)(2,1)}, bf16[2,1...) fusion(bf16[2,128,7168]{2,1,0:T(8,128)(2,1)} %param.8, ...), kind=kLoop, calls=%fused_computation.51 | loop fusion | bytes 6422556 | tf_op jit(solution)/shard_map/dynamic_slice | solution.py:53
  45.2 1.0 collective-permute-start.6
  46.1 4.5 %collective-permute-start.4 = (bf16[2,128,896]{2,1,0:T(8,128)(2,1)}, bf16[2,128,896]{2,1,0:T(8,128)(2,1)S(1)}, u32[]{:S(2)}, u32[]{:S(2)}) collective-permute-start(bf16[2,128,896]{2,1,0:T(8,128)(2,1)} %get-tuple-element.15), channel_id=1, source_target_pairs={{0,5},{1,6},{2,7},{3,0},{4,1},{5,2},{6,3},{7,4},{8,13},{9,14},{10,... | collective-permute-start | bytes 1376264 | tf_op jit(solution)/shard_map/ppermute | solution.py:56
  50.6 2.3 collective-permute-start.3
  52.9 2.6 %collective-permute-start.1 = (bf16[2,128,896]{2,1,0:T(8,128)(2,1)}, bf16[2,128,896]{2,1,0:T(8,128)(2,1)S(1)}, u32[]{:S(2)}, u32[]{:S(2)}) collective-permute-start(bf16[2,128,896]{2,1,0:T(8,128)(2,1)} %get-tuple-element.18), channel_id=1, source_target_pairs={{0,2},{1,3},{2,4},{3,5},{4,6},{5,7},{6,0},{7,1},{8,10},{9,11},{10,... | collective-permute-start | bytes 1376264 | tf_op jit(solution)/shard_map/ppermute | solution.py:56
  55.5 2.8 %collective-permute-start = (bf16[2,128,896]{2,1,0:T(8,128)(2,1)}, bf16[2,128,896]{2,1,0:T(8,128)(2,1)S(1)}, u32[]{:S(2)}, u32[]{:S(2)}) collective-permute-start(bf16[2,128,896]{2,1,0:T(8,128)(2,1)} %get-tuple-element.19), channel_id=1, source_target_pairs={{0,1},{1,2},{2,3},{3,4},{4,5},{5,6},{6,7},{7,0},{8,9},{9,10},{10,1... | collective-permute-start | bytes 1376264 | tf_op jit(solution)/shard_map/ppermute | solution.py:56
  58.3 1.8 bitcast_dynamic-update-slice_fusion.7
  60.1 21.7 %collective-permute-done = bf16[2,128,896]{2,1,0:T(8,128)(2,1)S(1)} collective-permute-done((bf16[2,128,896]{2,1,0:T(8,128)(2,1)}, bf16[2,128,896]{2,1,0:T(8,128)(2,1)S(1)}, u32[]{:S(2)}, u32[]{:S(2)}) %collective-permute-start) | collective-permute-done | bytes 458784 | tf_op jit(solution)/shard_map/ppermute | solution.py:56
  81.8 5.7 %collective-permute-start.2 = (bf16[2,128,896]{2,1,0:T(8,128)(2,1)}, bf16[2,128,896]{2,1,0:T(8,128)(2,1)S(1)}, u32[]{:S(2)}, u32[]{:S(2)}) collective-permute-start(bf16[2,128,896]{2,1,0:T(8,128)(2,1)} %get-tuple-element.17), channel_id=1, source_target_pairs={{0,3},{1,4},{2,5},{3,6},{4,7},{5,0},{6,1},{7,2},{8,11},{9,12},{10,... | collective-permute-start | bytes 1376264 | tf_op jit(solution)/shard_map/ppermute | solution.py:56
  87.6 0.8 bitcast_dynamic-update-slice_fusion.6
  88.4 3.0 %collective-permute-start.5 = (bf16[2,128,896]{2,1,0:T(8,128)(2,1)S(1)}, bf16[2,128,896]{2,1,0:T(8,128)(2,1)S(1)}, u32[]{:S(2)}, u32[]{:S(2)}) collective-permute-start(bf16[2,128,896]{2,1,0:T(8,128)(2,1)S(1)} %get-tuple-element.20), channel_id=1, source_target_pairs={{0,6},{1,7},{2,0},{3,1},{4,2},{5,3},{6,4},{7,5},{8,14},{9,15},{10,... | collective-permute-start | bytes 1376264 | tf_op jit(solution)/shard_map/ppermute | solution.py:56
  91.4 0.8 bitcast_dynamic-update-slice_fusion.5
  92.2 5.7 %collective-permute-done.2 = bf16[2,128,896]{2,1,0:T(8,128)(2,1)S(1)} collective-permute-done((bf16[2,128,896]{2,1,0:T(8,128)(2,1)}, bf16[2,128,896]{2,1,0:T(8,128)(2,1)S(1)}, u32[]{:S(2)}, u32[]{:S(2)}) %collective-permute-start.2) | collective-permute-done | bytes 458784 | tf_op jit(solution)/shard_map/ppermute | solution.py:56
  98.0 0.8 bitcast_dynamic-update-slice_fusion.4
  98.8 0.9 bitcast_dynamic-update-slice_fusion.3
  99.6 0.8 bitcast_dynamic-update-slice_fusion.2
  100.5 1.4 collective-permute-done.5
  101.9 0.8 bitcast_dynamic-update-slice_fusion.1
  102.7 0.8 bitcast_dynamic-update-slice_fusion
  103.5 4.8 %gather_fusion.1 = bf16[8,2,128,896]{3,2,1,0:T(8,128)(2,1)} fusion(bf16[8,2,128,896]{3,2,1,0:T(8,128)(2,1)} %bitcast_dynamic-update-slice_fusion, s32[1024]{0:T(1024)S(1)} %pad_clamp_fusion), kind=kCustom, calls=%fused_computation.1 | custom fusion | bytes 7340064 | tf_op jit(solution)/shard_map/jit(_take)/gather | solution.py:60
  108.3 0.2 all-to-all-done
  108.5 8.4 %reshape.157 = bf16[64,1,10776]{2,1,0:T(2,128)(2,1)S(1)} reshape(bf16[64,2,5388]{2,1,0:T(2,128)(2,1)} %all-to-all-done) | data formatting | bytes 2758656
  116.9 0.2 copy.95
  117.1 1.1 copy-done
  118.3 2.2 reshape.154
  120.4 5.6 %fusion.3 = f32[2,768,8,128]{1,3,0,2:T(8,128)S(1)} fusion(bf16[8,2,128,896]{3,2,1,0:T(8,128)(2,1)} %gather_fusion.1, pred[8]{0:T(512)(128)(4,1)S(1)} %compare_and_fusion.1, bf16[768,896,1,1]{1,0,2,3:T(8,128)(2,1)S(1)} %reshape.154), kind=kOutput, calls=%fused_computation.5 | convolution fusion | flops 2820407296 | bytes 11337736 | tf_op jit(solution)/shard_map/rd,behd->erbh/dot_general | solution.py:61
  126.0 3.3 %copy.81 = f32[2,768,8,128]{1,3,2,0:T(8,128)} copy(f32[2,768,8,128]{1,3,0,2:T(8,128)S(1)} %fusion.3) | data formatting | bytes 12582912 | tf_op jit(solution)/shard_map/rd,behd->erbh/transpose | solution.py:61
  129.3 1.0 copy-done.1
  130.3 0.2 copy.82
  130.5 0.7 slice_convert_fusion
  131.2 0.2 reshape.136
  131.3 0.1 copy.80
  131.5 49.0 %reduce-scatter.2.cloned.1.call-done = f32[2,768,128]{1,2,0:T(8,128)} async-done(((f32[2,768,1024]{1,2,0:T(8,128)}), f32[2,768,128]{1,2,0:T(8,128)}) %reduce-scatter.2.cloned.1.call-update) | async-done | bytes 786448 | tf_op jit(solution)/shard_map/reduce_scatter | solution.py:67
  180.5 1.3 multiply_reduce_fusion
  181.7 0.1 all_gather_reshape.3
  181.9 13.8 %all_gather.3 = f32[8,64,12,2]{1,3,2,0:T(2,128)S(1)} all-gather(f32[1,64,12,2]{1,3,2,0:T(2,128)S(1)} %copy.83), channel_id=1, replica_groups=mesh['node'=64,'local'=8] {'local'}, dimensions={0}, use_global_device_ids=true | all-gather | bytes 55296 | tf_op jit(solution)/shard_map/all_gather | solution.py:72
  195.8 0.7 copy.85
  196.5 15.3 %all-to-all-start.1 = ((f32[64,12,2]{1,2,0:T(2,128)}), f32[64,12,2]{1,2,0:T(2,128)S(1)}, u32[]{:S(2)}, u32[]{:S(2)}) async-start(f32[64,12,2]{1,2,0:T(2,128)} %copy.85), calls=%async_computation.2 | async-start | bytes 131072 | tf_op jit(solution)/shard_map/all_to_all | solution.py:73
  211.9 0.9 copy.88
  212.8 13.2 %all-to-all-done.1 = f32[64,12,2]{1,2,0:T(2,128)S(1)} async-done(((f32[64,12,2]{1,2,0:T(2,128)}), f32[64,12,2]{1,2,0:T(2,128)S(1)}, u32[]{:S(2)}, u32[]{:S(2)}) %all-to-all-start.1) | async-done | bytes 6176 | tf_op jit(solution)/shard_map/all_to_all | solution.py:73
  226.0 0.4 convolution_bitcast_fusion
  226.4 0.1 copy.86
  226.6 0.6 fusion.13
  227.2 0.7 copy.87
  (22 shorter events, 0.6 us)
Async XLA Ops:
  22.3 86.2 %all-to-all-start = ((bf16[64,2,5388]{2,1,0:T(2,128)(2,1)}), bf16[64,2,5388]{2,1,0:T(2,128)(2,1)}, u32[]{:S(2)}, u32[]{:S(2)}) async-start(bf16[64,2,5388]{2,1,0:T(2,128)(2,1)} %reshape.156), calls=%async_computation | async-start | bytes 2818048 | tf_op jit(solution)/shard_map/all_to_all | solution.py:45
  41.7 138.8 %reduce-scatter.2.cloned.1.call-start = ((), (), s32[]{:S(2)}) async-start(), calls=%async_computation.3 | async-start | bytes 7077888 | tf_op jit(solution)/shard_map/reduce_scatter | solution.py:67
  45.2 57.5 %collective-permute-start.6 = (bf16[2,128,896]{2,1,0:T(8,128)(2,1)S(1)}, bf16[2,128,896]{2,1,0:T(8,128)(2,1)S(1)}, u32[]{:S(2)}, u32[]{:S(2)}) collective-permute-start(bf16[2,128,896]{2,1,0:T(8,128)(2,1)S(1)} %get-tuple-element.14), channel_id=1, source_target_pairs={{0,7},{1,0},{2,1},{3,2},{4,3},{5,4},{6,5},{7,6},{8,15},{9,8},{10,9... | collective-permute-start | bytes 1376264 | tf_op jit(solution)/shard_map/ppermute | solution.py:56
  46.1 53.5 %collective-permute-start.4 = (bf16[2,128,896]{2,1,0:T(8,128)(2,1)}, bf16[2,128,896]{2,1,0:T(8,128)(2,1)S(1)}, u32[]{:S(2)}, u32[]{:S(2)}) collective-permute-start(bf16[2,128,896]{2,1,0:T(8,128)(2,1)} %get-tuple-element.15), channel_id=1, source_target_pairs={{0,5},{1,6},{2,7},{3,0},{4,1},{5,2},{6,3},{7,4},{8,13},{9,14},{10,... | collective-permute-start | bytes 1376264 | tf_op jit(solution)/shard_map/ppermute | solution.py:56
  50.6 48.2 %collective-permute-start.3 = (bf16[2,128,896]{2,1,0:T(8,128)(2,1)}, bf16[2,128,896]{2,1,0:T(8,128)(2,1)S(1)}, u32[]{:S(2)}, u32[]{:S(2)}) collective-permute-start(bf16[2,128,896]{2,1,0:T(8,128)(2,1)} %get-tuple-element.16), channel_id=1, source_target_pairs={{0,4},{1,5},{2,6},{3,7},{4,0},{5,1},{6,2},{7,3},{8,12},{9,13},{10,... | collective-permute-start | bytes 1376264 | tf_op jit(solution)/shard_map/ppermute | solution.py:56
  52.9 35.5 %collective-permute-start.1 = (bf16[2,128,896]{2,1,0:T(8,128)(2,1)}, bf16[2,128,896]{2,1,0:T(8,128)(2,1)S(1)}, u32[]{:S(2)}, u32[]{:S(2)}) collective-permute-start(bf16[2,128,896]{2,1,0:T(8,128)(2,1)} %get-tuple-element.18), channel_id=1, source_target_pairs={{0,2},{1,3},{2,4},{3,5},{4,6},{5,7},{6,0},{7,1},{8,10},{9,11},{10,... | collective-permute-start | bytes 1376264 | tf_op jit(solution)/shard_map/ppermute | solution.py:56
  55.5 26.3 %collective-permute-start = (bf16[2,128,896]{2,1,0:T(8,128)(2,1)}, bf16[2,128,896]{2,1,0:T(8,128)(2,1)S(1)}, u32[]{:S(2)}, u32[]{:S(2)}) collective-permute-start(bf16[2,128,896]{2,1,0:T(8,128)(2,1)} %get-tuple-element.19), channel_id=1, source_target_pairs={{0,1},{1,2},{2,3},{3,4},{4,5},{5,6},{6,7},{7,0},{8,9},{9,10},{10,1... | collective-permute-start | bytes 1376264 | tf_op jit(solution)/shard_map/ppermute | solution.py:56
  81.8 16.1 %collective-permute-start.2 = (bf16[2,128,896]{2,1,0:T(8,128)(2,1)}, bf16[2,128,896]{2,1,0:T(8,128)(2,1)S(1)}, u32[]{:S(2)}, u32[]{:S(2)}) collective-permute-start(bf16[2,128,896]{2,1,0:T(8,128)(2,1)} %get-tuple-element.17), channel_id=1, source_target_pairs={{0,3},{1,4},{2,5},{3,6},{4,7},{5,0},{6,1},{7,2},{8,11},{9,12},{10,... | collective-permute-start | bytes 1376264 | tf_op jit(solution)/shard_map/ppermute | solution.py:56
  88.4 13.5 %collective-permute-start.5 = (bf16[2,128,896]{2,1,0:T(8,128)(2,1)S(1)}, bf16[2,128,896]{2,1,0:T(8,128)(2,1)S(1)}, u32[]{:S(2)}, u32[]{:S(2)}) collective-permute-start(bf16[2,128,896]{2,1,0:T(8,128)(2,1)S(1)} %get-tuple-element.20), channel_id=1, source_target_pairs={{0,6},{1,7},{2,0},{3,1},{4,2},{5,3},{6,4},{7,5},{8,14},{9,15},{10,... | collective-permute-start | bytes 1376264 | tf_op jit(solution)/shard_map/ppermute | solution.py:56
  117.1 1.1 copy-start
  129.3 1.0 copy-start.1
  196.5 29.5 %all-to-all-start.1 = ((f32[64,12,2]{1,2,0:T(2,128)}), f32[64,12,2]{1,2,0:T(2,128)S(1)}, u32[]{:S(2)}, u32[]{:S(2)}) async-start(f32[64,12,2]{1,2,0:T(2,128)} %copy.85), calls=%async_computation.2 | async-start | bytes 131072 | tf_op jit(solution)/shard_map/all_to_all | solution.py:73
Sparse Core Ops, SparseCore 0:
  129.4 51.0 reduce-scatter.1

commit v6 on v5

--- a/solution.py
+++ b/solution.py
@@ -59,17 +59,29 @@
     block_order = (local_index - jnp.arange(local_count, dtype=jnp.int32)) % local_count
     weight_blocks = jnp.take(stacked, block_order, axis=0)
     partial_grads = jnp.einsum(
-        "rd,behd->erbh",
+        "rd,behd->berh",
         rows_in,
         weight_blocks,
         preferred_element_type=jnp.float32,
-    ).reshape(expert_count, slot_rows, -1)
-    hidden_grads = lax.psum_scatter(partial_grads, "local", scatter_dimension=2, tiled=True)
+    )
+    saved_blocks = lax.all_gather(saved_hidden, "local", axis=0, tiled=False)
+    partial_scores = jnp.sum(saved_blocks.astype(jnp.float32) * partial_grads, axis=(0, 3))
+    lane = partial_grads.shape[3]
+    score_rows = -(-slot_rows // lane)
+    extra_rows = -(-score_rows // 8) * 8
+    score_block = jnp.pad(
+        partial_scores, ((0, 0), (0, extra_rows * lane - slot_rows))
+    ).reshape(expert_count, extra_rows, lane)
+    extended = jnp.concatenate(
+        [partial_grads, jnp.broadcast_to(score_block[None], (local_count,) + score_block.shape)],
+        axis=2,
+    )
+    reduced = lax.psum_scatter(extended, "local", scatter_dimension=0, tiled=True)[0]
+    hidden_grads = reduced[:, :slot_rows, :]
+    scores = reduced[:, slot_rows:, :].reshape(expert_count, -1)[:, :slot_rows]
     scales = jnp.transpose(prob_in.reshape(slot_rows, expert_count).astype(jnp.float32))
     grad_hidden = (scales[:, :, None] * hidden_grads).astype(jnp.bfloat16)
-    partial_value = jnp.sum(saved_hidden.astype(jnp.float32) * hidden_grads, axis=2)
-    partial_value = jnp.transpose(partial_value).reshape(node_count, capacity, expert_count)
-    summed = jnp.sum(lax.all_gather(partial_value, "local", axis=0, tiled=False), axis=0)
+    summed = jnp.transpose(scores).reshape(node_count, capacity, expert_count)
     returned = lax.all_to_all(summed, "node", split_axis=0, concat_axis=0, tiled=True)
     per_node = jnp.einsum("tms,msc->tmc", select_full, returned, precision=lax.Precision.HIGHEST)
     grad_probs = jnp.einsum("tjm,tmc->tjc", listed, per_node, precision=lax.Precision.HIGHEST)

time: 236 us -> 241 us (1.021)
  blocking collectives: 13.8 us -> 0 us
  other arithmetic: 6.87 us -> 13.1 us
  waiting for transfers between devices: 91.3 us -> 96.7 us
  matrix products: 7.52 us -> 12.1 us
    all_gather x1 -> x0, blocking collectives: 13.8 us -> none  [on_device(): lax.all_gather(partial_value, 'local', axis=0, tiled=False)]
    concatenate x0 -> x1, other arithmetic: none -> 6.36 us  [on_device(): jnp.concatenate([partial_grads, jnp.broadcast_to(score_block[None], (loca...]
    reduce_scatter x1, waiting for transfers between devices: 49 us -> 55.1 us  [on_device(): lax.psum_scatter(extended, 'local', scatter_dimension=0, tiled=True)[0]]
    convert_element_type x0 -> x1, local copies, waits for them, and re-layouts: none -> 5.39 us  [on_device(): saved_blocks.astype(jnp.float32) * partial_grads]
    dot_general x1, matrix products: 5.56 us -> 10.1 us  [on_device(): jnp.einsum('rd,behd->berh', rows_in, weight_blocks, preferred_element_typ...]
    transpose x1, local copies, waits for them, and re-layouts: 3.26 us -> 0.01 us  [on_device(): summed = jnp.transpose(scores).reshape(node_count, capacity, expert_count)]
  transfers between devices with their start and end apart: 10 -> 11, of which waited for: 6 -> 6; matrix products, arithmetic and copies ran while one was open for 8% -> 19% of each run, Pallas kernels for 0% -> 0%
where the time goes in v6:
time: 241 us; the launch traced here: 239 us
  waiting for transfers between devices  96.7 us (40%)
  starting transfers between devices  56.6 us (23%)
  local copies, waits for them, and re-layouts  46.5 us (19%)
  between operations  14.4 us (6%)
  other arithmetic  13.1 us (5%)
  matrix products  12.1 us (5%)
    reduce_scatter x1, waiting for transfers between devices, on_device(): lax.psum_scatter(extended, 'local', scatter_dimension=0, tiled=True)[0]  55.1 us
    ppermute x7, waiting for transfers between devices, on_device(): piece = lax.ppermute(piece, 'local', perm=pairs)  28.8 us
    ppermute x7, starting transfers between devices, on_device(): piece = lax.ppermute(piece, 'local', perm=pairs)  21.8 us
    unnamed x18, local copies, waits for them, and re-layouts  20.8 us
    all_to_all x1, starting transfers between devices, on_device(): lax.all_to_all(payload, 'node', split_axis=0, concat_axis=0, tiled=True)  19.3 us
    all_to_all x1, starting transfers between devices, on_device(): lax.all_to_all(summed, 'node', split_axis=0, concat_axis=0, tiled=True)  15.4 us
    all_to_all x1, waiting for transfers between devices, on_device(): lax.all_to_all(summed, 'node', split_axis=0, concat_axis=0, tiled=True)  11.9 us
    dot_general x1, matrix products, on_device(): jnp.einsum('rd,behd->berh', rows_in, weight_blocks, preferred_element_typ...  10.1 us
  transfers between devices with their start and end apart: 11, of which 6 were waited for; matrix products, arithmetic and copies ran while one was open for 19% of the time, Pallas kernels for 0%

profile of v6, /device:TPU:1, one launch (start us, length us, event | category | flops | bytes accessed | tf_op | source)
XLA Modules:
  0.0 239.4 jit_solution(955602621427623206)
XLA Ops:
  7.2 0.7 all-gather.3.cloned.1.call-update
  7.9 0.8 copy.72
  8.7 0.3 convert_reduce_fusion.1
  9.0 0.2 reduce_window_sum.11
  9.3 2.3 convert_reduce_fusion
  11.6 0.8 copy.75
  12.4 0.3 fusion.15
  12.9 0.6 convolution_convert_fusion
  13.5 0.1 copy.78
  13.6 0.1 reshape.144
  13.8 1.0 concatenate.9
  14.7 2.8 %gather_fusion = bf16[768,896]{1,0:T(8,128)(2,1)S(1)} fusion(bf16[129,896]{1,0:T(8,128)(2,1)S(1)} %concatenate.9, s32[1024]{0:T(1024)S(1)} %pad_clamp_fusion.1), kind=kCustom, calls=%fused_computation | custom fusion | bytes 2755584 | tf_op jit(solution)/shard_map/jit(_take)/gather | solution.py:10
  17.5 0.3 reshape.143
  17.9 0.3 broadcast_select_fusion
  18.2 0.3 copy.90
  18.6 0.5 broadcast.179
  19.1 1.6 reduce
  20.7 2.3 reshape.163
  23.1 19.3 %all-to-all-start = ((bf16[64,2,5388]{2,1,0:T(2,128)(2,1)}), bf16[64,2,5388]{2,1,0:T(2,128)(2,1)}, u32[]{:S(2)}, u32[]{:S(2)}) async-start(bf16[64,2,5388]{2,1,0:T(2,128)(2,1)} %reshape.163), calls=%async_computation | async-start | bytes 2818048 | tf_op jit(solution)/shard_map/all_to_all | solution.py:45
  42.6 3.4 %constant_dynamic-slice_fusion = (bf16[2,128,896]{2,1,0:T(8,128)(2,1)S(1)}, bf16[2,128,896]{2,1,0:T(8,128)(2,1)}, bf16[2,128,896]{2,1,0:T(8,128)(2,1)}, bf16[2,1...) fusion(bf16[2,128,7168]{2,1,0:T(8,128)(2,1)} %param.8, ...), kind=kLoop, calls=%fused_computation.57 | loop fusion | bytes 6422556 | tf_op jit(solution)/shard_map/dynamic_slice | solution.py:53
  46.0 1.0 collective-permute-start.6
  46.9 4.5 %collective-permute-start.4 = (bf16[2,128,896]{2,1,0:T(8,128)(2,1)}, bf16[2,128,896]{2,1,0:T(8,128)(2,1)S(1)}, u32[]{:S(2)}, u32[]{:S(2)}) collective-permute-start(bf16[2,128,896]{2,1,0:T(8,128)(2,1)} %get-tuple-element.17), channel_id=1, source_target_pairs={{0,5},{1,6},{2,7},{3,0},{4,1},{5,2},{6,3},{7,4},{8,13},{9,14},{10,... | collective-permute-start | bytes 1376264 | tf_op jit(solution)/shard_map/ppermute | solution.py:56
  51.5 2.3 collective-permute-start.3
  53.7 2.6 %collective-permute-start.1 = (bf16[2,128,896]{2,1,0:T(8,128)(2,1)}, bf16[2,128,896]{2,1,0:T(8,128)(2,1)S(1)}, u32[]{:S(2)}, u32[]{:S(2)}) collective-permute-start(bf16[2,128,896]{2,1,0:T(8,128)(2,1)} %get-tuple-element.20), channel_id=1, source_target_pairs={{0,2},{1,3},{2,4},{3,5},{4,6},{5,7},{6,0},{7,1},{8,10},{9,11},{10,... | collective-permute-start | bytes 1376264 | tf_op jit(solution)/shard_map/ppermute | solution.py:56
  56.3 2.8 %collective-permute-start = (bf16[2,128,896]{2,1,0:T(8,128)(2,1)}, bf16[2,128,896]{2,1,0:T(8,128)(2,1)S(1)}, u32[]{:S(2)}, u32[]{:S(2)}) collective-permute-start(bf16[2,128,896]{2,1,0:T(8,128)(2,1)} %get-tuple-element.21), channel_id=1, source_target_pairs={{0,1},{1,2},{2,3},{3,4},{4,5},{5,6},{6,7},{7,0},{8,9},{9,10},{10,1... | collective-permute-start | bytes 1376264 | tf_op jit(solution)/shard_map/ppermute | solution.py:56
  59.1 1.8 bitcast_dynamic-update-slice_fusion.7
  61.0 21.7 %collective-permute-done = bf16[2,128,896]{2,1,0:T(8,128)(2,1)S(1)} collective-permute-done((bf16[2,128,896]{2,1,0:T(8,128)(2,1)}, bf16[2,128,896]{2,1,0:T(8,128)(2,1)S(1)}, u32[]{:S(2)}, u32[]{:S(2)}) %collective-permute-start) | collective-permute-done | bytes 458784 | tf_op jit(solution)/shard_map/ppermute | solution.py:56
  82.7 5.7 %collective-permute-start.2 = (bf16[2,128,896]{2,1,0:T(8,128)(2,1)}, bf16[2,128,896]{2,1,0:T(8,128)(2,1)S(1)}, u32[]{:S(2)}, u32[]{:S(2)}) collective-permute-start(bf16[2,128,896]{2,1,0:T(8,128)(2,1)} %get-tuple-element.19), channel_id=1, source_target_pairs={{0,3},{1,4},{2,5},{3,6},{4,7},{5,0},{6,1},{7,2},{8,11},{9,12},{10,... | collective-permute-start | bytes 1376264 | tf_op jit(solution)/shard_map/ppermute | solution.py:56
  88.4 0.8 bitcast_dynamic-update-slice_fusion.6
  89.2 3.0 %collective-permute-start.5 = (bf16[2,128,896]{2,1,0:T(8,128)(2,1)S(1)}, bf16[2,128,896]{2,1,0:T(8,128)(2,1)S(1)}, u32[]{:S(2)}, u32[]{:S(2)}) collective-permute-start(bf16[2,128,896]{2,1,0:T(8,128)(2,1)S(1)} %get-tuple-element.22), channel_id=1, source_target_pairs={{0,6},{1,7},{2,0},{3,1},{4,2},{5,3},{6,4},{7,5},{8,14},{9,15},{10,... | collective-permute-start | bytes 1376264 | tf_op jit(solution)/shard_map/ppermute | solution.py:56
  92.3 0.8 bitcast_dynamic-update-slice_fusion.5
  93.1 5.7 %collective-permute-done.2 = bf16[2,128,896]{2,1,0:T(8,128)(2,1)S(1)} collective-permute-done((bf16[2,128,896]{2,1,0:T(8,128)(2,1)}, bf16[2,128,896]{2,1,0:T(8,128)(2,1)S(1)}, u32[]{:S(2)}, u32[]{:S(2)}) %collective-permute-start.2) | collective-permute-done | bytes 458784 | tf_op jit(solution)/shard_map/ppermute | solution.py:56
  98.8 0.8 bitcast_dynamic-update-slice_fusion.4
  99.6 0.8 bitcast_dynamic-update-slice_fusion.3
  100.5 0.8 bitcast_dynamic-update-slice_fusion.2
  101.3 1.4 collective-permute-done.5
  102.7 0.8 bitcast_dynamic-update-slice_fusion.1
  103.5 0.8 bitcast_dynamic-update-slice_fusion
  104.3 4.8 %gather_fusion.1 = bf16[8,2,128,896]{3,2,1,0:T(8,128)(2,1)} fusion(bf16[8,2,128,896]{3,2,1,0:T(8,128)(2,1)} %bitcast_dynamic-update-slice_fusion, s32[1024]{0:T(1024)S(1)} %pad_clamp_fusion), kind=kCustom, calls=%fused_computation.1 | custom fusion | bytes 7340064 | tf_op jit(solution)/shard_map/jit(_take)/gather | solution.py:60
  109.1 0.2 all-to-all-done
  109.3 8.4 %reshape.164 = bf16[64,1,10776]{2,1,0:T(2,128)(2,1)S(1)} reshape(bf16[64,2,5388]{2,1,0:T(2,128)(2,1)} %all-to-all-done) | data formatting | bytes 2758656
  117.7 0.2 copy.96
  117.8 1.1 copy-done
  119.0 2.2 reshape.161
  121.2 5.4 %copy.81 = f32[16,768,128]{1,2,0:T(8,128)} copy(bf16[16,768,128]{2,1,0:T(8,128)(2,1)} %all-gather.3.cloned.1.call-done) | data formatting | bytes 9437184 | tf_op jit(solution)/shard_map/convert_element_type | solution.py:68
  126.6 10.1 %multiply_reduce_fusion = (f32[2,768]{1,0:T(2,128)S(1)}, f32[8,2,768,128]{2,3,1,0:T(8,128)}) fusion(f32[8,2,768,128]{2,3,1,0:T(8,128)} %bitcast.62, bf16[768,896,1,1]{1,0,2,3:T(8,128)(2,1)S(1)} %reshape.161, bf16[8,2,128,896]{3,2,1,0:T(8,128)(2,1)} %gather_fusion.1, pred[8]{0:T(512)(128)(4,1)S(1)} %compare_and_fusion.1), kind=kOutput, calls=%fused_computation.3 | convolution fusion | flops 2823551488 | bytes 17635336 | tf_op jit(solution)/shard_map/rd,behd->berh/dot_general | solution.py:61
  136.7 0.1 copy.82
  136.9 0.1 broadcast_in_dim.43
  137.0 6.4 %pad_maximum_fusion = f32[8,2,776,128]{2,3,1,0:T(8,128)} fusion(f32[8,2,8,128]{2,3,1,0:T(8,128)S(1)} %broadcast_in_dim.43, f32[8,2,768,128]{2,3,1,0:T(8,128)} %get-tuple-element.24), kind=kLoop, calls=%fused_computation.2 | loop fusion | flops 1589248 | bytes 12713984 | tf_op jit(solution)/shard_map/concatenate | solution.py:75
  143.4 0.7 slice_convert_fusion
  144.1 0.2 reshape.141
  144.2 0.1 copy.80
  144.4 55.1 %reduce-scatter.2.cloned.1.call-done = f32[1,2,776,128]{2,3,1,0:T(8,128)} async-done(((f32[8,2,776,128]{2,3,1,0:T(8,128)}), f32[1,2,776,128]{2,3,1,0:T(8,128)}) %reduce-scatter.2.cloned.1.call-update) | async-done | bytes 794640 | tf_op jit(solution)/shard_map/reduce_scatter | solution.py:79
  199.5 0.9 slice.27
  200.5 0.1 reshape.139
  200.6 0.7 copy.84
  201.3 15.4 %all-to-all-start.1 = ((f32[64,12,2]{1,2,0:T(2,128)}), f32[64,12,2]{1,2,0:T(2,128)S(1)}, u32[]{:S(2)}, u32[]{:S(2)}) async-start(f32[64,12,2]{1,2,0:T(2,128)} %copy.84), calls=%async_computation.2 | async-start | bytes 131072 | tf_op jit(solution)/shard_map/all_to_all | solution.py:85
  216.6 1.2 fusion.8
  217.8 0.9 copy.87
  218.7 11.9 %all-to-all-done.1 = f32[64,12,2]{1,2,0:T(2,128)S(1)} async-done(((f32[64,12,2]{1,2,0:T(2,128)}), f32[64,12,2]{1,2,0:T(2,128)S(1)}, u32[]{:S(2)}, u32[]{:S(2)}) %all-to-all-start.1) | async-done | bytes 6176 | tf_op jit(solution)/shard_map/all_to_all | solution.py:85
  230.6 0.4 convolution_bitcast_fusion
  231.1 0.1 copy.85
  231.2 0.6 fusion.14
  231.8 0.7 copy.86
  (28 shorter events, 0.8 us)
Async XLA Ops:
  7.2 114.1 %all-gather.3.cloned.1.call-start = ((), (), s32[]{:S(2)}) async-start(), calls=%async_computation.4 | async-start | bytes 3538944 | tf_op jit(solution)/shard_map/all_gather | solution.py:67
  23.1 86.2 %all-to-all-start = ((bf16[64,2,5388]{2,1,0:T(2,128)(2,1)}), bf16[64,2,5388]{2,1,0:T(2,128)(2,1)}, u32[]{:S(2)}, u32[]{:S(2)}) async-start(bf16[64,2,5388]{2,1,0:T(2,128)(2,1)} %reshape.163), calls=%async_computation | async-start | bytes 2818048 | tf_op jit(solution)/shard_map/all_to_all | solution.py:45
  42.4 157.0 %reduce-scatter.2.cloned.1.call-start = ((), (), s32[]{:S(2)}) async-start(), calls=%async_computation.3 | async-start | bytes 8257536 | tf_op jit(solution)/shard_map/reduce_scatter | solution.py:79
  46.0 57.5 %collective-permute-start.6 = (bf16[2,128,896]{2,1,0:T(8,128)(2,1)S(1)}, bf16[2,128,896]{2,1,0:T(8,128)(2,1)S(1)}, u32[]{:S(2)}, u32[]{:S(2)}) collective-permute-start(bf16[2,128,896]{2,1,0:T(8,128)(2,1)S(1)} %get-tuple-element.16), channel_id=1, source_target_pairs={{0,7},{1,0},{2,1},{3,2},{4,3},{5,4},{6,5},{7,6},{8,15},{9,8},{10,9... | collective-permute-start | bytes 1376264 | tf_op jit(solution)/shard_map/ppermute | solution.py:56
  46.9 53.5 %collective-permute-start.4 = (bf16[2,128,896]{2,1,0:T(8,128)(2,1)}, bf16[2,128,896]{2,1,0:T(8,128)(2,1)S(1)}, u32[]{:S(2)}, u32[]{:S(2)}) collective-permute-start(bf16[2,128,896]{2,1,0:T(8,128)(2,1)} %get-tuple-element.17), channel_id=1, source_target_pairs={{0,5},{1,6},{2,7},{3,0},{4,1},{5,2},{6,3},{7,4},{8,13},{9,14},{10,... | collective-permute-start | bytes 1376264 | tf_op jit(solution)/shard_map/ppermute | solution.py:56
  51.5 48.2 %collective-permute-start.3 = (bf16[2,128,896]{2,1,0:T(8,128)(2,1)}, bf16[2,128,896]{2,1,0:T(8,128)(2,1)S(1)}, u32[]{:S(2)}, u32[]{:S(2)}) collective-permute-start(bf16[2,128,896]{2,1,0:T(8,128)(2,1)} %get-tuple-element.18), channel_id=1, source_target_pairs={{0,4},{1,5},{2,6},{3,7},{4,0},{5,1},{6,2},{7,3},{8,12},{9,13},{10,... | collective-permute-start | bytes 1376264 | tf_op jit(solution)/shard_map/ppermute | solution.py:56
  53.7 35.5 %collective-permute-start.1 = (bf16[2,128,896]{2,1,0:T(8,128)(2,1)}, bf16[2,128,896]{2,1,0:T(8,128)(2,1)S(1)}, u32[]{:S(2)}, u32[]{:S(2)}) collective-permute-start(bf16[2,128,896]{2,1,0:T(8,128)(2,1)} %get-tuple-element.20), channel_id=1, source_target_pairs={{0,2},{1,3},{2,4},{3,5},{4,6},{5,7},{6,0},{7,1},{8,10},{9,11},{10,... | collective-permute-start | bytes 1376264 | tf_op jit(solution)/shard_map/ppermute | solution.py:56
  56.3 26.3 %collective-permute-start = (bf16[2,128,896]{2,1,0:T(8,128)(2,1)}, bf16[2,128,896]{2,1,0:T(8,128)(2,1)S(1)}, u32[]{:S(2)}, u32[]{:S(2)}) collective-permute-start(bf16[2,128,896]{2,1,0:T(8,128)(2,1)} %get-tuple-element.21), channel_id=1, source_target_pairs={{0,1},{1,2},{2,3},{3,4},{4,5},{5,6},{6,7},{7,0},{8,9},{9,10},{10,1... | collective-permute-start | bytes 1376264 | tf_op jit(solution)/shard_map/ppermute | solution.py:56
  82.7 16.1 %collective-permute-start.2 = (bf16[2,128,896]{2,1,0:T(8,128)(2,1)}, bf16[2,128,896]{2,1,0:T(8,128)(2,1)S(1)}, u32[]{:S(2)}, u32[]{:S(2)}) collective-permute-start(bf16[2,128,896]{2,1,0:T(8,128)(2,1)} %get-tuple-element.19), channel_id=1, source_target_pairs={{0,3},{1,4},{2,5},{3,6},{4,7},{5,0},{6,1},{7,2},{8,11},{9,12},{10,... | collective-permute-start | bytes 1376264 | tf_op jit(solution)/shard_map/ppermute | solution.py:56
  89.2 13.4 %collective-permute-start.5 = (bf16[2,128,896]{2,1,0:T(8,128)(2,1)S(1)}, bf16[2,128,896]{2,1,0:T(8,128)(2,1)S(1)}, u32[]{:S(2)}, u32[]{:S(2)}) collective-permute-start(bf16[2,128,896]{2,1,0:T(8,128)(2,1)S(1)} %get-tuple-element.22), channel_id=1, source_target_pairs={{0,6},{1,7},{2,0},{3,1},{4,2},{5,3},{6,4},{7,5},{8,14},{9,15},{10,... | collective-permute-start | bytes 1376264 | tf_op jit(solution)/shard_map/ppermute | solution.py:56
  117.8 1.1 copy-start
  201.3 29.4 %all-to-all-start.1 = ((f32[64,12,2]{1,2,0:T(2,128)}), f32[64,12,2]{1,2,0:T(2,128)S(1)}, u32[]{:S(2)}, u32[]{:S(2)}) async-start(f32[64,12,2]{1,2,0:T(2,128)} %copy.84), calls=%async_computation.2 | async-start | bytes 131072 | tf_op jit(solution)/shard_map/all_to_all | solution.py:85
Sparse Core Ops, SparseCore 0:
  10.1 41.1 all-gather.2
  143.5 55.9 reduce-scatter.1

commit v7 on v5

--- a/solution.py
+++ b/solution.py
@@ -64,12 +64,18 @@
         weight_blocks,
         preferred_element_type=jnp.float32,
     ).reshape(expert_count, slot_rows, -1)
+    saved_blocks = lax.all_gather(saved_hidden, "local", axis=0, tiled=False)
+    partial_scores = jnp.einsum(
+        "berh,erbh->er",
+        saved_blocks.astype(jnp.float32),
+        partial_grads.reshape(expert_count, slot_rows, local_count, -1),
+        precision=lax.Precision.HIGHEST,
+    )
+    partial_value = jnp.transpose(partial_scores).reshape(node_count, capacity, expert_count)
+    summed = jnp.sum(lax.all_gather(partial_value, "local", axis=0, tiled=False), axis=0)
     hidden_grads = lax.psum_scatter(partial_grads, "local", scatter_dimension=2, tiled=True)
     scales = jnp.transpose(prob_in.reshape(slot_rows, expert_count).astype(jnp.float32))
     grad_hidden = (scales[:, :, None] * hidden_grads).astype(jnp.bfloat16)
-    partial_value = jnp.sum(saved_hidden.astype(jnp.float32) * hidden_grads, axis=2)
-    partial_value = jnp.transpose(partial_value).reshape(node_count, capacity, expert_count)
-    summed = jnp.sum(lax.all_gather(partial_value, "local", axis=0, tiled=False), axis=0)
     returned = lax.all_to_all(summed, "node", split_axis=0, concat_axis=0, tiled=True)
     per_node = jnp.einsum("tms,msc->tmc", select_full, returned, precision=lax.Precision.HIGHEST)
     grad_probs = jnp.einsum("tjm,tmc->tjc", listed, per_node, precision=lax.Precision.HIGHEST)

time: 236 us -> 201 us (0.85)
  waiting for transfers between devices: 91.3 us -> 50.8 us
  local copies, waits for them, and re-layouts: 44.3 us -> 51.1 us
  starting transfers between devices: 56.5 us -> 51.7 us
  other arithmetic: 6.87 us -> 11.2 us
    reduce_scatter x1, waiting for transfers between devices: 49 us -> 0.01 us  [on_device(): lax.psum_scatter(partial_grads, 'local', scatter_dimension=2, tiled=True)]
    ppermute x7, waiting for transfers between devices: 28.9 us -> 37 us  [on_device(): piece = lax.ppermute(piece, 'local', perm=pairs)]
    unnamed x18, local copies, waits for them, and re-layouts: 21.8 us -> 28.2 us
    dot_general x0 -> x1, other arithmetic: none -> 4.41 us  [on_device(): jnp.einsum('berh,erbh->er', saved_blocks.astype(jnp.float32), partial_gra...]
    ppermute x7, starting transfers between devices: 21.8 us -> 18 us  [on_device(): piece = lax.ppermute(piece, 'local', perm=pairs)]
  transfers between devices with their start and end apart: 10 -> 11, of which waited for: 6 -> 7; matrix products, arithmetic and copies ran while one was open for 8% -> 25% of each run, Pallas kernels for 0% -> 0%
where the time goes in v7:
time: 201 us; the launch traced here: 200 us
  starting transfers between devices  51.7 us (26%)
  local copies, waits for them, and re-layouts  51.1 us (25%)
  waiting for transfers between devices  50.8 us (25%)
  between operations  14.5 us (7%)
  blocking collectives  13 us (6%)
  other arithmetic  11.2 us (6%)
  matrix products  7.52 us (4%)
    ppermute x7, waiting for transfers between devices, on_device(): piece = lax.ppermute(piece, 'local', perm=pairs)  37 us
    unnamed x18, local copies, waits for them, and re-layouts  28.2 us
    all_to_all x1, starting transfers between devices, on_device(): lax.all_to_all(payload, 'node', split_axis=0, concat_axis=0, tiled=True)  19.3 us
    ppermute x7, starting transfers between devices, on_device(): piece = lax.ppermute(piece, 'local', perm=pairs)  18 us
    all_to_all x1, starting transfers between devices, on_device(): lax.all_to_all(summed, 'node', split_axis=0, concat_axis=0, tiled=True)  14.3 us
    all_to_all x1, waiting for transfers between devices, on_device(): lax.all_to_all(summed, 'node', split_axis=0, concat_axis=0, tiled=True)  13.1 us
    all_gather x1, blocking collectives, on_device(): lax.all_gather(partial_value, 'local', axis=0, tiled=False)  13 us
    dot_general x1, matrix products, on_device(): jnp.einsum('rd,behd->erbh', rows_in, weight_blocks, preferred_element_typ...  5.56 us
  transfers between devices with their start and end apart: 11, of which 7 were waited for; matrix products, arithmetic and copies ran while one was open for 25% of the time, Pallas kernels for 0%

profile of v7, /device:TPU:1, one launch (start us, length us, event | category | flops | bytes accessed | tf_op | source)
XLA Modules:
  0.0 199.8 jit_solution(14682800685278625658)
XLA Ops:
  7.2 0.8 copy.68
  8.0 0.3 convert_reduce_fusion.1
  8.3 0.2 reduce_window_sum.11
  8.6 2.2 %convert_reduce_fusion = (s32[64,12]{1,0:T(8,128)S(1)}, s32[64,12]{1,0:T(8,128)S(1)}) fusion(s32[128,64]{0,1:T(8,128)S(1)} %copy.69, pred[128,64]{0,1:T(8,128)(4,1)S(1)} %broadcast_compare_fusion), kind=kLoop, calls=%fused_computation.16 | loop fusion | flops 588288 | bytes 47104 | tf_op jit(solution)/shard_map/reduce_sum | solution.py:29
  10.9 0.8 copy.71
  11.7 0.3 fusion.14
  12.1 0.6 convolution_convert_fusion
  12.8 0.1 copy.74
  12.9 0.1 reshape.139
  13.0 1.0 concatenate.6
  14.0 2.8 %gather_fusion = bf16[768,896]{1,0:T(8,128)(2,1)S(1)} fusion(bf16[129,896]{1,0:T(8,128)(2,1)S(1)} %concatenate.6, s32[1024]{0:T(1024)S(1)} %pad_clamp_fusion.1), kind=kCustom, calls=%fused_computation | custom fusion | bytes 2755584 | tf_op jit(solution)/shard_map/jit(_take)/gather | solution.py:10
  16.8 0.3 reshape.138
  17.2 0.3 broadcast_select_fusion
  17.5 0.3 copy.93
  17.8 0.5 broadcast.177
  18.3 1.6 reduce.2
  20.0 2.3 %reshape.160 = bf16[64,2,5388]{2,1,0:T(2,128)(2,1)} reshape(bf16[64,10776]{1,0:T(8,128)(2,1)S(1)} %reduce.2) | data formatting | bytes 2758656
  22.3 19.3 %all-to-all-start = ((bf16[64,2,5388]{2,1,0:T(2,128)(2,1)}), bf16[64,2,5388]{2,1,0:T(2,128)(2,1)}, u32[]{:S(2)}, u32[]{:S(2)}) async-start(bf16[64,2,5388]{2,1,0:T(2,128)(2,1)} %reshape.160), calls=%async_computation | async-start | bytes 2818048 | tf_op jit(solution)/shard_map/all_to_all | solution.py:45
  41.7 0.7 all-gather.3.cloned.1.call-update
  42.6 3.3 %constant_dynamic-slice_fusion = (bf16[2,128,896]{2,1,0:T(8,128)(2,1)S(1)}, bf16[2,128,896]{2,1,0:T(8,128)(2,1)}, bf16[2,128,896]{2,1,0:T(8,128)(2,1)}, bf16[2,1...) fusion(bf16[2,128,7168]{2,1,0:T(8,128)(2,1)} %param.8, ...), kind=kLoop, calls=%fused_computation.51 | loop fusion | bytes 6422556 | tf_op jit(solution)/shard_map/dynamic_slice | solution.py:53
  45.9 2.1 %collective-permute-start = (bf16[2,128,896]{2,1,0:T(8,128)(2,1)}, bf16[2,128,896]{2,1,0:T(8,128)(2,1)S(1)}, u32[]{:S(2)}, u32[]{:S(2)}) collective-permute-start(bf16[2,128,896]{2,1,0:T(8,128)(2,1)} %get-tuple-element.19), channel_id=1, source_target_pairs={{0,1},{1,2},{2,3},{3,4},{4,5},{5,6},{6,7},{7,0},{8,9},{9,10},{10,1... | collective-permute-start | bytes 1376264 | tf_op jit(solution)/shard_map/ppermute | solution.py:56
  48.0 3.2 %collective-permute-start.1 = (bf16[2,128,896]{2,1,0:T(8,128)(2,1)}, bf16[2,128,896]{2,1,0:T(8,128)(2,1)S(1)}, u32[]{:S(2)}, u32[]{:S(2)}) collective-permute-start(bf16[2,128,896]{2,1,0:T(8,128)(2,1)} %get-tuple-element.18), channel_id=1, source_target_pairs={{0,2},{1,3},{2,4},{3,5},{4,6},{5,7},{6,0},{7,1},{8,10},{9,11},{10,... | collective-permute-start | bytes 1376264 | tf_op jit(solution)/shard_map/ppermute | solution.py:56
  51.2 3.5 %collective-permute-start.2 = (bf16[2,128,896]{2,1,0:T(8,128)(2,1)}, bf16[2,128,896]{2,1,0:T(8,128)(2,1)S(1)}, u32[]{:S(2)}, u32[]{:S(2)}) collective-permute-start(bf16[2,128,896]{2,1,0:T(8,128)(2,1)} %get-tuple-element.17), channel_id=1, source_target_pairs={{0,3},{1,4},{2,5},{3,6},{4,7},{5,0},{6,1},{7,2},{8,11},{9,12},{10,... | collective-permute-start | bytes 1376264 | tf_op jit(solution)/shard_map/ppermute | solution.py:56
  54.7 2.3 %collective-permute-start.3 = (bf16[2,128,896]{2,1,0:T(8,128)(2,1)}, bf16[2,128,896]{2,1,0:T(8,128)(2,1)S(1)}, u32[]{:S(2)}, u32[]{:S(2)}) collective-permute-start(bf16[2,128,896]{2,1,0:T(8,128)(2,1)} %get-tuple-element.16), channel_id=1, source_target_pairs={{0,4},{1,5},{2,6},{3,7},{4,0},{5,1},{6,2},{7,3},{8,12},{9,13},{10,... | collective-permute-start | bytes 1376264 | tf_op jit(solution)/shard_map/ppermute | solution.py:56
  57.0 3.9 %collective-permute-start.4 = (bf16[2,128,896]{2,1,0:T(8,128)(2,1)}, bf16[2,128,896]{2,1,0:T(8,128)(2,1)S(1)}, u32[]{:S(2)}, u32[]{:S(2)}) collective-permute-start(bf16[2,128,896]{2,1,0:T(8,128)(2,1)} %get-tuple-element.15), channel_id=1, source_target_pairs={{0,5},{1,6},{2,7},{3,0},{4,1},{5,2},{6,3},{7,4},{8,13},{9,14},{10,... | collective-permute-start | bytes 1376264 | tf_op jit(solution)/shard_map/ppermute | solution.py:56
  61.0 1.8 bitcast_dynamic-update-slice_fusion.7
  62.8 2.9 %collective-permute-start.5 = (bf16[2,128,896]{2,1,0:T(8,128)(2,1)S(1)}, bf16[2,128,896]{2,1,0:T(8,128)(2,1)S(1)}, u32[]{:S(2)}, u32[]{:S(2)}) collective-permute-start(bf16[2,128,896]{2,1,0:T(8,128)(2,1)S(1)} %get-tuple-element.20), channel_id=1, source_target_pairs={{0,6},{1,7},{2,0},{3,1},{4,2},{5,3},{6,4},{7,5},{8,14},{9,15},{10,... | collective-permute-start | bytes 1376264 | tf_op jit(solution)/shard_map/ppermute | solution.py:56
  65.8 0.8 bitcast_dynamic-update-slice_fusion.6
  66.6 2.0 collective-permute-done.1
  68.6 0.8 bitcast_dynamic-update-slice_fusion.5
  69.4 17.6 %collective-permute-done.2 = bf16[2,128,896]{2,1,0:T(8,128)(2,1)S(1)} collective-permute-done((bf16[2,128,896]{2,1,0:T(8,128)(2,1)}, bf16[2,128,896]{2,1,0:T(8,128)(2,1)S(1)}, u32[]{:S(2)}, u32[]{:S(2)}) %collective-permute-start.2) | collective-permute-done | bytes 458784 | tf_op jit(solution)/shard_map/ppermute | solution.py:56
  87.0 0.8 bitcast_dynamic-update-slice_fusion.4
  87.8 13.9 %collective-permute-done.3 = bf16[2,128,896]{2,1,0:T(8,128)(2,1)S(1)} collective-permute-done((bf16[2,128,896]{2,1,0:T(8,128)(2,1)}, bf16[2,128,896]{2,1,0:T(8,128)(2,1)S(1)}, u32[]{:S(2)}, u32[]{:S(2)}) %collective-permute-start.3) | collective-permute-done | bytes 458784 | tf_op jit(solution)/shard_map/ppermute | solution.py:56
  101.7 0.8 bitcast_dynamic-update-slice_fusion.3
  102.5 1.7 collective-permute-done.4
  104.2 0.8 bitcast_dynamic-update-slice_fusion.2
  105.0 1.0 collective-permute-done.5
  106.1 0.8 bitcast_dynamic-update-slice_fusion.1
  106.9 0.8 collective-permute-done.6
  107.7 0.8 bitcast_dynamic-update-slice_fusion
  108.5 4.8 %gather_fusion.1 = bf16[8,2,128,896]{3,2,1,0:T(8,128)(2,1)} fusion(bf16[8,2,128,896]{3,2,1,0:T(8,128)(2,1)} %bitcast_dynamic-update-slice_fusion, s32[1024]{0:T(1024)S(1)} %pad_clamp_fusion), kind=kCustom, calls=%fused_computation.1 | custom fusion | bytes 7340064 | tf_op jit(solution)/shard_map/jit(_take)/gather | solution.py:60
  113.3 8.4 %reshape.161 = bf16[64,1,10776]{2,1,0:T(2,128)(2,1)S(1)} reshape(bf16[64,2,5388]{2,1,0:T(2,128)(2,1)} %all-to-all-done) | data formatting | bytes 2758656
  121.7 0.2 copy.95
  121.9 1.1 copy-done.1
  123.1 2.2 %reshape.155 = bf16[768,896,1,1]{1,0,2,3:T(8,128)(2,1)S(1)} reshape(bf16[64,10752]{1,0:T(8,128)(2,1)S(1)} %slice.13) | data formatting | bytes 2752512 | tf_op jit(solution)/shard_map/reshape | solution.py:46
  125.3 5.6 %fusion.3 = f32[2,768,8,128]{1,3,0,2:T(8,128)S(1)} fusion(bf16[8,2,128,896]{3,2,1,0:T(8,128)(2,1)} %gather_fusion.1, pred[8]{0:T(512)(128)(4,1)S(1)} %compare_and_fusion.1, bf16[768,896,1,1]{1,0,2,3:T(8,128)(2,1)S(1)} %reshape.155), kind=kOutput, calls=%fused_computation.6 | convolution fusion | flops 2820407296 | bytes 11337736 | tf_op jit(solution)/shard_map/rd,behd->erbh/dot_general | solution.py:61
  130.9 3.6 %copy.77 = f32[2,768,8,128]{1,3,2,0:T(8,128)} copy(f32[2,768,8,128]{1,3,0,2:T(8,128)S(1)} %fusion.3) | data formatting | bytes 12582912 | tf_op jit(solution)/shard_map/rd,behd->erbh/transpose | solution.py:61
  134.5 0.9 copy-done
  135.4 6.6 %copy.89 = f32[2,768,8,128]{3,1,0,2:T(8,128)} copy(f32[2,768,8,128]{1,3,0,2:T(8,128)} %copy-done) | data formatting | bytes 12582912
  142.0 4.4 %multiply_reduce_fusion = f32[2,768]{1,0:T(2,128)S(1)} fusion(f32[2,768,8,128]{3,1,0,2:T(8,128)} %copy.89, bf16[2,768,8,128]{3,1,0,2:T(8,128)(2,1)} %bitcast.56), kind=kLoop, calls=%fused_computation.2 | loop fusion | flops 4717056 | bytes 9443328 | tf_op jit(solution)/shard_map/berh,erbh->er/dot_general | solution.py:68
  146.4 0.1 all_gather_reshape.3
  146.6 13.0 %all_gather.11 = f32[8,64,12,2]{1,3,2,0:T(2,128)S(1)} all-gather(f32[1,64,12,2]{1,3,2,0:T(2,128)S(1)} %copy.78), channel_id=1, replica_groups=mesh['node'=64,'local'=8] {'local'}, dimensions={0}, use_global_device_ids=true | all-gather | bytes 55296 | tf_op jit(solution)/shard_map/all_gather | solution.py:75
  159.7 0.7 copy.80
  160.5 14.3 %all-to-all-start.1 = ((f32[64,12,2]{1,2,0:T(2,128)}), f32[64,12,2]{1,2,0:T(2,128)S(1)}, u32[]{:S(2)}, u32[]{:S(2)}) async-start(f32[64,12,2]{1,2,0:T(2,128)} %copy.80), calls=%async_computation.2 | async-start | bytes 131072 | tf_op jit(solution)/shard_map/all_to_all | solution.py:79
  174.8 0.7 slice_convert_fusion
  175.5 0.2 reshape.136
  175.7 0.1 copy.76
  175.9 13.1 %all-to-all-done.1 = f32[64,12,2]{1,2,0:T(2,128)S(1)} async-done(((f32[64,12,2]{1,2,0:T(2,128)}), f32[64,12,2]{1,2,0:T(2,128)S(1)}, u32[]{:S(2)}, u32[]{:S(2)}) %all-to-all-start.1) | async-done | bytes 6176 | tf_op jit(solution)/shard_map/all_to_all | solution.py:79
  189.0 0.4 convolution_bitcast_fusion
  189.4 0.1 copy.81
  189.5 0.6 fusion.13
  190.2 0.7 copy.82
  190.9 1.2 multiply_convert_fusion
  192.0 0.9 copy.83
  (26 shorter events, 0.8 us)
Async XLA Ops:
  22.3 91.0 %all-to-all-start = ((bf16[64,2,5388]{2,1,0:T(2,128)(2,1)}), bf16[64,2,5388]{2,1,0:T(2,128)(2,1)}, u32[]{:S(2)}, u32[]{:S(2)}) async-start(bf16[64,2,5388]{2,1,0:T(2,128)(2,1)} %reshape.160), calls=%async_computation | async-start | bytes 2818048 | tf_op jit(solution)/shard_map/all_to_all | solution.py:45
  41.7 100.3 %all-gather.3.cloned.1.call-start = ((), (), s32[]{:S(2)}) async-start(), calls=%async_computation.4 | async-start | bytes 3538944 | tf_op jit(solution)/shard_map/all_gather | solution.py:67
  42.4 148.4 %reduce-scatter.2.cloned.1.call-start = ((), (), s32[]{:S(2)}) async-start(), calls=%async_computation.3 | async-start | bytes 7077888 | tf_op jit(solution)/shard_map/reduce_scatter | solution.py:76
  45.9 17.0 %collective-permute-start = (bf16[2,128,896]{2,1,0:T(8,128)(2,1)}, bf16[2,128,896]{2,1,0:T(8,128)(2,1)S(1)}, u32[]{:S(2)}, u32[]{:S(2)}) collective-permute-start(bf16[2,128,896]{2,1,0:T(8,128)(2,1)} %get-tuple-element.19), channel_id=1, source_target_pairs={{0,1},{1,2},{2,3},{3,4},{4,5},{5,6},{6,7},{7,0},{8,9},{9,10},{10,1... | collective-permute-start | bytes 1376264 | tf_op jit(solution)/shard_map/ppermute | solution.py:56
  48.0 20.6 %collective-permute-start.1 = (bf16[2,128,896]{2,1,0:T(8,128)(2,1)}, bf16[2,128,896]{2,1,0:T(8,128)(2,1)S(1)}, u32[]{:S(2)}, u32[]{:S(2)}) collective-permute-start(bf16[2,128,896]{2,1,0:T(8,128)(2,1)} %get-tuple-element.18), channel_id=1, source_target_pairs={{0,2},{1,3},{2,4},{3,5},{4,6},{5,7},{6,0},{7,1},{8,10},{9,11},{10,... | collective-permute-start | bytes 1376264 | tf_op jit(solution)/shard_map/ppermute | solution.py:56
  51.2 35.7 %collective-permute-start.2 = (bf16[2,128,896]{2,1,0:T(8,128)(2,1)}, bf16[2,128,896]{2,1,0:T(8,128)(2,1)S(1)}, u32[]{:S(2)}, u32[]{:S(2)}) collective-permute-start(bf16[2,128,896]{2,1,0:T(8,128)(2,1)} %get-tuple-element.17), channel_id=1, source_target_pairs={{0,3},{1,4},{2,5},{3,6},{4,7},{5,0},{6,1},{7,2},{8,11},{9,12},{10,... | collective-permute-start | bytes 1376264 | tf_op jit(solution)/shard_map/ppermute | solution.py:56
  54.7 46.9 %collective-permute-start.3 = (bf16[2,128,896]{2,1,0:T(8,128)(2,1)}, bf16[2,128,896]{2,1,0:T(8,128)(2,1)S(1)}, u32[]{:S(2)}, u32[]{:S(2)}) collective-permute-start(bf16[2,128,896]{2,1,0:T(8,128)(2,1)} %get-tuple-element.16), channel_id=1, source_target_pairs={{0,4},{1,5},{2,6},{3,7},{4,0},{5,1},{6,2},{7,3},{8,12},{9,13},{10,... | collective-permute-start | bytes 1376264 | tf_op jit(solution)/shard_map/ppermute | solution.py:56
  57.0 47.2 %collective-permute-start.4 = (bf16[2,128,896]{2,1,0:T(8,128)(2,1)}, bf16[2,128,896]{2,1,0:T(8,128)(2,1)S(1)}, u32[]{:S(2)}, u32[]{:S(2)}) collective-permute-start(bf16[2,128,896]{2,1,0:T(8,128)(2,1)} %get-tuple-element.15), channel_id=1, source_target_pairs={{0,5},{1,6},{2,7},{3,0},{4,1},{5,2},{6,3},{7,4},{8,13},{9,14},{10,... | collective-permute-start | bytes 1376264 | tf_op jit(solution)/shard_map/ppermute | solution.py:56
  62.8 43.2 %collective-permute-start.5 = (bf16[2,128,896]{2,1,0:T(8,128)(2,1)S(1)}, bf16[2,128,896]{2,1,0:T(8,128)(2,1)S(1)}, u32[]{:S(2)}, u32[]{:S(2)}) collective-permute-start(bf16[2,128,896]{2,1,0:T(8,128)(2,1)S(1)} %get-tuple-element.20), channel_id=1, source_target_pairs={{0,6},{1,7},{2,0},{3,1},{4,2},{5,3},{6,4},{7,5},{8,14},{9,15},{10,... | collective-permute-start | bytes 1376264 | tf_op jit(solution)/shard_map/ppermute | solution.py:56
  68.6 39.1 %collective-permute-start.6 = (bf16[2,128,896]{2,1,0:T(8,128)(2,1)S(1)}, bf16[2,128,896]{2,1,0:T(8,128)(2,1)S(1)}, u32[]{:S(2)}, u32[]{:S(2)}) collective-permute-start(bf16[2,128,896]{2,1,0:T(8,128)(2,1)S(1)} %get-tuple-element.14), channel_id=1, source_target_pairs={{0,7},{1,0},{2,1},{3,2},{4,3},{5,4},{6,5},{7,6},{8,15},{9,8},{10,9... | collective-permute-start | bytes 1376264 | tf_op jit(solution)/shard_map/ppermute | solution.py:56
  121.9 1.1 copy-start.1
  130.9 4.5 %copy-start = (f32[2,768,8,128]{1,3,0,2:T(8,128)}, f32[2,768,8,128]{1,3,0,2:T(8,128)S(1)}, u32[]{:S(2)}) copy-start(f32[2,768,8,128]{1,3,0,2:T(8,128)S(1)} %fusion.3) | copy-start | bytes 18874372
  160.5 28.5 %all-to-all-start.1 = ((f32[64,12,2]{1,2,0:T(2,128)}), f32[64,12,2]{1,2,0:T(2,128)S(1)}, u32[]{:S(2)}, u32[]{:S(2)}) async-start(f32[64,12,2]{1,2,0:T(2,128)} %copy.80), calls=%async_computation.2 | async-start | bytes 131072 | tf_op jit(solution)/shard_map/all_to_all | solution.py:79
Sparse Core Ops, SparseCore 0:
  44.6 62.1 all-gather.2
  135.6 49.7 reduce-scatter.1

commit v8 on v5

--- a/solution.py
+++ b/solution.py
@@ -43,33 +43,44 @@
         axis=1,
     )
     payload_in = lax.all_to_all(payload, "node", split_axis=0, concat_axis=0, tiled=True)
-    rows_in = payload_in[:, : capacity * width].reshape(slot_rows, width)
-    prob_in = payload_in[:, capacity * width :]
     local_count = lax.axis_size("local")
     local_index = lax.axis_index("local")
     pieces = []
+    saved_pieces = []
     for step in range(local_count):
         target = (local_index + step) % local_count
         piece = lax.dynamic_slice_in_dim(weight_down, target * width, width, axis=2)
+        saved_piece = saved_hidden
         if step:
             pairs = [(j, (j + step) % local_count) for j in range(local_count)]
             piece = lax.ppermute(piece, "local", perm=pairs)
+            saved_piece = lax.ppermute(saved_piece, "local", perm=pairs)
         pieces.append(piece)
+        saved_pieces.append(saved_piece)
     stacked = jnp.stack(pieces, axis=0)
     block_order = (local_index - jnp.arange(local_count, dtype=jnp.int32)) % local_count
     weight_blocks = jnp.take(stacked, block_order, axis=0)
+    score_weights = jnp.einsum(
+        "berh,behd->erd",
+        jnp.stack(saved_pieces, axis=0),
+        stacked,
+        preferred_element_type=jnp.float32,
+    )
+    payload_in, score_weights = lax.optimization_barrier((payload_in, score_weights))
+    rows_in = payload_in[:, : capacity * width].reshape(slot_rows, width)
+    prob_in = payload_in[:, capacity * width :]
     partial_grads = jnp.einsum(
         "rd,behd->erbh",
         rows_in,
         weight_blocks,
         preferred_element_type=jnp.float32,
     ).reshape(expert_count, slot_rows, -1)
+    partial_scores = jnp.sum(rows_in.astype(jnp.float32)[None] * score_weights, axis=2)
+    partial_value = jnp.transpose(partial_scores).reshape(node_count, capacity, expert_count)
+    summed = jnp.sum(lax.all_gather(partial_value, "local", axis=0, tiled=False), axis=0)
     hidden_grads = lax.psum_scatter(partial_grads, "local", scatter_dimension=2, tiled=True)
     scales = jnp.transpose(prob_in.reshape(slot_rows, expert_count).astype(jnp.float32))
     grad_hidden = (scales[:, :, None] * hidden_grads).astype(jnp.bfloat16)
-    partial_value = jnp.sum(saved_hidden.astype(jnp.float32) * hidden_grads, axis=2)
-    partial_value = jnp.transpose(partial_value).reshape(node_count, capacity, expert_count)
-    summed = jnp.sum(lax.all_gather(partial_value, "local", axis=0, tiled=False), axis=0)
     returned = lax.all_to_all(summed, "node", split_axis=0, concat_axis=0, tiled=True)
     per_node = jnp.einsum("tms,msc->tmc", select_full, returned, precision=lax.Precision.HIGHEST)
     grad_probs = jnp.einsum("tjm,tmc->tjc", listed, per_node, precision=lax.Precision.HIGHEST)

time: 236 us -> 223 us (0.945)
  waiting for transfers between devices: 91.3 us -> 42 us
  starting transfers between devices: 56.5 us -> 69.8 us
  local copies, waits for them, and re-layouts: 44.3 us -> 56.7 us
  matrix products: 7.52 us -> 14.1 us
  other arithmetic: 6.87 us -> 11 us
    reduce_scatter x1, waiting for transfers between devices: 49 us -> 0.01 us  [on_device(): lax.psum_scatter(partial_grads, 'local', scatter_dimension=2, tiled=True)]
    ppermute x0 -> x7, starting transfers between devices: none -> 19.3 us  [on_device(): saved_piece = lax.ppermute(saved_piece, 'local', perm=pairs)]
    unnamed x18 -> x32, local copies, waits for them, and re-layouts: 21.8 us -> 32.9 us
    dot_general x0 -> x1, matrix products: none -> 6.6 us  [on_device(): jnp.einsum('berh,behd->erd', jnp.stack(saved_pieces, axis=0), stacked, pr...]
    ppermute x0 -> x7, waiting for transfers between devices: none -> 6.36 us  [on_device(): saved_piece = lax.ppermute(saved_piece, 'local', perm=pairs)]
    ppermute x7, waiting for transfers between devices: 28.9 us -> 22.5 us  [on_device(): piece = lax.ppermute(piece, 'local', perm=pairs)]
    ppermute x7, starting transfers between devices: 21.8 us -> 16.4 us  [on_device(): piece = lax.ppermute(piece, 'local', perm=pairs)]
  transfers between devices with their start and end apart: 10 -> 17, of which waited for: 6 -> 8; matrix products, arithmetic and copies ran while one was open for 8% -> 20% of each run, Pallas kernels for 0% -> 0%
where the time goes in v8:
time: 223 us; the launch traced here: 222 us
  starting transfers between devices  69.8 us (31%)
  local copies, waits for them, and re-layouts  56.7 us (25%)
  waiting for transfers between devices  42 us (19%)
  between operations  14.6 us (7%)
  matrix products  14.1 us (6%)
  blocking collectives  13.5 us (6%)
  other arithmetic  11 us (5%)
    unnamed x32, local copies, waits for them, and re-layouts  32.9 us
    ppermute x7, waiting for transfers between devices, on_device(): piece = lax.ppermute(piece, 'local', perm=pairs)  22.5 us
    all_to_all x1, starting transfers between devices, on_device(): lax.all_to_all(payload, 'node', split_axis=0, concat_axis=0, tiled=True)  19.3 us
    ppermute x7, starting transfers between devices, on_device(): saved_piece = lax.ppermute(saved_piece, 'local', perm=pairs)  19.3 us
    ppermute x7, starting transfers between devices, on_device(): piece = lax.ppermute(piece, 'local', perm=pairs)  16.4 us
    all_to_all x1, starting transfers between devices, on_device(): lax.all_to_all(summed, 'node', split_axis=0, concat_axis=0, tiled=True)  14.7 us
    all_gather x1, blocking collectives, on_device(): lax.all_gather(partial_value, 'local', axis=0, tiled=False)  13.5 us
    all_to_all x1, waiting for transfers between devices, on_device(): lax.all_to_all(summed, 'node', split_axis=0, concat_axis=0, tiled=True)  13.1 us
  transfers between devices with their start and end apart: 17, of which 8 were waited for; matrix products, arithmetic and copies ran while one was open for 20% of the time, Pallas kernels for 0%

profile of v8, /device:TPU:1, one launch (start us, length us, event | category | flops | bytes accessed | tf_op | source)
XLA Modules:
  0.0 221.8 jit_solution(18092324520098051074)
XLA Ops:
  7.2 0.8 copy.68
  8.6 2.2 %convert_reduce_fusion = (s32[64,12]{1,0:T(8,128)S(1)}, s32[64,12]{1,0:T(8,128)S(1)}) fusion(s32[128,64]{0,1:T(8,128)S(1)} %copy.69, pred[128,64]{0,1:T(8,128)(4,1)S(1)} %broadcast_compare_fusion), kind=kLoop, calls=%fused_computation.17 | loop fusion | flops 588288 | bytes 47104 | tf_op jit(solution)/shard_map/reduce_sum | solution.py:29
  10.8 0.6 compare_and_fusion
  11.6 1.0 concatenate.6
  12.5 2.8 %gather_fusion = bf16[768,896]{1,0:T(8,128)(2,1)S(1)} fusion(bf16[129,896]{1,0:T(8,128)(2,1)S(1)} %concatenate.6, s32[1024]{0:T(1024)S(1)} %pad_clamp_fusion.1), kind=kCustom, calls=%fused_computation | custom fusion | bytes 2755584 | tf_op jit(solution)/shard_map/jit(_take)/gather | solution.py:10
  17.4 0.5 convolution_convert_fusion
  18.2 0.5 broadcast.177
  18.7 1.6 reduce
  20.4 2.3 %reshape.162 = bf16[64,2,5388]{2,1,0:T(2,128)(2,1)} reshape(bf16[64,10776]{1,0:T(8,128)(2,1)S(1)} %reduce) | data formatting | bytes 2758656
  22.7 19.3 %all-to-all-start = ((bf16[64,2,5388]{2,1,0:T(2,128)(2,1)}), bf16[64,2,5388]{2,1,0:T(2,128)(2,1)}, u32[]{:S(2)}, u32[]{:S(2)}) async-start(bf16[64,2,5388]{2,1,0:T(2,128)(2,1)} %reshape.162), calls=%async_computation | async-start | bytes 2818048 | tf_op jit(solution)/shard_map/all_to_all | solution.py:45
  42.1 2.1 collective-permute-start
  44.3 3.2 %collective-permute-start.1 = (bf16[2,768,128]{2,1,0:T(8,128)(2,1)}, bf16[2,768,128]{2,1,0:T(8,128)(2,1)}, u32[]{:S(2)}, u32[]{:S(2)}) collective-permute-start(bf16[2,768,128]{2,1,0:T(8,128)(2,1)} %param.9), channel_id=1, source_target_pairs={{0,2},{1,3},{2,4},{3,5},{4,6},{5,7},{6,0},{7,1},{8,10},{9,11},{10,... | collective-permute-start | bytes 1179656 | tf_op jit(solution)/shard_map/ppermute | solution.py:57
  47.5 3.5 %collective-permute-start.2 = (bf16[2,768,128]{2,1,0:T(8,128)(2,1)}, bf16[2,768,128]{2,1,0:T(8,128)(2,1)}, u32[]{:S(2)}, u32[]{:S(2)}) collective-permute-start(bf16[2,768,128]{2,1,0:T(8,128)(2,1)} %param.9), channel_id=1, source_target_pairs={{0,3},{1,4},{2,5},{3,6},{4,7},{5,0},{6,1},{7,2},{8,11},{9,12},{10,... | collective-permute-start | bytes 1179656 | tf_op jit(solution)/shard_map/ppermute | solution.py:57
  51.0 2.3 %collective-permute-start.3 = (bf16[2,768,128]{2,1,0:T(8,128)(2,1)}, bf16[2,768,128]{2,1,0:T(8,128)(2,1)}, u32[]{:S(2)}, u32[]{:S(2)}) collective-permute-start(bf16[2,768,128]{2,1,0:T(8,128)(2,1)} %param.9), channel_id=1, source_target_pairs={{0,4},{1,5},{2,6},{3,7},{4,0},{5,1},{6,2},{7,3},{8,12},{9,13},{10,... | collective-permute-start | bytes 1179656 | tf_op jit(solution)/shard_map/ppermute | solution.py:57
  53.3 3.9 %collective-permute-start.4 = (bf16[2,768,128]{2,1,0:T(8,128)(2,1)}, bf16[2,768,128]{2,1,0:T(8,128)(2,1)}, u32[]{:S(2)}, u32[]{:S(2)}) collective-permute-start(bf16[2,768,128]{2,1,0:T(8,128)(2,1)} %param.9), channel_id=1, source_target_pairs={{0,5},{1,6},{2,7},{3,0},{4,1},{5,2},{6,3},{7,4},{8,13},{9,14},{10,... | collective-permute-start | bytes 1179656 | tf_op jit(solution)/shard_map/ppermute | solution.py:57
  57.3 1.8 bitcast_dynamic-update-slice_fusion.15
  59.2 2.2 %constant_dynamic-slice_fusion = (bf16[2,128,896]{2,1,0:T(8,128)(2,1)S(1)}, bf16[2,128,896]{2,1,0:T(8,128)(2,1)S(1)}, bf16[2,128,896]{2,1,0:T(8,128)(2,1)S(1)}, ...) fusion(bf16[2,128,7168]{2,1,0:T(8,128)(2,1)} %param.8, ...), kind=kLoop, calls=%fused_computation.60 | loop fusion | bytes 6422556 | tf_op jit(solution)/shard_map/dynamic_slice | solution.py:52
  61.4 1.8 bitcast_dynamic-update-slice_fusion.7
  63.3 2.7 %collective-permute-start.5 = (bf16[2,768,128]{2,1,0:T(8,128)(2,1)}, bf16[2,768,128]{2,1,0:T(8,128)(2,1)S(1)}, u32[]{:S(2)}, u32[]{:S(2)}) collective-permute-start(bf16[2,768,128]{2,1,0:T(8,128)(2,1)} %param.9), channel_id=1, source_target_pairs={{0,6},{1,7},{2,0},{3,1},{4,2},{5,3},{6,4},{7,5},{8,14},{9,15},{10,... | collective-permute-start | bytes 1179656 | tf_op jit(solution)/shard_map/ppermute | solution.py:57
  66.0 1.8 bitcast_dynamic-update-slice_fusion.14
  67.9 1.5 collective-permute-start.6
  69.4 1.8 bitcast_dynamic-update-slice_fusion.13
  71.5 1.8 bitcast_dynamic-update-slice_fusion.12
  73.3 6.3 %collective-permute-done.3 = bf16[2,768,128]{2,1,0:T(8,128)(2,1)} collective-permute-done((bf16[2,768,128]{2,1,0:T(8,128)(2,1)}, bf16[2,768,128]{2,1,0:T(8,128)(2,1)}, u32[]{:S(2)}, u32[]{:S(2)}) %collective-permute-start.3) | collective-permute-done | bytes 393248 | tf_op jit(solution)/shard_map/ppermute | solution.py:57
  79.6 1.9 collective-permute-start.8
  81.6 1.8 bitcast_dynamic-update-slice_fusion.11
  83.4 4.6 %collective-permute-start.9 = (bf16[2,128,896]{2,1,0:T(8,128)(2,1)S(1)}, bf16[2,128,896]{2,1,0:T(8,128)(2,1)S(1)}, u32[]{:S(2)}, u32[]{:S(2)}) collective-permute-start(bf16[2,128,896]{2,1,0:T(8,128)(2,1)S(1)} %get-tuple-element.21), channel_id=1, source_target_pairs={{0,3},{1,4},{2,5},{3,6},{4,7},{5,0},{6,1},{7,2},{8,11},{9,12},{10,... | collective-permute-start | bytes 1376264 | tf_op jit(solution)/shard_map/ppermute | solution.py:56
  88.0 1.8 bitcast_dynamic-update-slice_fusion.10
  89.8 1.9 collective-permute-start.10
  91.7 0.8 bitcast_dynamic-update-slice_fusion.9
  92.5 4.5 %collective-permute-start.11 = (bf16[2,128,896]{2,1,0:T(8,128)(2,1)S(1)}, bf16[2,128,896]{2,1,0:T(8,128)(2,1)S(1)}, u32[]{:S(2)}, u32[]{:S(2)}) collective-permute-start(bf16[2,128,896]{2,1,0:T(8,128)(2,1)S(1)} %get-tuple-element.19), channel_id=1, source_target_pairs={{0,5},{1,6},{2,7},{3,0},{4,1},{5,2},{6,3},{7,4},{8,13},{9,14},{10,... | collective-permute-start | bytes 1376264 | tf_op jit(solution)/shard_map/ppermute | solution.py:56
  97.0 0.8 bitcast_dynamic-update-slice_fusion.8
  97.8 2.5 %collective-permute-start.12 = (bf16[2,128,896]{2,1,0:T(8,128)(2,1)S(1)}, bf16[2,128,896]{2,1,0:T(8,128)(2,1)S(1)}, u32[]{:S(2)}, u32[]{:S(2)}) collective-permute-start(bf16[2,128,896]{2,1,0:T(8,128)(2,1)S(1)} %get-tuple-element.24), channel_id=1, source_target_pairs={{0,6},{1,7},{2,0},{3,1},{4,2},{5,3},{6,4},{7,5},{8,14},{9,15},{10,... | collective-permute-start | bytes 1376264 | tf_op jit(solution)/shard_map/ppermute | solution.py:56
  100.3 0.8 bitcast_dynamic-update-slice_fusion.6
  101.2 2.2 %collective-permute-done.8 = bf16[2,128,896]{2,1,0:T(8,128)(2,1)S(1)} collective-permute-done((bf16[2,128,896]{2,1,0:T(8,128)(2,1)S(1)}, bf16[2,128,896]{2,1,0:T(8,128)(2,1)S(1)}, u32[]{:S(2)}, u32[]{:S(2)}) %collective-permute-start.8) | collective-permute-done | bytes 458784 | tf_op jit(solution)/shard_map/ppermute | solution.py:56
  103.4 0.7 collective-permute-start.13
  104.1 0.8 bitcast_dynamic-update-slice_fusion.5
  104.9 0.8 collective-permute-done.9
  105.7 0.8 bitcast_dynamic-update-slice_fusion.4
  106.5 10.9 %collective-permute-done.10 = bf16[2,128,896]{2,1,0:T(8,128)(2,1)S(1)} collective-permute-done((bf16[2,128,896]{2,1,0:T(8,128)(2,1)S(1)}, bf16[2,128,896]{2,1,0:T(8,128)(2,1)S(1)}, u32[]{:S(2)}, u32[]{:S(2)}) %collective-permute-start.10) | collective-permute-done | bytes 458784 | tf_op jit(solution)/shard_map/ppermute | solution.py:56
  117.4 0.8 bitcast_dynamic-update-slice_fusion.3
  118.2 2.9 %collective-permute-done.11 = bf16[2,128,896]{2,1,0:T(8,128)(2,1)S(1)} collective-permute-done((bf16[2,128,896]{2,1,0:T(8,128)(2,1)S(1)}, bf16[2,128,896]{2,1,0:T(8,128)(2,1)S(1)}, u32[]{:S(2)}, u32[]{:S(2)}) %collective-permute-start.11) | collective-permute-done | bytes 458784 | tf_op jit(solution)/shard_map/ppermute | solution.py:56
  121.1 0.8 bitcast_dynamic-update-slice_fusion.2
  121.9 5.7 %collective-permute-done.12 = bf16[2,128,896]{2,1,0:T(8,128)(2,1)S(1)} collective-permute-done((bf16[2,128,896]{2,1,0:T(8,128)(2,1)S(1)}, bf16[2,128,896]{2,1,0:T(8,128)(2,1)S(1)}, u32[]{:S(2)}, u32[]{:S(2)}) %collective-permute-start.12) | collective-permute-done | bytes 458784 | tf_op jit(solution)/shard_map/ppermute | solution.py:56
  127.6 0.8 bitcast_dynamic-update-slice_fusion.1
  128.5 0.8 bitcast_dynamic-update-slice_fusion
  129.3 5.0 %gather_fusion.1 = bf16[8,2,128,896]{3,2,1,0:T(8,128)(2,1)} fusion(bf16[8,2,128,896]{3,2,0,1:T(8,128)(2,1)} %bitcast_dynamic-update-slice_fusion, s32[1024]{0:T(1024)S(1)} %pad_clamp_fusion), kind=kCustom, calls=%fused_computation.1 | custom fusion | bytes 7340064 | tf_op jit(solution)/shard_map/jit(_take)/gather | solution.py:62
  134.3 6.6 %convolution_bitcast_fusion = f32[2,768,896]{2,1,0:T(8,128)} fusion(bf16[8,2,768,128]{3,2,0,1:T(8,128)(2,1)S(1)} %copy-done.1, bf16[8,2,128,896]{3,2,0,1:T(8,128)(2,1)} %bitcast_dynamic-update-slice_fusion), kind=kOutput, calls=%fused_computation.7 | convolution fusion | flops 2818572288 | bytes 12320768 | tf_op jit(solution)/shard_map/berh,behd->erd/dot_general | solution.py:63
  141.0 8.4 %reshape.163 = bf16[64,1,10776]{2,1,0:T(2,128)(2,1)S(1)} reshape(bf16[64,2,5388]{2,1,0:T(2,128)(2,1)} %all-to-all-done) | data formatting | bytes 2758656
  149.5 1.1 copy-done
  150.7 2.2 reshape.160
  152.9 5.6 %fusion.3 = f32[2,768,8,128]{1,3,0,2:T(8,128)S(1)} fusion(bf16[8,2,128,896]{3,2,1,0:T(8,128)(2,1)} %gather_fusion.1, pred[8]{0:T(512)(128)(4,1)S(1)} %compare_and_fusion.1, bf16[768,896,1,1]{1,0,2,3:T(8,128)(2,1)S(1)} %reshape.160), kind=kOutput, calls=%fused_computation.6 | convolution fusion | flops 2820407296 | bytes 11337736 | tf_op jit(solution)/shard_map/rd,behd->erbh/dot_general | solution.py:72
  158.5 3.3 %copy.77 = f32[2,768,8,128]{1,3,2,0:T(8,128)} copy(f32[2,768,8,128]{1,3,0,2:T(8,128)S(1)} %fusion.3) | data formatting | bytes 12582912 | tf_op jit(solution)/shard_map/rd,behd->erbh/transpose | solution.py:72
  161.7 2.2 reshape.138
  164.1 3.5 %multiply_reduce_fusion = f32[2,768]{1,0:T(2,128)S(1)} fusion(f32[2,768,896]{2,1,0:T(8,128)} %convolution_bitcast_fusion, f32[768,896]{1,0:T(8,128)S(1)} %convert_element_type.31), kind=kLoop, calls=%fused_computation.2 | loop fusion | flops 2750976 | bytes 8263680 | tf_op jit(solution)/shard_map/reduce_sum | solution.py:78
  167.8 13.5 %all_gather.3 = f32[8,64,12,2]{1,3,2,0:T(2,128)S(1)} all-gather(f32[1,64,12,2]{1,3,2,0:T(2,128)S(1)} %copy.78), channel_id=1, replica_groups=mesh['node'=64,'local'=8] {'local'}, dimensions={0}, use_global_device_ids=true | all-gather | bytes 55296 | tf_op jit(solution)/shard_map/all_gather | solution.py:80
  181.3 0.7 copy.80
  182.1 14.7 %all-to-all-start.1 = ((f32[64,12,2]{1,2,0:T(2,128)}), f32[64,12,2]{1,2,0:T(2,128)S(1)}, u32[]{:S(2)}, u32[]{:S(2)}) async-start(f32[64,12,2]{1,2,0:T(2,128)} %copy.80), calls=%async_computation.2 | async-start | bytes 131072 | tf_op jit(solution)/shard_map/all_to_all | solution.py:84
  196.8 0.7 slice_convert_fusion
  197.8 13.1 %all-to-all-done.1 = f32[64,12,2]{1,2,0:T(2,128)S(1)} async-done(((f32[64,12,2]{1,2,0:T(2,128)}), f32[64,12,2]{1,2,0:T(2,128)S(1)}, u32[]{:S(2)}, u32[]{:S(2)}) %all-to-all-start.1) | async-done | bytes 6176 | tf_op jit(solution)/shard_map/all_to_all | solution.py:84
  211.5 0.6 fusion.13
  212.1 0.7 copy.82
  212.8 1.2 multiply_convert_fusion
  214.0 0.9 copy.83
  (55 shorter events, 4.9 us)
Async XLA Ops:
  8.6 3.0 %copy-start.3 = (pred[128,64]{0,1:T(8,128)(4,1)}, pred[128,64]{0,1:T(8,128)(4,1)S(1)}, u32[]{:S(2)}) copy-start(pred[128,64]{0,1:T(8,128)(4,1)S(1)} %broadcast_compare_fusion) | copy-start | bytes 24580
  15.4 0.7 copy-start.2
  16.1 0.7 copy-start.5
  16.4 1.0 copy-start.4
  22.7 118.2 %all-to-all-start = ((bf16[64,2,5388]{2,1,0:T(2,128)(2,1)}), bf16[64,2,5388]{2,1,0:T(2,128)(2,1)}, u32[]{:S(2)}, u32[]{:S(2)}) async-start(bf16[64,2,5388]{2,1,0:T(2,128)(2,1)} %reshape.162), calls=%async_computation | async-start | bytes 2818048 | tf_op jit(solution)/shard_map/all_to_all | solution.py:45
  42.1 170.8 %reduce-scatter.2.cloned.1.call-start = ((), (), s32[]{:S(2)}) async-start(), calls=%async_computation.3 | async-start | bytes 7077888 | tf_op jit(solution)/shard_map/reduce_scatter | solution.py:81
  42.1 21.2 %collective-permute-start = (bf16[2,768,128]{2,1,0:T(8,128)(2,1)}, bf16[2,768,128]{2,1,0:T(8,128)(2,1)}, u32[]{:S(2)}, u32[]{:S(2)}) collective-permute-start(bf16[2,768,128]{2,1,0:T(8,128)(2,1)} %param.9), channel_id=1, source_target_pairs={{0,1},{1,2},{2,3},{3,4},{4,5},{5,6},{6,7},{7,0},{8,9},{9,10},{10,1... | collective-permute-start | bytes 1179656 | tf_op jit(solution)/shard_map/ppermute | solution.py:57
  44.3 23.6 %collective-permute-start.1 = (bf16[2,768,128]{2,1,0:T(8,128)(2,1)}, bf16[2,768,128]{2,1,0:T(8,128)(2,1)}, u32[]{:S(2)}, u32[]{:S(2)}) collective-permute-start(bf16[2,768,128]{2,1,0:T(8,128)(2,1)} %param.9), channel_id=1, source_target_pairs={{0,2},{1,3},{2,4},{3,5},{4,6},{5,7},{6,0},{7,1},{8,10},{9,11},{10,... | collective-permute-start | bytes 1179656 | tf_op jit(solution)/shard_map/ppermute | solution.py:57
  47.5 23.7 %collective-permute-start.2 = (bf16[2,768,128]{2,1,0:T(8,128)(2,1)}, bf16[2,768,128]{2,1,0:T(8,128)(2,1)}, u32[]{:S(2)}, u32[]{:S(2)}) collective-permute-start(bf16[2,768,128]{2,1,0:T(8,128)(2,1)} %param.9), channel_id=1, source_target_pairs={{0,3},{1,4},{2,5},{3,6},{4,7},{5,0},{6,1},{7,2},{8,11},{9,12},{10,... | collective-permute-start | bytes 1179656 | tf_op jit(solution)/shard_map/ppermute | solution.py:57
  51.0 28.6 %collective-permute-start.3 = (bf16[2,768,128]{2,1,0:T(8,128)(2,1)}, bf16[2,768,128]{2,1,0:T(8,128)(2,1)}, u32[]{:S(2)}, u32[]{:S(2)}) collective-permute-start(bf16[2,768,128]{2,1,0:T(8,128)(2,1)} %param.9), channel_id=1, source_target_pairs={{0,4},{1,5},{2,6},{3,7},{4,0},{5,1},{6,2},{7,3},{8,12},{9,13},{10,... | collective-permute-start | bytes 1179656 | tf_op jit(solution)/shard_map/ppermute | solution.py:57
  53.3 30.1 %collective-permute-start.4 = (bf16[2,768,128]{2,1,0:T(8,128)(2,1)}, bf16[2,768,128]{2,1,0:T(8,128)(2,1)}, u32[]{:S(2)}, u32[]{:S(2)}) collective-permute-start(bf16[2,768,128]{2,1,0:T(8,128)(2,1)} %param.9), channel_id=1, source_target_pairs={{0,5},{1,6},{2,7},{3,0},{4,1},{5,2},{6,3},{7,4},{8,13},{9,14},{10,... | collective-permute-start | bytes 1179656 | tf_op jit(solution)/shard_map/ppermute | solution.py:57
  63.3 26.5 %collective-permute-start.5 = (bf16[2,768,128]{2,1,0:T(8,128)(2,1)}, bf16[2,768,128]{2,1,0:T(8,128)(2,1)S(1)}, u32[]{:S(2)}, u32[]{:S(2)}) collective-permute-start(bf16[2,768,128]{2,1,0:T(8,128)(2,1)} %param.9), channel_id=1, source_target_pairs={{0,6},{1,7},{2,0},{3,1},{4,2},{5,3},{6,4},{7,5},{8,14},{9,15},{10,... | collective-permute-start | bytes 1179656 | tf_op jit(solution)/shard_map/ppermute | solution.py:57
  67.9 24.6 %collective-permute-start.6 = (bf16[2,768,128]{2,1,0:T(8,128)(2,1)}, bf16[2,768,128]{2,1,0:T(8,128)(2,1)S(1)}, u32[]{:S(2)}, u32[]{:S(2)}) collective-permute-start(bf16[2,768,128]{2,1,0:T(8,128)(2,1)} %param.9), channel_id=1, source_target_pairs={{0,7},{1,0},{2,1},{3,2},{4,3},{5,4},{6,5},{7,6},{8,15},{9,8},{10,9... | collective-permute-start | bytes 1179656 | tf_op jit(solution)/shard_map/ppermute | solution.py:57
  71.2 26.6 %collective-permute-start.7 = (bf16[2,128,896]{2,1,0:T(8,128)(2,1)S(1)}, bf16[2,128,896]{2,1,0:T(8,128)(2,1)S(1)}, u32[]{:S(2)}, u32[]{:S(2)}) collective-permute-start(bf16[2,128,896]{2,1,0:T(8,128)(2,1)S(1)} %get-tuple-element.23), channel_id=1, source_target_pairs={{0,1},{1,2},{2,3},{3,4},{4,5},{5,6},{6,7},{7,0},{8,9},{9,10},{10,1... | collective-permute-start | bytes 1376264 | tf_op jit(solution)/shard_map/ppermute | solution.py:56
  79.6 23.8 %collective-permute-start.8 = (bf16[2,128,896]{2,1,0:T(8,128)(2,1)S(1)}, bf16[2,128,896]{2,1,0:T(8,128)(2,1)S(1)}, u32[]{:S(2)}, u32[]{:S(2)}) collective-permute-start(bf16[2,128,896]{2,1,0:T(8,128)(2,1)S(1)} %get-tuple-element.22), channel_id=1, source_target_pairs={{0,2},{1,3},{2,4},{3,5},{4,6},{5,7},{6,0},{7,1},{8,10},{9,11},{10,... | collective-permute-start | bytes 1376264 | tf_op jit(solution)/shard_map/ppermute | solution.py:56
  83.4 22.3 %collective-permute-start.9 = (bf16[2,128,896]{2,1,0:T(8,128)(2,1)S(1)}, bf16[2,128,896]{2,1,0:T(8,128)(2,1)S(1)}, u32[]{:S(2)}, u32[]{:S(2)}) collective-permute-start(bf16[2,128,896]{2,1,0:T(8,128)(2,1)S(1)} %get-tuple-element.21), channel_id=1, source_target_pairs={{0,3},{1,4},{2,5},{3,6},{4,7},{5,0},{6,1},{7,2},{8,11},{9,12},{10,... | collective-permute-start | bytes 1376264 | tf_op jit(solution)/shard_map/ppermute | solution.py:56
  89.8 27.6 %collective-permute-start.10 = (bf16[2,128,896]{2,1,0:T(8,128)(2,1)S(1)}, bf16[2,128,896]{2,1,0:T(8,128)(2,1)S(1)}, u32[]{:S(2)}, u32[]{:S(2)}) collective-permute-start(bf16[2,128,896]{2,1,0:T(8,128)(2,1)S(1)} %get-tuple-element.20), channel_id=1, source_target_pairs={{0,4},{1,5},{2,6},{3,7},{4,0},{5,1},{6,2},{7,3},{8,12},{9,13},{10,... | collective-permute-start | bytes 1376264 | tf_op jit(solution)/shard_map/ppermute | solution.py:56
  92.5 28.7 %collective-permute-start.11 = (bf16[2,128,896]{2,1,0:T(8,128)(2,1)S(1)}, bf16[2,128,896]{2,1,0:T(8,128)(2,1)S(1)}, u32[]{:S(2)}, u32[]{:S(2)}) collective-permute-start(bf16[2,128,896]{2,1,0:T(8,128)(2,1)S(1)} %get-tuple-element.19), channel_id=1, source_target_pairs={{0,5},{1,6},{2,7},{3,0},{4,1},{5,2},{6,3},{7,4},{8,13},{9,14},{10,... | collective-permute-start | bytes 1376264 | tf_op jit(solution)/shard_map/ppermute | solution.py:56
  97.8 29.8 %collective-permute-start.12 = (bf16[2,128,896]{2,1,0:T(8,128)(2,1)S(1)}, bf16[2,128,896]{2,1,0:T(8,128)(2,1)S(1)}, u32[]{:S(2)}, u32[]{:S(2)}) collective-permute-start(bf16[2,128,896]{2,1,0:T(8,128)(2,1)S(1)} %get-tuple-element.24), channel_id=1, source_target_pairs={{0,6},{1,7},{2,0},{3,1},{4,2},{5,3},{6,4},{7,5},{8,14},{9,15},{10,... | collective-permute-start | bytes 1376264 | tf_op jit(solution)/shard_map/ppermute | solution.py:56
  103.4 25.1 %collective-permute-start.13 = (bf16[2,128,896]{2,1,0:T(8,128)(2,1)S(1)}, bf16[2,128,896]{2,1,0:T(8,128)(2,1)S(1)}, u32[]{:S(2)}, u32[]{:S(2)}) collective-permute-start(bf16[2,128,896]{2,1,0:T(8,128)(2,1)S(1)} %get-tuple-element.18), channel_id=1, source_target_pairs={{0,7},{1,0},{2,1},{3,2},{4,3},{5,4},{6,5},{7,6},{8,15},{9,8},{10,9... | collective-permute-start | bytes 1376264 | tf_op jit(solution)/shard_map/ppermute | solution.py:56
  129.3 5.1 %copy-start.1 = (bf16[8,2,768,128]{3,2,0,1:T(8,128)(2,1)S(1)}, bf16[8,2,768,128]{3,2,0,1:T(8,128)(2,1)}, u32[]{:S(2)}) copy-start(bf16[8,2,768,128]{3,2,0,1:T(8,128)(2,1)} %bitcast_dynamic-update-slice_fusion.8) | copy-start | bytes 9437188
  149.5 1.1 copy-start
  182.1 28.9 %all-to-all-start.1 = ((f32[64,12,2]{1,2,0:T(2,128)}), f32[64,12,2]{1,2,0:T(2,128)S(1)}, u32[]{:S(2)}, u32[]{:S(2)}) async-start(f32[64,12,2]{1,2,0:T(2,128)} %copy.80), calls=%async_computation.2 | async-start | bytes 131072 | tf_op jit(solution)/shard_map/all_to_all | solution.py:84
Sparse Core Ops, SparseCore 0:
  161.9 50.4 reduce-scatter.1

commit v9 on v7

--- a/solution.py
+++ b/solution.py
@@ -58,19 +58,15 @@
     stacked = jnp.stack(pieces, axis=0)
     block_order = (local_index - jnp.arange(local_count, dtype=jnp.int32)) % local_count
     weight_blocks = jnp.take(stacked, block_order, axis=0)
+    weight_cols = jnp.transpose(weight_blocks, (1, 0, 2, 3)).reshape(expert_count, -1, width)
     partial_grads = jnp.einsum(
-        "rd,behd->erbh",
+        "rd,ehd->erh",
         rows_in,
-        weight_blocks,
+        weight_cols,
         preferred_element_type=jnp.float32,
-    ).reshape(expert_count, slot_rows, -1)
-    saved_blocks = lax.all_gather(saved_hidden, "local", axis=0, tiled=False)
-    partial_scores = jnp.einsum(
-        "berh,erbh->er",
-        saved_blocks.astype(jnp.float32),
-        partial_grads.reshape(expert_count, slot_rows, local_count, -1),
-        precision=lax.Precision.HIGHEST,
     )
+    saved_full = lax.all_gather(saved_hidden, "local", axis=2, tiled=True)
+    partial_scores = jnp.sum(saved_full.astype(jnp.float32) * partial_grads, axis=2)
     partial_value = jnp.transpose(partial_scores).reshape(node_count, capacity, expert_count)
     summed = jnp.sum(lax.all_gather(partial_value, "local", axis=0, tiled=False), axis=0)
     hidden_grads = lax.psum_scatter(partial_grads, "local", scatter_dimension=2, tiled=True)

time: 201 us -> 196 us (0.975)
  local copies, waits for them, and re-layouts: 51.1 us -> 43.3 us
  starting transfers between devices: 51.7 us -> 56 us
  matrix products: 7.52 us -> 11.1 us
  waiting for transfers between devices: 50.8 us -> 48 us
    ppermute x7, waiting for transfers between devices: 37 us -> 28.8 us  [on_device(): piece = lax.ppermute(piece, 'local', perm=pairs)]
    reduce_scatter x1, waiting for transfers between devices: 0.01 us -> 5.96 us  [on_device(): lax.psum_scatter(partial_grads, 'local', scatter_dimension=2, tiled=True)]
    unnamed x18, local copies, waits for them, and re-layouts: 28.2 us -> 22.7 us
    dot_general x1 -> x0, other arithmetic: 4.41 us -> none  [on_device(): jnp.einsum('berh,erbh->er', saved_blocks.astype(jnp.float32), partial_gra...]
    ppermute x7, starting transfers between devices: 18 us -> 21.9 us  [on_device(): piece = lax.ppermute(piece, 'local', perm=pairs)]
    transpose x1 -> x0, local copies, waits for them, and re-layouts: 3.61 us -> none  [on_device(): jnp.einsum('rd,behd->erbh', rows_in, weight_blocks, preferred_element_typ...]
    dot_general x1, matrix products: 5.56 us -> 9.16 us  [on_device(): jnp.einsum('rd,ehd->erh', rows_in, weight_cols, preferred_element_type=jn...]
    select_n x1 -> x2, other arithmetic: 0.01 us -> 2.48 us  [on_device(): weight_blocks = jnp.take(stacked, block_order, axis=0)]
  transfers between devices with their start and end apart: 11 -> 11, of which waited for: 7 -> 5; matrix products, arithmetic and copies ran while one was open for 25% -> 25% of each run, Pallas kernels for 0% -> 0%
where the time goes in v9:
time: 196 us
  starting transfers between devices  56 us (29%)
  waiting for transfers between devices  48 us (24%)
  local copies, waits for them, and re-layouts  43.3 us (22%)
  between operations  14.5 us (7%)
  blocking collectives  13.5 us (7%)
  matrix products  11.1 us (6%)
  other arithmetic  9.25 us (5%)
    ppermute x7, waiting for transfers between devices, on_device(): piece = lax.ppermute(piece, 'local', perm=pairs)  28.8 us
    unnamed x18, local copies, waits for them, and re-layouts  22.7 us
    ppermute x7, starting transfers between devices, on_device(): piece = lax.ppermute(piece, 'local', perm=pairs)  21.9 us
    all_to_all x1, starting transfers between devices, on_device(): lax.all_to_all(payload, 'node', split_axis=0, concat_axis=0, tiled=True)  19.3 us
    all_to_all x1, starting transfers between devices, on_device(): lax.all_to_all(summed, 'node', split_axis=0, concat_axis=0, tiled=True)  14.8 us
    all_gather x1, blocking collectives, on_device(): lax.all_gather(partial_value, 'local', axis=0, tiled=False)  13.5 us
    all_to_all x1, waiting for transfers between devices, on_device(): lax.all_to_all(summed, 'node', split_axis=0, concat_axis=0, tiled=True)  13.1 us
    dot_general x1, matrix products, on_device(): jnp.einsum('rd,ehd->erh', rows_in, weight_cols, preferred_element_type=jn...  9.16 us
  transfers between devices with their start and end apart: 11, of which 5 were waited for; matrix products, arithmetic and copies ran while one was open for 25% of the time, Pallas kernels for 0%

profile of v9, /device:TPU:1, one launch (start us, length us, event | category | flops | bytes accessed | tf_op | source)
XLA Modules:
  0.0 195.6 jit_solution(2527995417976677778)
XLA Ops:
  7.2 2.0 %copy.96 = bf16[2,768,128]{1,2,0:T(8,128)(2,1)} copy(bf16[2,768,128]{2,1,0:T(8,128)(2,1)} %param.9) | data formatting | bytes 786432 | tf_op args[4]
  9.2 0.8 copy.86
  10.0 0.3 convert_reduce_fusion.1
  10.4 0.2 reduce_window_sum.11
  10.6 2.3 %convert_reduce_fusion = (s32[64,12]{1,0:T(8,128)S(1)}, s32[64,12]{1,0:T(8,128)S(1)}) fusion(s32[128,64]{0,1:T(8,128)S(1)} %copy.87, pred[128,64]{0,1:T(8,128)(4,1)S(1)} %broadcast_compare_fusion), kind=kLoop, calls=%fused_computation.12 | loop fusion | flops 588288 | bytes 47104 | tf_op jit(solution)/shard_map/reduce_sum | solution.py:29
  12.9 0.8 copy.89
  13.7 0.3 fusion.6
  14.1 0.1 copy.90
  14.2 0.6 convolution_convert_fusion
  14.7 0.1 copy.91
  14.8 0.1 copy.92
  14.9 0.1 reshape.139
  15.1 2.8 %gather_fusion = bf16[768,896]{1,0:T(8,128)(2,1)S(1)} fusion(bf16[129,896]{1,0:T(8,128)(2,1)S(1)} %concatenate.6, s32[1024]{0:T(1024)S(1)} %pad_clamp_fusion.1), kind=kCustom, calls=%fused_computation | custom fusion | bytes 2755584 | tf_op jit(solution)/shard_map/jit(_take)/gather | solution.py:10
  17.9 0.3 reshape.138
  18.3 0.3 broadcast_select_fusion
  18.6 0.3 copy.106
  18.9 0.1 maximum_bitcast_fusion
  19.0 0.5 broadcast.182
  19.5 1.6 reduce
  21.1 2.3 %reshape.156 = bf16[64,2,5388]{2,1,0:T(2,128)(2,1)} reshape(bf16[64,10776]{1,0:T(8,128)(2,1)S(1)} %reduce) | data formatting | bytes 2758656
  23.5 19.3 %all-to-all-start = ((bf16[64,2,5388]{2,1,0:T(2,128)(2,1)}), bf16[64,2,5388]{2,1,0:T(2,128)(2,1)}, u32[]{:S(2)}, u32[]{:S(2)}) async-start(bf16[64,2,5388]{2,1,0:T(2,128)(2,1)} %reshape.156), calls=%async_computation | async-start | bytes 2818048 | tf_op jit(solution)/shard_map/all_to_all | solution.py:45
  43.0 3.4 %constant_dynamic-slice_fusion = (bf16[2,128,896]{2,1,0:T(8,128)(2,1)S(1)}, bf16[2,128,896]{2,1,0:T(8,128)(2,1)}, bf16[2,128,896]{2,1,0:T(8,128)(2,1)}, bf16[2,1...) fusion(bf16[2,128,7168]{2,1,0:T(8,128)(2,1)} %param.8, ...), kind=kLoop, calls=%fused_computation.47 | loop fusion | bytes 6422556 | tf_op jit(solution)/shard_map/dynamic_slice | solution.py:53
  46.3 1.0 collective-permute-start.6
  47.3 4.5 %collective-permute-start.4 = (bf16[2,128,896]{2,1,0:T(8,128)(2,1)}, bf16[2,128,896]{2,1,0:T(8,128)(2,1)S(1)}, u32[]{:S(2)}, u32[]{:S(2)}) collective-permute-start(bf16[2,128,896]{2,1,0:T(8,128)(2,1)} %get-tuple-element.19), channel_id=1, source_target_pairs={{0,5},{1,6},{2,7},{3,0},{4,1},{5,2},{6,3},{7,4},{8,13},{9,14},{10,... | collective-permute-start | bytes 1376264 | tf_op jit(solution)/shard_map/ppermute | solution.py:56
  51.8 2.3 %collective-permute-start.3 = (bf16[2,128,896]{2,1,0:T(8,128)(2,1)}, bf16[2,128,896]{2,1,0:T(8,128)(2,1)S(1)}, u32[]{:S(2)}, u32[]{:S(2)}) collective-permute-start(bf16[2,128,896]{2,1,0:T(8,128)(2,1)} %get-tuple-element.20), channel_id=1, source_target_pairs={{0,4},{1,5},{2,6},{3,7},{4,0},{5,1},{6,2},{7,3},{8,12},{9,13},{10,... | collective-permute-start | bytes 1376264 | tf_op jit(solution)/shard_map/ppermute | solution.py:56
  54.1 2.6 %collective-permute-start.1 = (bf16[2,128,896]{2,1,0:T(8,128)(2,1)}, bf16[2,128,896]{2,1,0:T(8,128)(2,1)S(1)}, u32[]{:S(2)}, u32[]{:S(2)}) collective-permute-start(bf16[2,128,896]{2,1,0:T(8,128)(2,1)} %get-tuple-element.22), channel_id=1, source_target_pairs={{0,2},{1,3},{2,4},{3,5},{4,6},{5,7},{6,0},{7,1},{8,10},{9,11},{10,... | collective-permute-start | bytes 1376264 | tf_op jit(solution)/shard_map/ppermute | solution.py:56
  56.7 2.8 %collective-permute-start = (bf16[2,128,896]{2,1,0:T(8,128)(2,1)}, bf16[2,128,896]{2,1,0:T(8,128)(2,1)S(1)}, u32[]{:S(2)}, u32[]{:S(2)}) collective-permute-start(bf16[2,128,896]{2,1,0:T(8,128)(2,1)} %get-tuple-element.23), channel_id=1, source_target_pairs={{0,1},{1,2},{2,3},{3,4},{4,5},{5,6},{6,7},{7,0},{8,9},{9,10},{10,1... | collective-permute-start | bytes 1376264 | tf_op jit(solution)/shard_map/ppermute | solution.py:56
  59.5 1.8 bitcast_dynamic-update-slice_fusion.7
  61.3 21.7 %collective-permute-done = bf16[2,128,896]{2,1,0:T(8,128)(2,1)S(1)} collective-permute-done((bf16[2,128,896]{2,1,0:T(8,128)(2,1)}, bf16[2,128,896]{2,1,0:T(8,128)(2,1)S(1)}, u32[]{:S(2)}, u32[]{:S(2)}) %collective-permute-start) | collective-permute-done | bytes 458784 | tf_op jit(solution)/shard_map/ppermute | solution.py:56
  83.0 5.7 %collective-permute-start.2 = (bf16[2,128,896]{2,1,0:T(8,128)(2,1)}, bf16[2,128,896]{2,1,0:T(8,128)(2,1)S(1)}, u32[]{:S(2)}, u32[]{:S(2)}) collective-permute-start(bf16[2,128,896]{2,1,0:T(8,128)(2,1)} %get-tuple-element.21), channel_id=1, source_target_pairs={{0,3},{1,4},{2,5},{3,6},{4,7},{5,0},{6,1},{7,2},{8,11},{9,12},{10,... | collective-permute-start | bytes 1376264 | tf_op jit(solution)/shard_map/ppermute | solution.py:56
  88.8 0.8 bitcast_dynamic-update-slice_fusion.6
  89.6 3.0 %collective-permute-start.5 = (bf16[2,128,896]{2,1,0:T(8,128)(2,1)S(1)}, bf16[2,128,896]{2,1,0:T(8,128)(2,1)S(1)}, u32[]{:S(2)}, u32[]{:S(2)}) collective-permute-start(bf16[2,128,896]{2,1,0:T(8,128)(2,1)S(1)} %get-tuple-element.24), channel_id=1, source_target_pairs={{0,6},{1,7},{2,0},{3,1},{4,2},{5,3},{6,4},{7,5},{8,14},{9,15},{10,... | collective-permute-start | bytes 1376264 | tf_op jit(solution)/shard_map/ppermute | solution.py:56
  92.6 0.8 bitcast_dynamic-update-slice_fusion.5
  93.4 5.7 %collective-permute-done.2 = bf16[2,128,896]{2,1,0:T(8,128)(2,1)S(1)} collective-permute-done((bf16[2,128,896]{2,1,0:T(8,128)(2,1)}, bf16[2,128,896]{2,1,0:T(8,128)(2,1)S(1)}, u32[]{:S(2)}, u32[]{:S(2)}) %collective-permute-start.2) | collective-permute-done | bytes 458784 | tf_op jit(solution)/shard_map/ppermute | solution.py:56
  99.2 0.8 bitcast_dynamic-update-slice_fusion.4
  100.0 0.8 bitcast_dynamic-update-slice_fusion.3
  100.8 0.8 bitcast_dynamic-update-slice_fusion.2
  101.6 1.4 collective-permute-done.5
  103.0 0.8 bitcast_dynamic-update-slice_fusion.1
  103.9 0.8 bitcast_dynamic-update-slice_fusion
  104.7 4.8 %gather_fusion.1 = bf16[8,2,128,896]{3,2,1,0:T(8,128)(2,1)} fusion(bf16[8,2,128,896]{3,2,1,0:T(8,128)(2,1)} %bitcast_dynamic-update-slice_fusion, s32[1024]{0:T(1024)S(1)} %pad_clamp_fusion), kind=kCustom, calls=%fused_computation.1 | custom fusion | bytes 7340064 | tf_op jit(solution)/shard_map/jit(_take)/gather | solution.py:60
  109.5 2.5 %select_bitcast_fusion = bf16[2,8,128,896]{3,2,0,1:T(8,128)(2,1)S(1)} fusion(bf16[8,2,128,896]{3,2,1,0:T(8,128)(2,1)} %gather_fusion.1, pred[8]{0:T(512)(128)(4,1)S(1)} %compare_and_fusion.1), kind=kLoop, calls=%fused_computation.3 | loop fusion | flops 1835008 | bytes 7340040 | tf_op jit(solution)/shard_map/jit(_take)/select_n | solution.py:60
  112.0 2.2 %copy.95 = bf16[2,8,128,896]{3,2,1,0:T(8,128)(2,1)} copy(bf16[2,8,128,896]{3,2,0,1:T(8,128)(2,1)S(1)} %select_bitcast_fusion) | data formatting | bytes 7340032 | tf_op jit(solution)/shard_map/jit(_take)/select_n | solution.py:60
  114.2 8.4 %reshape.157 = bf16[64,1,10776]{2,1,0:T(2,128)(2,1)S(1)} reshape(bf16[64,2,5388]{2,1,0:T(2,128)(2,1)} %all-to-all-done) | data formatting | bytes 2758656
  122.6 0.2 copy.108
  122.8 1.1 copy-done
  123.9 0.1 slice.13
  124.0 2.2 %reshape.154 = bf16[768,896,1]{1,0,2:T(8,128)(2,1)S(1)} reshape(bf16[64,10752]{1,0:T(8,128)(2,1)S(1)} %slice.13) | data formatting | bytes 2752512 | tf_op jit(solution)/shard_map/reshape | solution.py:46
  126.2 9.2 %multiply_reduce_fusion = (f32[2,768]{1,0:T(2,128)S(1)}, f32[2,768,1024]{1,2,0:T(8,128)}) fusion(bf16[2,768,1024]{1,2,0:T(8,128)(2,1)} %all-gather.2.cloned.1.call-done, bf16[2,1024,896]{2,1,0:T(8,128)(2,1)} %bitcast.53, bf16[768,896,1]{1,0,2:T(8,128)(2,1)S(1)} %reshape.154), kind=kOutput, calls=%fused_computation.2 | convolution fusion | flops 2823289344 | bytes 14489600 | tf_op jit(solution)/shard_map/rd,ehd->erh/dot_general | solution.py:62
  135.4 0.1 all_gather_reshape.3
  135.6 13.5 %all_gather.7 = f32[8,64,12,2]{1,3,2,0:T(2,128)S(1)} all-gather(f32[1,64,12,2]{1,3,2,0:T(2,128)S(1)} %copy.97), channel_id=1, replica_groups=mesh['node'=64,'local'=8] {'local'}, dimensions={0}, use_global_device_ids=true | all-gather | bytes 55296 | tf_op jit(solution)/shard_map/all_gather | solution.py:71
  149.2 0.7 copy.99
  149.9 14.8 %all-to-all-start.1 = ((f32[64,12,2]{1,2,0:T(2,128)}), f32[64,12,2]{1,2,0:T(2,128)S(1)}, u32[]{:S(2)}, u32[]{:S(2)}) async-start(f32[64,12,2]{1,2,0:T(2,128)} %copy.99), calls=%async_computation.2 | async-start | bytes 131072 | tf_op jit(solution)/shard_map/all_to_all | solution.py:75
  164.7 0.7 slice_convert_fusion
  165.4 0.2 reshape.136
  165.6 0.1 copy.94
  165.7 13.1 %all-to-all-done.1 = f32[64,12,2]{1,2,0:T(2,128)S(1)} async-done(((f32[64,12,2]{1,2,0:T(2,128)}), f32[64,12,2]{1,2,0:T(2,128)S(1)}, u32[]{:S(2)}, u32[]{:S(2)}) %all-to-all-start.1) | async-done | bytes 6176 | tf_op jit(solution)/shard_map/all_to_all | solution.py:75
  178.8 0.4 convolution_bitcast_fusion.1
  179.3 0.1 copy.100
  179.4 0.6 fusion.5
  180.0 0.7 copy.101
  180.7 6.0 %reduce-scatter.2.cloned.1.call-done = f32[2,768,128]{1,2,0:T(8,128)} async-done(((f32[2,768,1024]{1,2,0:T(8,128)}), f32[2,768,128]{1,2,0:T(8,128)}) %reduce-scatter.2.cloned.1.call-update) | async-done | bytes 786448 | tf_op jit(solution)/shard_map/reduce_scatter | solution.py:72
  186.7 1.2 multiply_convert_fusion
  187.9 0.9 copy.102
  (26 shorter events, 0.5 us)
Async XLA Ops:
  7.2 7.9 %copy-start.1 = (bf16[128,896]{1,0:T(8,128)(2,1)S(1)}, bf16[128,896]{1,0:T(8,128)(2,1)}, u32[]{:S(2)}) copy-start(bf16[128,896]{1,0:T(8,128)(2,1)} %param.5) | copy-start | bytes 688132
  7.2 119.0 %all-gather.2.cloned.1.call-start = ((), (), s32[]{:S(2)}) async-start(), calls=%async_computation.4 | async-start | bytes 3538944 | tf_op jit(solution)/shard_map/all_gather | solution.py:68
  23.5 90.8 %all-to-all-start = ((bf16[64,2,5388]{2,1,0:T(2,128)(2,1)}), bf16[64,2,5388]{2,1,0:T(2,128)(2,1)}, u32[]{:S(2)}, u32[]{:S(2)}) async-start(bf16[64,2,5388]{2,1,0:T(2,128)(2,1)} %reshape.156), calls=%async_computation | async-start | bytes 2818048 | tf_op jit(solution)/shard_map/all_to_all | solution.py:45
  42.8 143.9 %reduce-scatter.2.cloned.1.call-start = ((), (), s32[]{:S(2)}) async-start(), calls=%async_computation.3 | async-start | bytes 7077888 | tf_op jit(solution)/shard_map/reduce_scatter | solution.py:72
  46.3 57.6 %collective-permute-start.6 = (bf16[2,128,896]{2,1,0:T(8,128)(2,1)S(1)}, bf16[2,128,896]{2,1,0:T(8,128)(2,1)S(1)}, u32[]{:S(2)}, u32[]{:S(2)}) collective-permute-start(bf16[2,128,896]{2,1,0:T(8,128)(2,1)S(1)} %get-tuple-element.18), channel_id=1, source_target_pairs={{0,7},{1,0},{2,1},{3,2},{4,3},{5,4},{6,5},{7,6},{8,15},{9,8},{10,9... | collective-permute-start | bytes 1376264 | tf_op jit(solution)/shard_map/ppermute | solution.py:56
  47.3 53.5 %collective-permute-start.4 = (bf16[2,128,896]{2,1,0:T(8,128)(2,1)}, bf16[2,128,896]{2,1,0:T(8,128)(2,1)S(1)}, u32[]{:S(2)}, u32[]{:S(2)}) collective-permute-start(bf16[2,128,896]{2,1,0:T(8,128)(2,1)} %get-tuple-element.19), channel_id=1, source_target_pairs={{0,5},{1,6},{2,7},{3,0},{4,1},{5,2},{6,3},{7,4},{8,13},{9,14},{10,... | collective-permute-start | bytes 1376264 | tf_op jit(solution)/shard_map/ppermute | solution.py:56
  51.8 48.2 %collective-permute-start.3 = (bf16[2,128,896]{2,1,0:T(8,128)(2,1)}, bf16[2,128,896]{2,1,0:T(8,128)(2,1)S(1)}, u32[]{:S(2)}, u32[]{:S(2)}) collective-permute-start(bf16[2,128,896]{2,1,0:T(8,128)(2,1)} %get-tuple-element.20), channel_id=1, source_target_pairs={{0,4},{1,5},{2,6},{3,7},{4,0},{5,1},{6,2},{7,3},{8,12},{9,13},{10,... | collective-permute-start | bytes 1376264 | tf_op jit(solution)/shard_map/ppermute | solution.py:56
  54.1 35.5 %collective-permute-start.1 = (bf16[2,128,896]{2,1,0:T(8,128)(2,1)}, bf16[2,128,896]{2,1,0:T(8,128)(2,1)S(1)}, u32[]{:S(2)}, u32[]{:S(2)}) collective-permute-start(bf16[2,128,896]{2,1,0:T(8,128)(2,1)} %get-tuple-element.22), channel_id=1, source_target_pairs={{0,2},{1,3},{2,4},{3,5},{4,6},{5,7},{6,0},{7,1},{8,10},{9,11},{10,... | collective-permute-start | bytes 1376264 | tf_op jit(solution)/shard_map/ppermute | solution.py:56
  56.7 26.3 %collective-permute-start = (bf16[2,128,896]{2,1,0:T(8,128)(2,1)}, bf16[2,128,896]{2,1,0:T(8,128)(2,1)S(1)}, u32[]{:S(2)}, u32[]{:S(2)}) collective-permute-start(bf16[2,128,896]{2,1,0:T(8,128)(2,1)} %get-tuple-element.23), channel_id=1, source_target_pairs={{0,1},{1,2},{2,3},{3,4},{4,5},{5,6},{6,7},{7,0},{8,9},{9,10},{10,1... | collective-permute-start | bytes 1376264 | tf_op jit(solution)/shard_map/ppermute | solution.py:56
  83.0 16.1 %collective-permute-start.2 = (bf16[2,128,896]{2,1,0:T(8,128)(2,1)}, bf16[2,128,896]{2,1,0:T(8,128)(2,1)S(1)}, u32[]{:S(2)}, u32[]{:S(2)}) collective-permute-start(bf16[2,128,896]{2,1,0:T(8,128)(2,1)} %get-tuple-element.21), channel_id=1, source_target_pairs={{0,3},{1,4},{2,5},{3,6},{4,7},{5,0},{6,1},{7,2},{8,11},{9,12},{10,... | collective-permute-start | bytes 1376264 | tf_op jit(solution)/shard_map/ppermute | solution.py:56
  89.6 13.4 %collective-permute-start.5 = (bf16[2,128,896]{2,1,0:T(8,128)(2,1)S(1)}, bf16[2,128,896]{2,1,0:T(8,128)(2,1)S(1)}, u32[]{:S(2)}, u32[]{:S(2)}) collective-permute-start(bf16[2,128,896]{2,1,0:T(8,128)(2,1)S(1)} %get-tuple-element.24), channel_id=1, source_target_pairs={{0,6},{1,7},{2,0},{3,1},{4,2},{5,3},{6,4},{7,5},{8,14},{9,15},{10,... | collective-permute-start | bytes 1376264 | tf_op jit(solution)/shard_map/ppermute | solution.py:56
  122.8 1.1 copy-start
  149.9 28.9 %all-to-all-start.1 = ((f32[64,12,2]{1,2,0:T(2,128)}), f32[64,12,2]{1,2,0:T(2,128)S(1)}, u32[]{:S(2)}, u32[]{:S(2)}) async-start(f32[64,12,2]{1,2,0:T(2,128)} %copy.99), calls=%async_computation.2 | async-start | bytes 131072 | tf_op jit(solution)/shard_map/all_to_all | solution.py:75
Sparse Core Ops, SparseCore 0:
  10.7 41.1 all-gather.1
  135.5 51.1 reduce-scatter.1

commit v10 on v9

--- a/solution.py
+++ b/solution.py
@@ -33,7 +33,12 @@
     prob_send = jnp.einsum(
         "tms,tmc->msc", select_full, picked, precision=lax.Precision.HIGHEST
     ).astype(jnp.bfloat16)
-    rows_send = gather_slots(grad_out, source_row, slot_valid)
+    rows_send = jnp.einsum(
+        "tms,td->msd",
+        select_mask.astype(grad_out.dtype),
+        grad_out,
+        preferred_element_type=jnp.float32,
+    ).astype(grad_out.dtype)
     width = grad_out.shape[1]
     payload = jnp.concatenate(
         [

time: 196 us -> 192 us (0.980)
  local copies, waits for them, and re-layouts: 43.3 us -> 39.8 us
  other arithmetic: 9.25 us -> 6.79 us
    gather x2 -> x0, local copies, waits for them, and re-layouts: 3.16 us -> none  [gather_slots(): return jnp.take(padded, index, axis=0)]
    reduce_sum x1 -> x0, other arithmetic: 2.25 us -> none  [on_device(): slot_valid = jnp.sum(select_count, axis=0) > 0]
    unnamed x18 -> x17, local copies, waits for them, and re-layouts: 22.7 us -> 22.4 us
  transfers between devices with their start and end apart: 11 -> 11, of which waited for: 5 -> 5; matrix products, arithmetic and copies ran while one was open for 25% -> 23% of each run, Pallas kernels for 0% -> 0%
where the time goes in v10:
time: 192 us; the launch traced here: 191 us
  starting transfers between devices  56.3 us (29%)
  waiting for transfers between devices  49.3 us (26%)
  local copies, waits for them, and re-layouts  39.8 us (21%)
  between operations  14.4 us (8%)
  blocking collectives  12.5 us (7%)
  matrix products  11.6 us (6%)
  other arithmetic  6.79 us (4%)
    ppermute x7, waiting for transfers between devices, on_device(): piece = lax.ppermute(piece, 'local', perm=pairs)  30.5 us
    unnamed x17, local copies, waits for them, and re-layouts  22.4 us
    ppermute x7, starting transfers between devices, on_device(): piece = lax.ppermute(piece, 'local', perm=pairs)  21.9 us
    all_to_all x1, starting transfers between devices, on_device(): lax.all_to_all(payload, 'node', split_axis=0, concat_axis=0, tiled=True)  19.3 us
    all_to_all x1, starting transfers between devices, on_device(): lax.all_to_all(summed, 'node', split_axis=0, concat_axis=0, tiled=True)  15 us
    all_to_all x1, waiting for transfers between devices, on_device(): lax.all_to_all(summed, 'node', split_axis=0, concat_axis=0, tiled=True)  13.1 us
    all_gather x1, blocking collectives, on_device(): lax.all_gather(partial_value, 'local', axis=0, tiled=False)  12.5 us
    dot_general x1, matrix products, on_device(): jnp.einsum('rd,ehd->erh', rows_in, weight_cols, preferred_element_type=jn...  9.13 us
  transfers between devices with their start and end apart: 11, of which 5 were waited for; matrix products, arithmetic and copies ran while one was open for 23% of the time, Pallas kernels for 0%

profile of v10, /device:TPU:1, one launch (start us, length us, event | category | flops | bytes accessed | tf_op | source)
XLA Modules:
  0.0 190.7 jit_solution(6376451649860610809)
XLA Ops:
  7.2 2.0 %copy.109 = bf16[2,768,128]{1,2,0:T(8,128)(2,1)} copy(bf16[2,768,128]{2,1,0:T(8,128)(2,1)} %param.9) | data formatting | bytes 786432 | tf_op args[4]
  9.2 0.8 copy.97
  10.0 0.3 convert_reduce_fusion
  10.3 0.1 copy.99
  10.4 0.2 reduce_window_sum.11
  10.6 0.1 copy.98
  10.6 0.8 copy.102
  11.5 0.3 fusion.4
  11.8 0.1 copy.103
  11.9 0.1 fusion.1
  12.0 0.5 convolution_convert_fusion.1
  12.6 0.1 copy.104
  12.7 0.1 copy.105
  12.8 0.5 fusion
  13.3 0.1 copy.119
  13.4 0.1 maximum_bitcast_fusion
  13.5 0.5 broadcast.121
  14.1 1.6 reduce
  15.7 2.3 %reshape.114 = bf16[64,2,5388]{2,1,0:T(2,128)(2,1)} reshape(bf16[64,10776]{1,0:T(8,128)(2,1)S(1)} %reduce) | data formatting | bytes 2758656
  18.1 19.3 %all-to-all-start = ((bf16[64,2,5388]{2,1,0:T(2,128)(2,1)}), bf16[64,2,5388]{2,1,0:T(2,128)(2,1)}, u32[]{:S(2)}, u32[]{:S(2)}) async-start(bf16[64,2,5388]{2,1,0:T(2,128)(2,1)} %reshape.114), calls=%async_computation | async-start | bytes 2818048 | tf_op jit(solution)/shard_map/all_to_all | solution.py:50
  37.6 3.3 %constant_dynamic-slice_fusion = (bf16[2,128,896]{2,1,0:T(8,128)(2,1)S(1)}, bf16[2,128,896]{2,1,0:T(8,128)(2,1)}, bf16[2,128,896]{2,1,0:T(8,128)(2,1)}, bf16[2,1...) fusion(bf16[2,128,7168]{2,1,0:T(8,128)(2,1)} %param.8, ...), kind=kLoop, calls=%fused_computation.38 | loop fusion | bytes 6422556 | tf_op jit(solution)/shard_map/dynamic_slice | solution.py:58
  40.9 1.0 collective-permute-start.6
  41.9 4.6 %collective-permute-start.4 = (bf16[2,128,896]{2,1,0:T(8,128)(2,1)}, bf16[2,128,896]{2,1,0:T(8,128)(2,1)S(1)}, u32[]{:S(2)}, u32[]{:S(2)}) collective-permute-start(bf16[2,128,896]{2,1,0:T(8,128)(2,1)} %get-tuple-element.17), channel_id=1, source_target_pairs={{0,5},{1,6},{2,7},{3,0},{4,1},{5,2},{6,3},{7,4},{8,13},{9,14},{10,... | collective-permute-start | bytes 1376264 | tf_op jit(solution)/shard_map/ppermute | solution.py:61
  46.5 2.3 %collective-permute-start.3 = (bf16[2,128,896]{2,1,0:T(8,128)(2,1)}, bf16[2,128,896]{2,1,0:T(8,128)(2,1)S(1)}, u32[]{:S(2)}, u32[]{:S(2)}) collective-permute-start(bf16[2,128,896]{2,1,0:T(8,128)(2,1)} %get-tuple-element.18), channel_id=1, source_target_pairs={{0,4},{1,5},{2,6},{3,7},{4,0},{5,1},{6,2},{7,3},{8,12},{9,13},{10,... | collective-permute-start | bytes 1376264 | tf_op jit(solution)/shard_map/ppermute | solution.py:61
  48.7 2.6 %collective-permute-start.1 = (bf16[2,128,896]{2,1,0:T(8,128)(2,1)}, bf16[2,128,896]{2,1,0:T(8,128)(2,1)S(1)}, u32[]{:S(2)}, u32[]{:S(2)}) collective-permute-start(bf16[2,128,896]{2,1,0:T(8,128)(2,1)} %get-tuple-element.20), channel_id=1, source_target_pairs={{0,2},{1,3},{2,4},{3,5},{4,6},{5,7},{6,0},{7,1},{8,10},{9,11},{10,... | collective-permute-start | bytes 1376264 | tf_op jit(solution)/shard_map/ppermute | solution.py:61
  51.3 2.8 %collective-permute-start = (bf16[2,128,896]{2,1,0:T(8,128)(2,1)}, bf16[2,128,896]{2,1,0:T(8,128)(2,1)S(1)}, u32[]{:S(2)}, u32[]{:S(2)}) collective-permute-start(bf16[2,128,896]{2,1,0:T(8,128)(2,1)} %get-tuple-element.21), channel_id=1, source_target_pairs={{0,1},{1,2},{2,3},{3,4},{4,5},{5,6},{6,7},{7,0},{8,9},{9,10},{10,1... | collective-permute-start | bytes 1376264 | tf_op jit(solution)/shard_map/ppermute | solution.py:61
  54.1 1.8 bitcast_dynamic-update-slice_fusion.7
  55.9 21.8 %collective-permute-done = bf16[2,128,896]{2,1,0:T(8,128)(2,1)S(1)} collective-permute-done((bf16[2,128,896]{2,1,0:T(8,128)(2,1)}, bf16[2,128,896]{2,1,0:T(8,128)(2,1)S(1)}, u32[]{:S(2)}, u32[]{:S(2)}) %collective-permute-start) | collective-permute-done | bytes 458784 | tf_op jit(solution)/shard_map/ppermute | solution.py:61
  77.8 5.7 %collective-permute-start.2 = (bf16[2,128,896]{2,1,0:T(8,128)(2,1)}, bf16[2,128,896]{2,1,0:T(8,128)(2,1)S(1)}, u32[]{:S(2)}, u32[]{:S(2)}) collective-permute-start(bf16[2,128,896]{2,1,0:T(8,128)(2,1)} %get-tuple-element.19), channel_id=1, source_target_pairs={{0,3},{1,4},{2,5},{3,6},{4,7},{5,0},{6,1},{7,2},{8,11},{9,12},{10,... | collective-permute-start | bytes 1376264 | tf_op jit(solution)/shard_map/ppermute | solution.py:61
  83.5 0.8 bitcast_dynamic-update-slice_fusion.6
  84.3 3.0 %collective-permute-start.5 = (bf16[2,128,896]{2,1,0:T(8,128)(2,1)S(1)}, bf16[2,128,896]{2,1,0:T(8,128)(2,1)S(1)}, u32[]{:S(2)}, u32[]{:S(2)}) collective-permute-start(bf16[2,128,896]{2,1,0:T(8,128)(2,1)S(1)} %get-tuple-element.22), channel_id=1, source_target_pairs={{0,6},{1,7},{2,0},{3,1},{4,2},{5,3},{6,4},{7,5},{8,14},{9,15},{10,... | collective-permute-start | bytes 1376264 | tf_op jit(solution)/shard_map/ppermute | solution.py:61
  87.3 0.8 bitcast_dynamic-update-slice_fusion.5
  88.1 4.9 %collective-permute-done.2 = bf16[2,128,896]{2,1,0:T(8,128)(2,1)S(1)} collective-permute-done((bf16[2,128,896]{2,1,0:T(8,128)(2,1)}, bf16[2,128,896]{2,1,0:T(8,128)(2,1)S(1)}, u32[]{:S(2)}, u32[]{:S(2)}) %collective-permute-start.2) | collective-permute-done | bytes 458784 | tf_op jit(solution)/shard_map/ppermute | solution.py:61
  93.1 0.8 bitcast_dynamic-update-slice_fusion.4
  93.9 0.8 bitcast_dynamic-update-slice_fusion.3
  94.7 0.8 bitcast_dynamic-update-slice_fusion.2
  95.5 3.7 %collective-permute-done.5 = bf16[2,128,896]{2,1,0:T(8,128)(2,1)S(1)} collective-permute-done((bf16[2,128,896]{2,1,0:T(8,128)(2,1)S(1)}, bf16[2,128,896]{2,1,0:T(8,128)(2,1)S(1)}, u32[]{:S(2)}, u32[]{:S(2)}) %collective-permute-start.5) | collective-permute-done | bytes 458784 | tf_op jit(solution)/shard_map/ppermute | solution.py:61
  99.3 0.8 bitcast_dynamic-update-slice_fusion.1
  100.1 0.8 bitcast_dynamic-update-slice_fusion
  100.9 4.8 %gather_fusion = bf16[8,2,128,896]{3,2,1,0:T(8,128)(2,1)} fusion(bf16[8,2,128,896]{3,2,1,0:T(8,128)(2,1)} %bitcast_dynamic-update-slice_fusion, s32[1024]{0:T(1024)S(1)} %pad_clamp_fusion), kind=kCustom, calls=%fused_computation | custom fusion | bytes 7340064 | tf_op jit(solution)/shard_map/jit(_take)/gather | solution.py:65
  105.7 2.5 %select_bitcast_fusion = bf16[2,8,128,896]{3,2,0,1:T(8,128)(2,1)S(1)} fusion(bf16[8,2,128,896]{3,2,1,0:T(8,128)(2,1)} %gather_fusion, pred[8]{0:T(512)(128)(4,1)S(1)} %compare_and_fusion), kind=kLoop, calls=%fused_computation.2 | loop fusion | flops 1835008 | bytes 7340040 | tf_op jit(solution)/shard_map/jit(_take)/select_n | solution.py:65
  108.2 2.2 %copy.108 = bf16[2,8,128,896]{3,2,1,0:T(8,128)(2,1)} copy(bf16[2,8,128,896]{3,2,0,1:T(8,128)(2,1)S(1)} %select_bitcast_fusion) | data formatting | bytes 7340032 | tf_op jit(solution)/shard_map/jit(_take)/select_n | solution.py:65
  110.5 8.4 %reshape.115 = bf16[64,1,10776]{2,1,0:T(2,128)(2,1)S(1)} reshape(bf16[64,2,5388]{2,1,0:T(2,128)(2,1)} %all-to-all-done) | data formatting | bytes 2758656
  118.9 0.2 copy.123
  119.0 1.1 copy-done.1
  120.1 0.1 slice.11
  120.2 2.2 %reshape.112 = bf16[768,896,1]{1,0,2:T(8,128)(2,1)S(1)} reshape(bf16[64,10752]{1,0:T(8,128)(2,1)S(1)} %slice.11) | data formatting | bytes 2752512 | tf_op jit(solution)/shard_map/reshape | solution.py:51
  122.4 9.1 %multiply_reduce_fusion = (f32[2,768]{1,0:T(2,128)S(1)}, f32[2,768,1024]{1,2,0:T(8,128)}) fusion(bf16[2,768,1024]{1,2,0:T(8,128)(2,1)} %all-gather.2.cloned.1.call-done, bf16[2,1024,896]{2,1,0:T(8,128)(2,1)} %bitcast.52, bf16[768,896,1]{1,0,2:T(8,128)(2,1)S(1)} %reshape.112), kind=kOutput, calls=%fused_computation.1 | convolution fusion | flops 2823289344 | bytes 14489600 | tf_op jit(solution)/shard_map/rd,ehd->erh/dot_general | solution.py:67
  131.6 0.1 all_gather_reshape.3
  131.7 0.1 copy.110
  131.8 12.5 %all_gather.7 = f32[8,64,12,2]{1,3,2,0:T(2,128)S(1)} all-gather(f32[1,64,12,2]{1,3,2,0:T(2,128)S(1)} %copy.110), channel_id=1, replica_groups=mesh['node'=64,'local'=8] {'local'}, dimensions={0}, use_global_device_ids=true | all-gather | bytes 55296 | tf_op jit(solution)/shard_map/all_gather | solution.py:76
  144.3 0.7 copy.112
  145.1 15.0 %all-to-all-start.1 = ((f32[64,12,2]{1,2,0:T(2,128)}), f32[64,12,2]{1,2,0:T(2,128)S(1)}, u32[]{:S(2)}, u32[]{:S(2)}) async-start(f32[64,12,2]{1,2,0:T(2,128)} %copy.112), calls=%async_computation.2 | async-start | bytes 131072 | tf_op jit(solution)/shard_map/all_to_all | solution.py:80
  160.1 0.7 slice_convert_fusion
  160.8 0.2 reshape.102
  161.0 0.1 copy.107
  161.1 13.1 %all-to-all-done.1 = f32[64,12,2]{1,2,0:T(2,128)S(1)} async-done(((f32[64,12,2]{1,2,0:T(2,128)}), f32[64,12,2]{1,2,0:T(2,128)S(1)}, u32[]{:S(2)}, u32[]{:S(2)}) %all-to-all-start.1) | async-done | bytes 6176 | tf_op jit(solution)/shard_map/all_to_all | solution.py:80
  174.2 0.4 convolution_bitcast_fusion.1
  174.7 0.1 copy.113
  174.8 0.6 fusion.3
  175.4 0.7 copy.114
  176.1 5.6 %reduce-scatter.2.cloned.1.call-done = f32[2,768,128]{1,2,0:T(8,128)} async-done(((f32[2,768,1024]{1,2,0:T(8,128)}), f32[2,768,128]{1,2,0:T(8,128)}) %reduce-scatter.2.cloned.1.call-update) | async-done | bytes 786448 | tf_op jit(solution)/shard_map/reduce_scatter | solution.py:77
  181.7 1.2 multiply_convert_fusion
  182.9 0.9 copy.115
  (19 shorter events, 0.3 us)
Async XLA Ops:
  7.2 5.6 %copy-start = (bf16[128,896]{1,0:T(8,128)(2,1)S(1)}, bf16[128,896]{1,0:T(8,128)(2,1)}, u32[]{:S(2)}) copy-start(bf16[128,896]{1,0:T(8,128)(2,1)} %param.5) | copy-start | bytes 688132
  7.2 115.2 %all-gather.2.cloned.1.call-start = ((), (), s32[]{:S(2)}) async-start(), calls=%async_computation.4 | async-start | bytes 3538944 | tf_op jit(solution)/shard_map/all_gather | solution.py:73
  18.1 92.4 %all-to-all-start = ((bf16[64,2,5388]{2,1,0:T(2,128)(2,1)}), bf16[64,2,5388]{2,1,0:T(2,128)(2,1)}, u32[]{:S(2)}, u32[]{:S(2)}) async-start(bf16[64,2,5388]{2,1,0:T(2,128)(2,1)} %reshape.114), calls=%async_computation | async-start | bytes 2818048 | tf_op jit(solution)/shard_map/all_to_all | solution.py:50
  37.4 144.3 %reduce-scatter.2.cloned.1.call-start = ((), (), s32[]{:S(2)}) async-start(), calls=%async_computation.3 | async-start | bytes 7077888 | tf_op jit(solution)/shard_map/reduce_scatter | solution.py:77
  40.9 59.2 %collective-permute-start.6 = (bf16[2,128,896]{2,1,0:T(8,128)(2,1)S(1)}, bf16[2,128,896]{2,1,0:T(8,128)(2,1)S(1)}, u32[]{:S(2)}, u32[]{:S(2)}) collective-permute-start(bf16[2,128,896]{2,1,0:T(8,128)(2,1)S(1)} %get-tuple-element.16), channel_id=1, source_target_pairs={{0,7},{1,0},{2,1},{3,2},{4,3},{5,4},{6,5},{7,6},{8,15},{9,8},{10,9... | collective-permute-start | bytes 1376264 | tf_op jit(solution)/shard_map/ppermute | solution.py:61
  41.9 52.9 %collective-permute-start.4 = (bf16[2,128,896]{2,1,0:T(8,128)(2,1)}, bf16[2,128,896]{2,1,0:T(8,128)(2,1)S(1)}, u32[]{:S(2)}, u32[]{:S(2)}) collective-permute-start(bf16[2,128,896]{2,1,0:T(8,128)(2,1)} %get-tuple-element.17), channel_id=1, source_target_pairs={{0,5},{1,6},{2,7},{3,0},{4,1},{5,2},{6,3},{7,4},{8,13},{9,14},{10,... | collective-permute-start | bytes 1376264 | tf_op jit(solution)/shard_map/ppermute | solution.py:61
  46.5 47.4 %collective-permute-start.3 = (bf16[2,128,896]{2,1,0:T(8,128)(2,1)}, bf16[2,128,896]{2,1,0:T(8,128)(2,1)S(1)}, u32[]{:S(2)}, u32[]{:S(2)}) collective-permute-start(bf16[2,128,896]{2,1,0:T(8,128)(2,1)} %get-tuple-element.18), channel_id=1, source_target_pairs={{0,4},{1,5},{2,6},{3,7},{4,0},{5,1},{6,2},{7,3},{8,12},{9,13},{10,... | collective-permute-start | bytes 1376264 | tf_op jit(solution)/shard_map/ppermute | solution.py:61
  48.7 35.6 %collective-permute-start.1 = (bf16[2,128,896]{2,1,0:T(8,128)(2,1)}, bf16[2,128,896]{2,1,0:T(8,128)(2,1)S(1)}, u32[]{:S(2)}, u32[]{:S(2)}) collective-permute-start(bf16[2,128,896]{2,1,0:T(8,128)(2,1)} %get-tuple-element.20), channel_id=1, source_target_pairs={{0,2},{1,3},{2,4},{3,5},{4,6},{5,7},{6,0},{7,1},{8,10},{9,11},{10,... | collective-permute-start | bytes 1376264 | tf_op jit(solution)/shard_map/ppermute | solution.py:61
  51.3 26.4 %collective-permute-start = (bf16[2,128,896]{2,1,0:T(8,128)(2,1)}, bf16[2,128,896]{2,1,0:T(8,128)(2,1)S(1)}, u32[]{:S(2)}, u32[]{:S(2)}) collective-permute-start(bf16[2,128,896]{2,1,0:T(8,128)(2,1)} %get-tuple-element.21), channel_id=1, source_target_pairs={{0,1},{1,2},{2,3},{3,4},{4,5},{5,6},{6,7},{7,0},{8,9},{9,10},{10,1... | collective-permute-start | bytes 1376264 | tf_op jit(solution)/shard_map/ppermute | solution.py:61
  77.8 15.3 %collective-permute-start.2 = (bf16[2,128,896]{2,1,0:T(8,128)(2,1)}, bf16[2,128,896]{2,1,0:T(8,128)(2,1)S(1)}, u32[]{:S(2)}, u32[]{:S(2)}) collective-permute-start(bf16[2,128,896]{2,1,0:T(8,128)(2,1)} %get-tuple-element.19), channel_id=1, source_target_pairs={{0,3},{1,4},{2,5},{3,6},{4,7},{5,0},{6,1},{7,2},{8,11},{9,12},{10,... | collective-permute-start | bytes 1376264 | tf_op jit(solution)/shard_map/ppermute | solution.py:61
  84.3 14.9 %collective-permute-start.5 = (bf16[2,128,896]{2,1,0:T(8,128)(2,1)S(1)}, bf16[2,128,896]{2,1,0:T(8,128)(2,1)S(1)}, u32[]{:S(2)}, u32[]{:S(2)}) collective-permute-start(bf16[2,128,896]{2,1,0:T(8,128)(2,1)S(1)} %get-tuple-element.22), channel_id=1, source_target_pairs={{0,6},{1,7},{2,0},{3,1},{4,2},{5,3},{6,4},{7,5},{8,14},{9,15},{10,... | collective-permute-start | bytes 1376264 | tf_op jit(solution)/shard_map/ppermute | solution.py:61
  119.0 1.1 copy-start.1
  145.1 29.1 %all-to-all-start.1 = ((f32[64,12,2]{1,2,0:T(2,128)}), f32[64,12,2]{1,2,0:T(2,128)S(1)}, u32[]{:S(2)}, u32[]{:S(2)}) async-start(f32[64,12,2]{1,2,0:T(2,128)} %copy.112), calls=%async_computation.2 | async-start | bytes 131072 | tf_op jit(solution)/shard_map/all_to_all | solution.py:80
Sparse Core Ops, SparseCore 0:
  10.7 43.7 all-gather.1
  131.7 49.9 reduce-scatter.1

commit v11 on v10

--- a/solution.py
+++ b/solution.py
@@ -64,17 +64,24 @@
     block_order = (local_index - jnp.arange(local_count, dtype=jnp.int32)) % local_count
     weight_blocks = jnp.take(stacked, block_order, axis=0)
     weight_cols = jnp.transpose(weight_blocks, (1, 0, 2, 3)).reshape(expert_count, -1, width)
-    partial_grads = jnp.einsum(
-        "rd,ehd->erh",
-        rows_in,
-        weight_cols,
-        preferred_element_type=jnp.float32,
-    )
     saved_full = lax.all_gather(saved_hidden, "local", axis=2, tiled=True)
-    partial_scores = jnp.sum(saved_full.astype(jnp.float32) * partial_grads, axis=2)
+    score_list = []
+    hidden_list = []
+    for expert in range(expert_count):
+        expert_grads = jnp.einsum(
+            "rd,hd->rh",
+            rows_in,
+            weight_cols[expert],
+            preferred_element_type=jnp.float32,
+        )
+        score_list.append(jnp.sum(saved_full[expert].astype(jnp.float32) * expert_grads, axis=1))
+        hidden_list.append(
+            lax.psum_scatter(expert_grads, "local", scatter_dimension=1, tiled=True)
+        )
+    partial_scores = jnp.stack(score_list, axis=0)
     partial_value = jnp.transpose(partial_scores).reshape(node_count, capacity, expert_count)
     summed = jnp.sum(lax.all_gather(partial_value, "local", axis=0, tiled=False), axis=0)
-    hidden_grads = lax.psum_scatter(partial_grads, "local", scatter_dimension=2, tiled=True)
+    hidden_grads = jnp.stack(hidden_list, axis=0)
     scales = jnp.transpose(prob_in.reshape(slot_rows, expert_count).astype(jnp.float32))
     grad_hidden = (scales[:, :, None] * hidden_grads).astype(jnp.bfloat16)
     returned = lax.all_to_all(summed, "node", split_axis=0, concat_axis=0, tiled=True)

time: 192 us -> 227 us (1.18)
  waiting for transfers between devices: 49.3 us -> 85.5 us
  starting transfers between devices: 56.3 us -> 51.7 us
    reduce_scatter x1 -> x2, waiting for transfers between devices: 5.62 us -> 34.5 us  [on_device(): lax.psum_scatter(expert_grads, 'local', scatter_dimension=1, tiled=True)]
    ppermute x7, waiting for transfers between devices: 30.5 us -> 37.2 us  [on_device(): piece = lax.ppermute(piece, 'local', perm=pairs)]
    ppermute x7, starting transfers between devices: 21.9 us -> 17.8 us  [on_device(): piece = lax.ppermute(piece, 'local', perm=pairs)]
    dot_general x1 -> x2, matrix products: 9.13 us -> 11.1 us  [on_device(): jnp.einsum('rd,hd->rh', rows_in, weight_cols[expert], preferred_element_t...]
    unnamed x17 -> x19, local copies, waits for them, and re-layouts: 22.4 us -> 21.2 us
  transfers between devices with their start and end apart: 11 -> 12, of which waited for: 5 -> 8; matrix products, arithmetic and copies ran while one was open for 23% -> 21% of each run, Pallas kernels for 0% -> 0%
where the time goes in v11:
time: 227 us; the launch traced here: 225 us
  waiting for transfers between devices  85.5 us (38%)
  starting transfers between devices  51.7 us (23%)
  local copies, waits for them, and re-layouts  39.4 us (17%)
  between operations  14.2 us (6%)
  matrix products  13.6 us (6%)
  blocking collectives  13 us (6%)
  other arithmetic  7.77 us (3%)
    ppermute x7, waiting for transfers between devices, on_device(): piece = lax.ppermute(piece, 'local', perm=pairs)  37.2 us
    reduce_scatter x2, waiting for transfers between devices, on_device(): lax.psum_scatter(expert_grads, 'local', scatter_dimension=1, tiled=True)  34.5 us
    unnamed x19, local copies, waits for them, and re-layouts  21.2 us
    all_to_all x1, starting transfers between devices, on_device(): lax.all_to_all(payload, 'node', split_axis=0, concat_axis=0, tiled=True)  19.3 us
    ppermute x7, starting transfers between devices, on_device(): piece = lax.ppermute(piece, 'local', perm=pairs)  17.8 us
    all_to_all x1, starting transfers between devices, on_device(): lax.all_to_all(summed, 'node', split_axis=0, concat_axis=0, tiled=True)  14.3 us
    all_to_all x1, waiting for transfers between devices, on_device(): lax.all_to_all(summed, 'node', split_axis=0, concat_axis=0, tiled=True)  13.1 us
    all_gather x1, blocking collectives, on_device(): lax.all_gather(partial_value, 'local', axis=0, tiled=False)  13 us
  transfers between devices with their start and end apart: 12, of which 8 were waited for; matrix products, arithmetic and copies ran while one was open for 21% of the time, Pallas kernels for 0%

profile of v11, /device:TPU:1, one launch (start us, length us, event | category | flops | bytes accessed | tf_op | source)
XLA Modules:
  0.0 225.3 jit_solution(4478231196607287884)
XLA Ops:
  7.2 0.9 copy.73
  8.0 0.8 copy.68
  8.8 0.3 convert_reduce_fusion
  9.1 0.3 fusion.7
  9.4 0.1 copy.74
  9.6 0.2 reduce_window_sum.11
  9.9 0.1 fusion.4
  10.0 0.5 convolution_convert_fusion.1
  10.6 0.1 copy.75
  10.7 0.1 copy.76
  10.8 0.5 fusion.2
  11.3 0.1 copy.87
  11.4 0.1 maximum_bitcast_fusion
  11.5 0.5 broadcast.121
  12.1 1.6 reduce
  13.7 2.3 %reshape.119 = bf16[64,2,5388]{2,1,0:T(2,128)(2,1)} reshape(bf16[64,10776]{1,0:T(8,128)(2,1)S(1)} %reduce) | data formatting | bytes 2758656
  16.1 19.3 %all-to-all-start = ((bf16[64,2,5388]{2,1,0:T(2,128)(2,1)}), bf16[64,2,5388]{2,1,0:T(2,128)(2,1)}, u32[]{:S(2)}, u32[]{:S(2)}) async-start(bf16[64,2,5388]{2,1,0:T(2,128)(2,1)} %reshape.119), calls=%async_computation | async-start | bytes 2818048 | tf_op jit(solution)/shard_map/all_to_all | solution.py:50
  35.5 0.7 all-gather.2.cloned.1.call-update
  36.3 3.3 %constant_dynamic-slice_fusion = (bf16[2,128,896]{2,1,0:T(8,128)(2,1)S(1)}, bf16[2,128,896]{2,1,0:T(8,128)(2,1)}, bf16[2,128,896]{2,1,0:T(8,128)(2,1)}, bf16[2,1...) fusion(bf16[2,128,7168]{2,1,0:T(8,128)(2,1)} %param.8, ...), kind=kLoop, calls=%fused_computation.44 | loop fusion | bytes 6422556 | tf_op jit(solution)/shard_map/dynamic_slice | solution.py:58
  39.6 2.1 collective-permute-start
  41.7 3.2 %collective-permute-start.1 = (bf16[2,128,896]{2,1,0:T(8,128)(2,1)}, bf16[2,128,896]{2,1,0:T(8,128)(2,1)S(1)}, u32[]{:S(2)}, u32[]{:S(2)}) collective-permute-start(bf16[2,128,896]{2,1,0:T(8,128)(2,1)} %get-tuple-element.10), channel_id=1, source_target_pairs={{0,2},{1,3},{2,4},{3,5},{4,6},{5,7},{6,0},{7,1},{8,10},{9,11},{10,... | collective-permute-start | bytes 1376264 | tf_op jit(solution)/shard_map/ppermute | solution.py:61
  44.9 3.5 %collective-permute-start.2 = (bf16[2,128,896]{2,1,0:T(8,128)(2,1)}, bf16[2,128,896]{2,1,0:T(8,128)(2,1)S(1)}, u32[]{:S(2)}, u32[]{:S(2)}) collective-permute-start(bf16[2,128,896]{2,1,0:T(8,128)(2,1)} %get-tuple-element.9), channel_id=1, source_target_pairs={{0,3},{1,4},{2,5},{3,6},{4,7},{5,0},{6,1},{7,2},{8,11},{9,12},{10,... | collective-permute-start | bytes 1376264 | tf_op jit(solution)/shard_map/ppermute | solution.py:61
  48.5 2.3 %collective-permute-start.3 = (bf16[2,128,896]{2,1,0:T(8,128)(2,1)}, bf16[2,128,896]{2,1,0:T(8,128)(2,1)S(1)}, u32[]{:S(2)}, u32[]{:S(2)}) collective-permute-start(bf16[2,128,896]{2,1,0:T(8,128)(2,1)} %get-tuple-element.8), channel_id=1, source_target_pairs={{0,4},{1,5},{2,6},{3,7},{4,0},{5,1},{6,2},{7,3},{8,12},{9,13},{10,... | collective-permute-start | bytes 1376264 | tf_op jit(solution)/shard_map/ppermute | solution.py:61
  50.7 3.9 %collective-permute-start.4 = (bf16[2,128,896]{2,1,0:T(8,128)(2,1)}, bf16[2,128,896]{2,1,0:T(8,128)(2,1)S(1)}, u32[]{:S(2)}, u32[]{:S(2)}) collective-permute-start(bf16[2,128,896]{2,1,0:T(8,128)(2,1)} %get-tuple-element.7), channel_id=1, source_target_pairs={{0,5},{1,6},{2,7},{3,0},{4,1},{5,2},{6,3},{7,4},{8,13},{9,14},{10,... | collective-permute-start | bytes 1376264 | tf_op jit(solution)/shard_map/ppermute | solution.py:61
  54.7 1.8 bitcast_dynamic-update-slice_fusion.7
  56.6 2.7 %collective-permute-start.5 = (bf16[2,128,896]{2,1,0:T(8,128)(2,1)S(1)}, bf16[2,128,896]{2,1,0:T(8,128)(2,1)S(1)}, u32[]{:S(2)}, u32[]{:S(2)}) collective-permute-start(bf16[2,128,896]{2,1,0:T(8,128)(2,1)S(1)} %get-tuple-element.12), channel_id=1, source_target_pairs={{0,6},{1,7},{2,0},{3,1},{4,2},{5,3},{6,4},{7,5},{8,14},{9,15},{10,... | collective-permute-start | bytes 1376264 | tf_op jit(solution)/shard_map/ppermute | solution.py:61
  59.3 0.8 bitcast_dynamic-update-slice_fusion.6
  60.1 2.2 collective-permute-done.1
  62.3 0.8 bitcast_dynamic-update-slice_fusion.5
  63.1 14.5 %collective-permute-done.2 = bf16[2,128,896]{2,1,0:T(8,128)(2,1)S(1)} collective-permute-done((bf16[2,128,896]{2,1,0:T(8,128)(2,1)}, bf16[2,128,896]{2,1,0:T(8,128)(2,1)S(1)}, u32[]{:S(2)}, u32[]{:S(2)}) %collective-permute-start.2) | collective-permute-done | bytes 458784 | tf_op jit(solution)/shard_map/ppermute | solution.py:61
  77.6 0.8 bitcast_dynamic-update-slice_fusion.4
  78.4 17.0 %collective-permute-done.3 = bf16[2,128,896]{2,1,0:T(8,128)(2,1)S(1)} collective-permute-done((bf16[2,128,896]{2,1,0:T(8,128)(2,1)}, bf16[2,128,896]{2,1,0:T(8,128)(2,1)S(1)}, u32[]{:S(2)}, u32[]{:S(2)}) %collective-permute-start.3) | collective-permute-done | bytes 458784 | tf_op jit(solution)/shard_map/ppermute | solution.py:61
  95.4 0.8 bitcast_dynamic-update-slice_fusion.3
  96.2 1.7 collective-permute-done.4
  97.9 0.8 bitcast_dynamic-update-slice_fusion.2
  98.7 1.1 collective-permute-done.5
  99.8 0.8 bitcast_dynamic-update-slice_fusion.1
  100.6 0.8 collective-permute-done.6
  101.4 0.8 bitcast_dynamic-update-slice_fusion
  102.2 4.8 %gather_fusion = bf16[8,2,128,896]{3,2,1,0:T(8,128)(2,1)} fusion(bf16[8,2,128,896]{3,2,1,0:T(8,128)(2,1)} %bitcast_dynamic-update-slice_fusion, s32[1024]{0:T(1024)S(1)} %pad_clamp_fusion), kind=kCustom, calls=%fused_computation | custom fusion | bytes 7340064 | tf_op jit(solution)/shard_map/jit(_take)/gather | solution.py:65
  107.1 2.5 %select_bitcast_fusion = bf16[2,8,128,896]{3,2,0,1:T(8,128)(2,1)S(1)} fusion(bf16[8,2,128,896]{3,2,1,0:T(8,128)(2,1)} %gather_fusion, pred[8]{0:T(512)(128)(4,1)S(1)} %compare_and_fusion), kind=kLoop, calls=%fused_computation.1 | loop fusion | flops 1835008 | bytes 7340040 | tf_op jit(solution)/shard_map/jit(_take)/select_n | solution.py:65
  109.5 2.2 fusion.16
  111.8 8.4 %reshape.120 = bf16[64,1,10776]{2,1,0:T(2,128)(2,1)S(1)} reshape(bf16[64,2,5388]{2,1,0:T(2,128)(2,1)} %all-to-all-done) | data formatting | bytes 2758656
  120.2 0.2 copy.91
  120.4 1.1 copy-done.1
  121.6 3.0 %reshape.105 = bf16[768,896]{1,0:T(8,128)(2,1)} reshape(bf16[64,10752]{1,0:T(8,128)(2,1)S(1)} %slice.29) | data formatting | bytes 2752512 | tf_op jit(solution)/shard_map/reshape | solution.py:51
  124.6 4.8 %fusion.17 = f32[768,1024]{1,0:T(8,128)} fusion(bf16[768,896]{1,0:T(8,128)(2,1)} %reshape.105, bf16[1024,896]{1,0:T(8,128)(2,1)S(1)} %bitcast.67), kind=kOutput, calls=%fused_computation.58 | convolution fusion | flops 1409286144 | bytes 6356992 | tf_op jit(solution)/shard_map/rd,hd->rh/dot_general | solution.py:71
  129.5 0.2 reduce-scatter.3.cloned.1.call-start
  129.7 1.6 copy-done.2
  131.3 6.3 %fusion.1 = (f32[768]{0:T(1024)S(1)}, f32[768]{0:T(1024)S(1)}, f32[768,1024]{1,0:T(8,128)}) fusion(bf16[2,768,1024]{2,1,0:T(8,128)(2,1)} %all-gather.2.cloned.1.call-done, f32[768,1024]{1,0:T(8,128)S(1)} %copy-done.2, bf16[768,896]{1,0:T(8,128)(2,1)} %reshape.105, bf16[1024,896]{1,0:T(8,128)(2,1)} %bitcast.66), kind=kOutput, calls=%fused_computation.5 | convolution fusion | flops 1414003200 | bytes 12654592 | tf_op jit(solution)/shard_map/rd,hd->rh/dot_general | solution.py:71
  137.7 0.1 all_gather_reshape.3
  137.9 13.0 %all_gather.7 = f32[8,64,12,2]{1,3,2,0:T(2,128)S(1)} all-gather(f32[1,64,12,2]{1,3,2,0:T(2,128)S(1)} %copy.79), channel_id=1, replica_groups=mesh['node'=64,'local'=8] {'local'}, dimensions={0}, use_global_device_ids=true | all-gather | bytes 55296 | tf_op jit(solution)/shard_map/all_gather | solution.py:83
  151.0 0.7 copy.81
  151.8 14.3 %all-to-all-start.1 = ((f32[64,12,2]{1,2,0:T(2,128)}), f32[64,12,2]{1,2,0:T(2,128)S(1)}, u32[]{:S(2)}, u32[]{:S(2)}) async-start(f32[64,12,2]{1,2,0:T(2,128)} %copy.81), calls=%async_computation.3 | async-start | bytes 131072 | tf_op jit(solution)/shard_map/all_to_all | solution.py:87
  166.1 0.7 slice_convert_fusion
  166.8 0.2 reshape.109
  167.0 0.1 copy.78
  167.1 13.1 %all-to-all-done.1 = f32[64,12,2]{1,2,0:T(2,128)S(1)} async-done(((f32[64,12,2]{1,2,0:T(2,128)}), f32[64,12,2]{1,2,0:T(2,128)S(1)}, u32[]{:S(2)}, u32[]{:S(2)}) %all-to-all-start.1) | async-done | bytes 6176 | tf_op jit(solution)/shard_map/all_to_all | solution.py:87
  180.3 0.4 convolution_bitcast_fusion
  180.7 0.1 copy.82
  180.8 0.6 fusion.6
  181.5 0.7 copy.83
  182.1 34.5 %reduce-scatter.3.cloned.1.call-done = f32[768,128]{1,0:T(8,128)} async-done(((f32[768,1024]{1,0:T(8,128)}), f32[768,128]{1,0:T(8,128)}) %reduce-scatter.3.cloned.1.call-update) | async-done | bytes 393232 | tf_op jit(solution)/shard_map/reduce_scatter | solution.py:79
  216.6 2.1 fusion.3
  (28 shorter events, 0.6 us)
Async XLA Ops:
  7.2 3.6 %copy-start = (bf16[128,896]{1,0:T(8,128)(2,1)S(1)}, bf16[128,896]{1,0:T(8,128)(2,1)}, u32[]{:S(2)}) copy-start(bf16[128,896]{1,0:T(8,128)(2,1)} %param.5) | copy-start | bytes 688132
  16.1 95.7 %all-to-all-start = ((bf16[64,2,5388]{2,1,0:T(2,128)(2,1)}), bf16[64,2,5388]{2,1,0:T(2,128)(2,1)}, u32[]{:S(2)}, u32[]{:S(2)}) async-start(bf16[64,2,5388]{2,1,0:T(2,128)(2,1)} %reshape.119), calls=%async_computation | async-start | bytes 2818048 | tf_op jit(solution)/shard_map/all_to_all | solution.py:50
  35.4 94.3 %all-gather.2.cloned.1.call-start = ((), (), s32[]{:S(2)}) async-start(), calls=%async_computation.6 | async-start | bytes 3538944 | tf_op jit(solution)/shard_map/all_gather | solution.py:67
  36.1 146.0 %reduce-scatter.5.cloned.1.call-start = ((), (), s32[]{:S(2)}) async-start(), calls=%async_computation.5 | async-start | bytes 3538944 | tf_op jit(solution)/shard_map/reduce_scatter | solution.py:79
  39.6 17.0 %collective-permute-start = (bf16[2,128,896]{2,1,0:T(8,128)(2,1)}, bf16[2,128,896]{2,1,0:T(8,128)(2,1)S(1)}, u32[]{:S(2)}, u32[]{:S(2)}) collective-permute-start(bf16[2,128,896]{2,1,0:T(8,128)(2,1)} %get-tuple-element.11), channel_id=1, source_target_pairs={{0,1},{1,2},{2,3},{3,4},{4,5},{5,6},{6,7},{7,0},{8,9},{9,10},{10,1... | collective-permute-start | bytes 1376264 | tf_op jit(solution)/shard_map/ppermute | solution.py:61
  41.7 20.6 %collective-permute-start.1 = (bf16[2,128,896]{2,1,0:T(8,128)(2,1)}, bf16[2,128,896]{2,1,0:T(8,128)(2,1)S(1)}, u32[]{:S(2)}, u32[]{:S(2)}) collective-permute-start(bf16[2,128,896]{2,1,0:T(8,128)(2,1)} %get-tuple-element.10), channel_id=1, source_target_pairs={{0,2},{1,3},{2,4},{3,5},{4,6},{5,7},{6,0},{7,1},{8,10},{9,11},{10,... | collective-permute-start | bytes 1376264 | tf_op jit(solution)/shard_map/ppermute | solution.py:61
  44.9 32.6 %collective-permute-start.2 = (bf16[2,128,896]{2,1,0:T(8,128)(2,1)}, bf16[2,128,896]{2,1,0:T(8,128)(2,1)S(1)}, u32[]{:S(2)}, u32[]{:S(2)}) collective-permute-start(bf16[2,128,896]{2,1,0:T(8,128)(2,1)} %get-tuple-element.9), channel_id=1, source_target_pairs={{0,3},{1,4},{2,5},{3,6},{4,7},{5,0},{6,1},{7,2},{8,11},{9,12},{10,... | collective-permute-start | bytes 1376264 | tf_op jit(solution)/shard_map/ppermute | solution.py:61
  48.5 46.9 %collective-permute-start.3 = (bf16[2,128,896]{2,1,0:T(8,128)(2,1)}, bf16[2,128,896]{2,1,0:T(8,128)(2,1)S(1)}, u32[]{:S(2)}, u32[]{:S(2)}) collective-permute-start(bf16[2,128,896]{2,1,0:T(8,128)(2,1)} %get-tuple-element.8), channel_id=1, source_target_pairs={{0,4},{1,5},{2,6},{3,7},{4,0},{5,1},{6,2},{7,3},{8,12},{9,13},{10,... | collective-permute-start | bytes 1376264 | tf_op jit(solution)/shard_map/ppermute | solution.py:61
  50.7 47.2 %collective-permute-start.4 = (bf16[2,128,896]{2,1,0:T(8,128)(2,1)}, bf16[2,128,896]{2,1,0:T(8,128)(2,1)S(1)}, u32[]{:S(2)}, u32[]{:S(2)}) collective-permute-start(bf16[2,128,896]{2,1,0:T(8,128)(2,1)} %get-tuple-element.7), channel_id=1, source_target_pairs={{0,5},{1,6},{2,7},{3,0},{4,1},{5,2},{6,3},{7,4},{8,13},{9,14},{10,... | collective-permute-start | bytes 1376264 | tf_op jit(solution)/shard_map/ppermute | solution.py:61
  56.6 43.2 %collective-permute-start.5 = (bf16[2,128,896]{2,1,0:T(8,128)(2,1)S(1)}, bf16[2,128,896]{2,1,0:T(8,128)(2,1)S(1)}, u32[]{:S(2)}, u32[]{:S(2)}) collective-permute-start(bf16[2,128,896]{2,1,0:T(8,128)(2,1)S(1)} %get-tuple-element.12), channel_id=1, source_target_pairs={{0,6},{1,7},{2,0},{3,1},{4,2},{5,3},{6,4},{7,5},{8,14},{9,15},{10,... | collective-permute-start | bytes 1376264 | tf_op jit(solution)/shard_map/ppermute | solution.py:61
  62.3 39.1 %collective-permute-start.6 = (bf16[2,128,896]{2,1,0:T(8,128)(2,1)S(1)}, bf16[2,128,896]{2,1,0:T(8,128)(2,1)S(1)}, u32[]{:S(2)}, u32[]{:S(2)}) collective-permute-start(bf16[2,128,896]{2,1,0:T(8,128)(2,1)S(1)} %get-tuple-element.6), channel_id=1, source_target_pairs={{0,7},{1,0},{2,1},{3,2},{4,3},{5,4},{6,5},{7,6},{8,15},{9,8},{10,9... | collective-permute-start | bytes 1376264 | tf_op jit(solution)/shard_map/ppermute | solution.py:61
  120.4 1.2 copy-start.1
  120.4 4.3 %copy-start.3 = (bf16[1,8,128,896]{3,2,0,1:T(8,128)(2,1)S(1)}, bf16[1,8,128,896]{3,2,0,1:T(8,128)(2,1)}, u32[]{:S(2)}) copy-start(bf16[1,8,128,896]{3,2,0,1:T(8,128)(2,1)} %get-tuple-element.5) | copy-start | bytes 5505028
  129.4 1.9 copy-start.2
  129.5 87.2 %reduce-scatter.3.cloned.1.call-start = ((), (), s32[]{:S(2)}) async-start(), calls=%async_computation.4 | async-start | bytes 3538944 | tf_op jit(solution)/shard_map/reduce_scatter | solution.py:79
  151.8 28.5 %all-to-all-start.1 = ((f32[64,12,2]{1,2,0:T(2,128)}), f32[64,12,2]{1,2,0:T(2,128)S(1)}, u32[]{:S(2)}, u32[]{:S(2)}) async-start(f32[64,12,2]{1,2,0:T(2,128)} %copy.81), calls=%async_computation.3 | async-start | bytes 131072 | tf_op jit(solution)/shard_map/all_to_all | solution.py:87
Sparse Core Ops, SparseCore 0:
  38.4 60.9 all-gather.1
  129.6 41.4 reduce-scatter.4
  173.9 42.6 reduce-scatter.2

commit v12 on v10

--- a/solution.py
+++ b/solution.py
@@ -71,7 +71,8 @@
         preferred_element_type=jnp.float32,
     )
     saved_full = lax.all_gather(saved_hidden, "local", axis=2, tiled=True)
-    partial_scores = jnp.sum(saved_full.astype(jnp.float32) * partial_grads, axis=2)
+    held_grads = lax.optimization_barrier(partial_grads)
+    partial_scores = jnp.sum(saved_full.astype(jnp.float32) * held_grads, axis=2)
     partial_value = jnp.transpose(partial_scores).reshape(node_count, capacity, expert_count)
     summed = jnp.sum(lax.all_gather(partial_value, "local", axis=0, tiled=False), axis=0)
     hidden_grads = lax.psum_scatter(partial_grads, "local", scatter_dimension=2, tiled=True)

time: 192 us -> 192 us (level)
  starting transfers between devices: 56.3 us -> 51.7 us
  other arithmetic: 6.79 us -> 11.2 us
    ppermute x7, waiting for transfers between devices: 30.5 us -> 36.9 us  [on_device(): piece = lax.ppermute(piece, 'local', perm=pairs)]
    reduce_scatter x1, waiting for transfers between devices: 5.62 us -> 0.98 us  [on_device(): lax.psum_scatter(partial_grads, 'local', scatter_dimension=2, tiled=True)]
    reduce_sum x0 -> x1, other arithmetic: none -> 4.36 us  [on_device(): jnp.sum(saved_full.astype(jnp.float32) * held_grads, axis=2)]
    ppermute x7, starting transfers between devices: 21.9 us -> 17.9 us  [on_device(): piece = lax.ppermute(piece, 'local', perm=pairs)]
    unnamed x17 -> x19, local copies, waits for them, and re-layouts: 22.4 us -> 21.5 us
  transfers between devices with their start and end apart: 11 -> 11, of which waited for: 5 -> 8; matrix products, arithmetic and copies ran while one was open for 23% -> 26% of each run, Pallas kernels for 0% -> 0%
where the time goes in v12:
time: 192 us; the launch traced here: 191 us
  starting transfers between devices  51.7 us (27%)
  waiting for transfers between devices  51.1 us (27%)
  local copies, waits for them, and re-layouts  38.9 us (20%)
  between operations  14.4 us (8%)
  blocking collectives  13.1 us (7%)
  other arithmetic  11.2 us (6%)
  matrix products  10.7 us (6%)
    ppermute x7, waiting for transfers between devices, on_device(): piece = lax.ppermute(piece, 'local', perm=pairs)  36.9 us
    unnamed x19, local copies, waits for them, and re-layouts  21.5 us
    all_to_all x1, starting transfers between devices, on_device(): lax.all_to_all(payload, 'node', split_axis=0, concat_axis=0, tiled=True)  19.3 us
    ppermute x7, starting transfers between devices, on_device(): piece = lax.ppermute(piece, 'local', perm=pairs)  17.9 us
    all_to_all x1, starting transfers between devices, on_device(): lax.all_to_all(summed, 'node', split_axis=0, concat_axis=0, tiled=True)  14.3 us
    all_to_all x1, waiting for transfers between devices, on_device(): lax.all_to_all(summed, 'node', split_axis=0, concat_axis=0, tiled=True)  13.1 us
    all_gather x1, blocking collectives, on_device(): lax.all_gather(partial_value, 'local', axis=0, tiled=False)  13.1 us
    dot_general x1, matrix products, on_device(): jnp.einsum('rd,ehd->erh', rows_in, weight_cols, preferred_element_type=jn...  8.19 us
  transfers between devices with their start and end apart: 11, of which 8 were waited for; matrix products, arithmetic and copies ran while one was open for 26% of the time, Pallas kernels for 0%

profile of v12, /device:TPU:1, one launch (start us, length us, event | category | flops | bytes accessed | tf_op | source)
XLA Modules:
  0.0 191.0 jit_solution(3008205002682476440)
XLA Ops:
  7.2 0.8 copy.97
  8.0 0.3 convert_reduce_fusion
  8.3 0.2 reduce_window_sum.11
  8.6 0.8 copy.102
  9.5 0.3 fusion.4
  9.8 0.1 copy.103
  9.9 0.1 fusion.1
  10.0 0.5 convolution_convert_fusion.1
  10.6 0.1 copy.104
  10.7 0.1 copy.105
  10.8 0.5 fusion
  11.3 0.1 copy.119
  11.4 0.1 maximum_bitcast_fusion
  11.5 0.5 broadcast.121
  12.1 1.7 reduce
  13.8 2.4 %reshape.114 = bf16[64,2,5388]{2,1,0:T(2,128)(2,1)} reshape(bf16[64,10776]{1,0:T(8,128)(2,1)S(1)} %reduce) | data formatting | bytes 2758656
  16.1 19.3 %all-to-all-start = ((bf16[64,2,5388]{2,1,0:T(2,128)(2,1)}), bf16[64,2,5388]{2,1,0:T(2,128)(2,1)}, u32[]{:S(2)}, u32[]{:S(2)}) async-start(bf16[64,2,5388]{2,1,0:T(2,128)(2,1)} %reshape.114), calls=%async_computation | async-start | bytes 2818048 | tf_op jit(solution)/shard_map/all_to_all | solution.py:50
  35.5 0.9 copy.109
  36.6 3.3 %constant_dynamic-slice_fusion = (bf16[2,128,896]{2,1,0:T(8,128)(2,1)S(1)}, bf16[2,128,896]{2,1,0:T(8,128)(2,1)}, bf16[2,128,896]{2,1,0:T(8,128)(2,1)}, bf16[2,1...) fusion(bf16[2,128,7168]{2,1,0:T(8,128)(2,1)} %param.8, ...), kind=kLoop, calls=%fused_computation.38 | loop fusion | bytes 6422556 | tf_op jit(solution)/shard_map/dynamic_slice | solution.py:58
  39.9 2.1 %collective-permute-start = (bf16[2,128,896]{2,1,0:T(8,128)(2,1)}, bf16[2,128,896]{2,1,0:T(8,128)(2,1)S(1)}, u32[]{:S(2)}, u32[]{:S(2)}) collective-permute-start(bf16[2,128,896]{2,1,0:T(8,128)(2,1)} %get-tuple-element.21), channel_id=1, source_target_pairs={{0,1},{1,2},{2,3},{3,4},{4,5},{5,6},{6,7},{7,0},{8,9},{9,10},{10,1... | collective-permute-start | bytes 1376264 | tf_op jit(solution)/shard_map/ppermute | solution.py:61
  42.1 3.2 %collective-permute-start.1 = (bf16[2,128,896]{2,1,0:T(8,128)(2,1)}, bf16[2,128,896]{2,1,0:T(8,128)(2,1)S(1)}, u32[]{:S(2)}, u32[]{:S(2)}) collective-permute-start(bf16[2,128,896]{2,1,0:T(8,128)(2,1)} %get-tuple-element.20), channel_id=1, source_target_pairs={{0,2},{1,3},{2,4},{3,5},{4,6},{5,7},{6,0},{7,1},{8,10},{9,11},{10,... | collective-permute-start | bytes 1376264 | tf_op jit(solution)/shard_map/ppermute | solution.py:61
  45.3 3.5 %collective-permute-start.2 = (bf16[2,128,896]{2,1,0:T(8,128)(2,1)}, bf16[2,128,896]{2,1,0:T(8,128)(2,1)S(1)}, u32[]{:S(2)}, u32[]{:S(2)}) collective-permute-start(bf16[2,128,896]{2,1,0:T(8,128)(2,1)} %get-tuple-element.19), channel_id=1, source_target_pairs={{0,3},{1,4},{2,5},{3,6},{4,7},{5,0},{6,1},{7,2},{8,11},{9,12},{10,... | collective-permute-start | bytes 1376264 | tf_op jit(solution)/shard_map/ppermute | solution.py:61
  48.8 2.3 %collective-permute-start.3 = (bf16[2,128,896]{2,1,0:T(8,128)(2,1)}, bf16[2,128,896]{2,1,0:T(8,128)(2,1)S(1)}, u32[]{:S(2)}, u32[]{:S(2)}) collective-permute-start(bf16[2,128,896]{2,1,0:T(8,128)(2,1)} %get-tuple-element.18), channel_id=1, source_target_pairs={{0,4},{1,5},{2,6},{3,7},{4,0},{5,1},{6,2},{7,3},{8,12},{9,13},{10,... | collective-permute-start | bytes 1376264 | tf_op jit(solution)/shard_map/ppermute | solution.py:61
  51.0 3.9 %collective-permute-start.4 = (bf16[2,128,896]{2,1,0:T(8,128)(2,1)}, bf16[2,128,896]{2,1,0:T(8,128)(2,1)S(1)}, u32[]{:S(2)}, u32[]{:S(2)}) collective-permute-start(bf16[2,128,896]{2,1,0:T(8,128)(2,1)} %get-tuple-element.17), channel_id=1, source_target_pairs={{0,5},{1,6},{2,7},{3,0},{4,1},{5,2},{6,3},{7,4},{8,13},{9,14},{10,... | collective-permute-start | bytes 1376264 | tf_op jit(solution)/shard_map/ppermute | solution.py:61
  55.0 1.8 bitcast_dynamic-update-slice_fusion.7
  56.9 2.9 %collective-permute-start.5 = (bf16[2,128,896]{2,1,0:T(8,128)(2,1)S(1)}, bf16[2,128,896]{2,1,0:T(8,128)(2,1)S(1)}, u32[]{:S(2)}, u32[]{:S(2)}) collective-permute-start(bf16[2,128,896]{2,1,0:T(8,128)(2,1)S(1)} %get-tuple-element.22), channel_id=1, source_target_pairs={{0,6},{1,7},{2,0},{3,1},{4,2},{5,3},{6,4},{7,5},{8,14},{9,15},{10,... | collective-permute-start | bytes 1376264 | tf_op jit(solution)/shard_map/ppermute | solution.py:61
  59.8 0.8 bitcast_dynamic-update-slice_fusion.6
  60.6 1.6 collective-permute-done.1
  62.2 0.8 bitcast_dynamic-update-slice_fusion.5
  63.0 17.6 %collective-permute-done.2 = bf16[2,128,896]{2,1,0:T(8,128)(2,1)S(1)} collective-permute-done((bf16[2,128,896]{2,1,0:T(8,128)(2,1)}, bf16[2,128,896]{2,1,0:T(8,128)(2,1)S(1)}, u32[]{:S(2)}, u32[]{:S(2)}) %collective-permute-start.2) | collective-permute-done | bytes 458784 | tf_op jit(solution)/shard_map/ppermute | solution.py:61
  80.7 0.8 bitcast_dynamic-update-slice_fusion.4
  81.5 14.2 %collective-permute-done.3 = bf16[2,128,896]{2,1,0:T(8,128)(2,1)S(1)} collective-permute-done((bf16[2,128,896]{2,1,0:T(8,128)(2,1)}, bf16[2,128,896]{2,1,0:T(8,128)(2,1)S(1)}, u32[]{:S(2)}, u32[]{:S(2)}) %collective-permute-start.3) | collective-permute-done | bytes 458784 | tf_op jit(solution)/shard_map/ppermute | solution.py:61
  95.7 0.8 bitcast_dynamic-update-slice_fusion.3
  96.5 1.7 collective-permute-done.4
  98.2 0.9 bitcast_dynamic-update-slice_fusion.2
  99.1 1.1 collective-permute-done.5
  100.1 0.9 bitcast_dynamic-update-slice_fusion.1
  101.0 0.7 collective-permute-done.6
  101.7 0.8 bitcast_dynamic-update-slice_fusion
  102.6 4.9 %gather_fusion = bf16[8,2,128,896]{3,2,1,0:T(8,128)(2,1)} fusion(bf16[8,2,128,896]{3,2,1,0:T(8,128)(2,1)} %bitcast_dynamic-update-slice_fusion, s32[1024]{0:T(1024)S(1)} %pad_clamp_fusion), kind=kCustom, calls=%fused_computation | custom fusion | bytes 7340064 | tf_op jit(solution)/shard_map/jit(_take)/gather | solution.py:65
  107.5 2.5 %select_bitcast_fusion = bf16[2,8,128,896]{3,2,0,1:T(8,128)(2,1)S(1)} fusion(bf16[8,2,128,896]{3,2,1,0:T(8,128)(2,1)} %gather_fusion, pred[8]{0:T(512)(128)(4,1)S(1)} %compare_and_fusion), kind=kLoop, calls=%fused_computation.2 | loop fusion | flops 1835008 | bytes 7340040 | tf_op jit(solution)/shard_map/jit(_take)/select_n | solution.py:65
  109.9 2.2 %copy.108 = bf16[2,8,128,896]{3,2,1,0:T(8,128)(2,1)} copy(bf16[2,8,128,896]{3,2,0,1:T(8,128)(2,1)S(1)} %select_bitcast_fusion) | data formatting | bytes 7340032 | tf_op jit(solution)/shard_map/jit(_take)/select_n | solution.py:65
  112.1 8.4 %reshape.115 = bf16[64,1,10776]{2,1,0:T(2,128)(2,1)S(1)} reshape(bf16[64,2,5388]{2,1,0:T(2,128)(2,1)} %all-to-all-done) | data formatting | bytes 2758656
  120.6 0.2 copy.123
  120.7 1.1 copy-done.1
  121.8 0.1 slice.11
  121.9 2.2 %reshape.112 = bf16[768,896,1]{1,0,2:T(8,128)(2,1)S(1)} reshape(bf16[64,10752]{1,0:T(8,128)(2,1)S(1)} %slice.11) | data formatting | bytes 2752512 | tf_op jit(solution)/shard_map/reshape | solution.py:51
  124.1 8.2 %convolution_bitcast_fusion = f32[2,768,1024]{1,2,0:T(8,128)} fusion(bf16[2,1024,896]{2,1,0:T(8,128)(2,1)} %bitcast.52, bf16[768,896,1]{1,0,2:T(8,128)(2,1)S(1)} %reshape.112), kind=kOutput, calls=%fused_computation.3 | convolution fusion | flops 2818572288 | bytes 11337728 | tf_op jit(solution)/shard_map/rd,ehd->erh/dot_general | solution.py:67
  132.3 4.4 %multiply_reduce_fusion = f32[2,768]{1,0:T(2,128)S(1)} fusion(f32[2,768,1024]{1,2,0:T(8,128)} %convolution_bitcast_fusion, bf16[2,768,1024]{1,2,0:T(8,128)(2,1)} %all-gather.2.cloned.1.call-done), kind=kLoop, calls=%fused_computation.1 | loop fusion | flops 4717056 | bytes 9443328 | tf_op jit(solution)/shard_map/reduce_sum | solution.py:75
  136.7 0.1 all_gather_reshape.3
  136.9 13.1 %all_gather.7 = f32[8,64,12,2]{1,3,2,0:T(2,128)S(1)} all-gather(f32[1,64,12,2]{1,3,2,0:T(2,128)S(1)} %copy.110), channel_id=1, replica_groups=mesh['node'=64,'local'=8] {'local'}, dimensions={0}, use_global_device_ids=true | all-gather | bytes 55296 | tf_op jit(solution)/shard_map/all_gather | solution.py:77
  150.0 0.7 copy.112
  150.8 14.3 %all-to-all-start.1 = ((f32[64,12,2]{1,2,0:T(2,128)}), f32[64,12,2]{1,2,0:T(2,128)S(1)}, u32[]{:S(2)}, u32[]{:S(2)}) async-start(f32[64,12,2]{1,2,0:T(2,128)} %copy.112), calls=%async_computation.2 | async-start | bytes 131072 | tf_op jit(solution)/shard_map/all_to_all | solution.py:81
  165.1 0.7 slice_convert_fusion
  165.8 0.2 reshape.102
  166.0 0.1 copy.107
  166.1 13.1 %all-to-all-done.1 = f32[64,12,2]{1,2,0:T(2,128)S(1)} async-done(((f32[64,12,2]{1,2,0:T(2,128)}), f32[64,12,2]{1,2,0:T(2,128)S(1)}, u32[]{:S(2)}, u32[]{:S(2)}) %all-to-all-start.1) | async-done | bytes 6176 | tf_op jit(solution)/shard_map/all_to_all | solution.py:81
  179.2 0.4 convolution_bitcast_fusion.1
  179.7 0.1 copy.113
  179.8 0.6 fusion.3
  180.4 0.7 copy.114
  181.1 1.0 reduce-scatter.2.cloned.1.call-done
  182.1 1.2 multiply_convert_fusion
  183.3 0.9 copy.115
  (22 shorter events, 0.5 us)
Async XLA Ops:
  7.2 3.6 %copy-start = (bf16[128,896]{1,0:T(8,128)(2,1)S(1)}, bf16[128,896]{1,0:T(8,128)(2,1)}, u32[]{:S(2)}) copy-start(bf16[128,896]{1,0:T(8,128)(2,1)} %param.5) | copy-start | bytes 688132
  12.1 23.5 %copy-start.2 = (bf16[2,768,128]{2,1,0:T(8,128)(2,1)S(1)}, bf16[2,768,128]{2,1,0:T(8,128)(2,1)}, u32[]{:S(2)}) copy-start(bf16[2,768,128]{2,1,0:T(8,128)(2,1)} %param.9) | copy-start | bytes 1179652
  16.1 96.0 %all-to-all-start = ((bf16[64,2,5388]{2,1,0:T(2,128)(2,1)}), bf16[64,2,5388]{2,1,0:T(2,128)(2,1)}, u32[]{:S(2)}, u32[]{:S(2)}) async-start(bf16[64,2,5388]{2,1,0:T(2,128)(2,1)} %reshape.114), calls=%async_computation | async-start | bytes 2818048 | tf_op jit(solution)/shard_map/all_to_all | solution.py:50
  35.5 96.9 %all-gather.2.cloned.1.call-start = ((), (), s32[]{:S(2)}) async-start(), calls=%async_computation.4 | async-start | bytes 3538944 | tf_op jit(solution)/shard_map/all_gather | solution.py:73
  36.5 145.6 %reduce-scatter.2.cloned.1.call-start = ((), (), s32[]{:S(2)}) async-start(), calls=%async_computation.3 | async-start | bytes 7077888 | tf_op jit(solution)/shard_map/reduce_scatter | solution.py:78
  39.9 16.9 %collective-permute-start = (bf16[2,128,896]{2,1,0:T(8,128)(2,1)}, bf16[2,128,896]{2,1,0:T(8,128)(2,1)S(1)}, u32[]{:S(2)}, u32[]{:S(2)}) collective-permute-start(bf16[2,128,896]{2,1,0:T(8,128)(2,1)} %get-tuple-element.21), channel_id=1, source_target_pairs={{0,1},{1,2},{2,3},{3,4},{4,5},{5,6},{6,7},{7,0},{8,9},{9,10},{10,1... | collective-permute-start | bytes 1376264 | tf_op jit(solution)/shard_map/ppermute | solution.py:61
  42.1 20.2 %collective-permute-start.1 = (bf16[2,128,896]{2,1,0:T(8,128)(2,1)}, bf16[2,128,896]{2,1,0:T(8,128)(2,1)S(1)}, u32[]{:S(2)}, u32[]{:S(2)}) collective-permute-start(bf16[2,128,896]{2,1,0:T(8,128)(2,1)} %get-tuple-element.20), channel_id=1, source_target_pairs={{0,2},{1,3},{2,4},{3,5},{4,6},{5,7},{6,0},{7,1},{8,10},{9,11},{10,... | collective-permute-start | bytes 1376264 | tf_op jit(solution)/shard_map/ppermute | solution.py:61
  45.3 35.4 %collective-permute-start.2 = (bf16[2,128,896]{2,1,0:T(8,128)(2,1)}, bf16[2,128,896]{2,1,0:T(8,128)(2,1)S(1)}, u32[]{:S(2)}, u32[]{:S(2)}) collective-permute-start(bf16[2,128,896]{2,1,0:T(8,128)(2,1)} %get-tuple-element.19), channel_id=1, source_target_pairs={{0,3},{1,4},{2,5},{3,6},{4,7},{5,0},{6,1},{7,2},{8,11},{9,12},{10,... | collective-permute-start | bytes 1376264 | tf_op jit(solution)/shard_map/ppermute | solution.py:61
  48.8 46.9 %collective-permute-start.3 = (bf16[2,128,896]{2,1,0:T(8,128)(2,1)}, bf16[2,128,896]{2,1,0:T(8,128)(2,1)S(1)}, u32[]{:S(2)}, u32[]{:S(2)}) collective-permute-start(bf16[2,128,896]{2,1,0:T(8,128)(2,1)} %get-tuple-element.18), channel_id=1, source_target_pairs={{0,4},{1,5},{2,6},{3,7},{4,0},{5,1},{6,2},{7,3},{8,12},{9,13},{10,... | collective-permute-start | bytes 1376264 | tf_op jit(solution)/shard_map/ppermute | solution.py:61
  51.0 47.2 %collective-permute-start.4 = (bf16[2,128,896]{2,1,0:T(8,128)(2,1)}, bf16[2,128,896]{2,1,0:T(8,128)(2,1)S(1)}, u32[]{:S(2)}, u32[]{:S(2)}) collective-permute-start(bf16[2,128,896]{2,1,0:T(8,128)(2,1)} %get-tuple-element.17), channel_id=1, source_target_pairs={{0,5},{1,6},{2,7},{3,0},{4,1},{5,2},{6,3},{7,4},{8,13},{9,14},{10,... | collective-permute-start | bytes 1376264 | tf_op jit(solution)/shard_map/ppermute | solution.py:61
  56.9 43.3 %collective-permute-start.5 = (bf16[2,128,896]{2,1,0:T(8,128)(2,1)S(1)}, bf16[2,128,896]{2,1,0:T(8,128)(2,1)S(1)}, u32[]{:S(2)}, u32[]{:S(2)}) collective-permute-start(bf16[2,128,896]{2,1,0:T(8,128)(2,1)S(1)} %get-tuple-element.22), channel_id=1, source_target_pairs={{0,6},{1,7},{2,0},{3,1},{4,2},{5,3},{6,4},{7,5},{8,14},{9,15},{10,... | collective-permute-start | bytes 1376264 | tf_op jit(solution)/shard_map/ppermute | solution.py:61
  62.2 39.5 %collective-permute-start.6 = (bf16[2,128,896]{2,1,0:T(8,128)(2,1)S(1)}, bf16[2,128,896]{2,1,0:T(8,128)(2,1)S(1)}, u32[]{:S(2)}, u32[]{:S(2)}) collective-permute-start(bf16[2,128,896]{2,1,0:T(8,128)(2,1)S(1)} %get-tuple-element.16), channel_id=1, source_target_pairs={{0,7},{1,0},{2,1},{3,2},{4,3},{5,4},{6,5},{7,6},{8,15},{9,8},{10,9... | collective-permute-start | bytes 1376264 | tf_op jit(solution)/shard_map/ppermute | solution.py:61
  120.7 1.1 copy-start.1
  150.8 28.5 %all-to-all-start.1 = ((f32[64,12,2]{1,2,0:T(2,128)}), f32[64,12,2]{1,2,0:T(2,128)S(1)}, u32[]{:S(2)}, u32[]{:S(2)}) async-start(f32[64,12,2]{1,2,0:T(2,128)} %copy.112), calls=%async_computation.2 | async-start | bytes 131072 | tf_op jit(solution)/shard_map/all_to_all | solution.py:81
Sparse Core Ops, SparseCore 0:
  39.0 61.8 all-gather.1
  132.4 49.6 reduce-scatter.1

commit v13 on v10

--- a/solution.py
+++ b/solution.py
@@ -40,16 +40,18 @@
         preferred_element_type=jnp.float32,
     ).astype(grad_out.dtype)
     width = grad_out.shape[1]
+    halves = 2
+    per_half = capacity // halves
     payload = jnp.concatenate(
         [
-            rows_send.reshape(node_count, capacity * width),
-            prob_send.reshape(node_count, capacity * expert_count),
+            rows_send.reshape(node_count, halves, per_half * width),
+            prob_send.reshape(node_count, halves, per_half * expert_count),
         ],
-        axis=1,
+        axis=2,
     )
     payload_in = lax.all_to_all(payload, "node", split_axis=0, concat_axis=0, tiled=True)
-    rows_in = payload_in[:, : capacity * width].reshape(slot_rows, width)
-    prob_in = payload_in[:, capacity * width :]
+    rows_in = payload_in[:, :, : per_half * width].reshape(slot_rows, width)
+    prob_in = payload_in[:, :, per_half * width :]
     local_count = lax.axis_size("local")
     local_index = lax.axis_index("local")
     pieces = []

time: 192 us -> 183 us (0.953)
  local copies, waits for them, and re-layouts: 39.8 us -> 30.8 us
    unnamed x17 -> x16, local copies, waits for them, and re-layouts: 22.4 us -> 11.5 us
    concatenate x0 -> x1, other arithmetic: none -> 2.37 us  [on_device(): jnp.concatenate([rows_send.reshape(node_count, halves, per_half * width),...]
  transfers between devices with their start and end apart: 11 -> 11, of which waited for: 5 -> 5; matrix products, arithmetic and copies ran while one was open for 23% -> 20% of each run, Pallas kernels for 0% -> 0%
where the time goes in v13:
time: 183 us; the launch traced here: 182 us
  starting transfers between devices  56.2 us (31%)
  waiting for transfers between devices  49.2 us (27%)
  local copies, waits for them, and re-layouts  30.8 us (17%)
  between operations  14.4 us (8%)
  blocking collectives  12.5 us (7%)
  matrix products  12 us (7%)
  other arithmetic  6.72 us (4%)
    ppermute x7, waiting for transfers between devices, on_device(): piece = lax.ppermute(piece, 'local', perm=pairs)  29.9 us
    ppermute x7, starting transfers between devices, on_device(): piece = lax.ppermute(piece, 'local', perm=pairs)  22 us
    all_to_all x1, starting transfers between devices, on_device(): lax.all_to_all(payload, 'node', split_axis=0, concat_axis=0, tiled=True)  19.1 us
    all_to_all x1, starting transfers between devices, on_device(): lax.all_to_all(summed, 'node', split_axis=0, concat_axis=0, tiled=True)  15 us
    all_to_all x1, waiting for transfers between devices, on_device(): lax.all_to_all(summed, 'node', split_axis=0, concat_axis=0, tiled=True)  13.8 us
    all_gather x1, blocking collectives, on_device(): lax.all_gather(partial_value, 'local', axis=0, tiled=False)  12.5 us
    unnamed x16, local copies, waits for them, and re-layouts  11.5 us
    dot_general x1, matrix products, on_device(): jnp.einsum('rd,ehd->erh', rows_in, weight_cols, preferred_element_type=jn...  9.58 us
  transfers between devices with their start and end apart: 11, of which 5 were waited for; matrix products, arithmetic and copies ran while one was open for 20% of the time, Pallas kernels for 0%

profile of v13, /device:TPU:1, one launch (start us, length us, event | category | flops | bytes accessed | tf_op | source)
XLA Modules:
  0.0 181.9 jit_solution(16893146861389067005)
XLA Ops:
  7.2 0.0 all-gather.2.cloned.1.call-start
  7.2 2.0 %copy.87 = bf16[2,768,128]{1,2,0:T(8,128)(2,1)} copy(bf16[2,768,128]{2,1,0:T(8,128)(2,1)} %param.9) | data formatting | bytes 786432 | tf_op args[4]
  9.2 0.0 all-gather.2.cloned.1.call-update
  9.2 0.8 copy.76
  10.0 0.3 convert_reduce_fusion
  10.3 0.1 copy.78
  10.4 0.2 reduce_window_sum.11
  10.6 0.1 copy.77
  10.6 0.0 copy-start.1
  10.6 0.8 copy.81
  11.5 0.3 fusion.3
  11.8 0.1 copy.82
  11.9 0.1 fusion
  12.1 0.5 convolution_convert_fusion.1
  12.6 0.1 copy.83
  12.7 0.1 copy.84
  12.9 0.5 convolution_convert_fusion
  13.4 0.8 copy.80
  14.2 0.8 reshape.94
  15.0 2.4 %pad_maximum_fusion = bf16[64,2,5388]{2,1,0:T(2,128)(2,1)} fusion(bf16[64,2,12]{2,1,0:T(2,128)(2,1)S(1)} %copy.84, bf16[64,2,5376]{2,1,0:T(2,128)(2,1)S(1)} %reshape.94), kind=kLoop, calls=%fused_computation.5 | loop fusion | flops 2758656 | bytes 2758656 | tf_op jit(solution)/shard_map/concatenate | solution.py:45
  17.4 19.1 %all-to-all-start = ((bf16[64,2,5388]{2,1,0:T(2,128)(2,1)}), bf16[64,2,5388]{2,1,0:T(2,128)(2,1)S(1)}, u32[]{:S(2)}, u32[]{:S(2)}) async-start(bf16[64,2,5388]{2,1,0:T(2,128)(2,1)} %pad_maximum_fusion), calls=%async_computation | async-start | bytes 2818048 | tf_op jit(solution)/shard_map/all_to_all | solution.py:52
  36.5 0.0 reduce-scatter.2.cloned.1.call-start
  36.7 3.7 %constant_dynamic-slice_fusion = (bf16[2,128,896]{2,1,0:T(8,128)(2,1)}, bf16[2,128,896]{2,1,0:T(8,128)(2,1)}, bf16[2,128,896]{2,1,0:T(8,128)(2,1)}, bf16[2,128,8...) fusion(bf16[2,128,7168]{2,1,0:T(8,128)(2,1)} %param.8, ...), kind=kLoop, calls=%fused_computation.36 | loop fusion | bytes 6422556 | tf_op jit(solution)/shard_map/dynamic_slice | solution.py:60
  40.4 1.0 collective-permute-start.6
  41.3 4.6 %collective-permute-start.4 = (bf16[2,128,896]{2,1,0:T(8,128)(2,1)}, bf16[2,128,896]{2,1,0:T(8,128)(2,1)S(1)}, u32[]{:S(2)}, u32[]{:S(2)}) collective-permute-start(bf16[2,128,896]{2,1,0:T(8,128)(2,1)} %get-tuple-element.15), channel_id=1, source_target_pairs={{0,5},{1,6},{2,7},{3,0},{4,1},{5,2},{6,3},{7,4},{8,13},{9,14},{10,... | collective-permute-start | bytes 1376264 | tf_op jit(solution)/shard_map/ppermute | solution.py:63
  45.9 2.3 %collective-permute-start.3 = (bf16[2,128,896]{2,1,0:T(8,128)(2,1)}, bf16[2,128,896]{2,1,0:T(8,128)(2,1)S(1)}, u32[]{:S(2)}, u32[]{:S(2)}) collective-permute-start(bf16[2,128,896]{2,1,0:T(8,128)(2,1)} %get-tuple-element.16), channel_id=1, source_target_pairs={{0,4},{1,5},{2,6},{3,7},{4,0},{5,1},{6,2},{7,3},{8,12},{9,13},{10,... | collective-permute-start | bytes 1376264 | tf_op jit(solution)/shard_map/ppermute | solution.py:63
  48.2 2.6 %collective-permute-start.1 = (bf16[2,128,896]{2,1,0:T(8,128)(2,1)}, bf16[2,128,896]{2,1,0:T(8,128)(2,1)S(1)}, u32[]{:S(2)}, u32[]{:S(2)}) collective-permute-start(bf16[2,128,896]{2,1,0:T(8,128)(2,1)} %get-tuple-element.18), channel_id=1, source_target_pairs={{0,2},{1,3},{2,4},{3,5},{4,6},{5,7},{6,0},{7,1},{8,10},{9,11},{10,... | collective-permute-start | bytes 1376264 | tf_op jit(solution)/shard_map/ppermute | solution.py:63
  50.8 2.8 %collective-permute-start = (bf16[2,128,896]{2,1,0:T(8,128)(2,1)}, bf16[2,128,896]{2,1,0:T(8,128)(2,1)}, u32[]{:S(2)}, u32[]{:S(2)}) collective-permute-start(bf16[2,128,896]{2,1,0:T(8,128)(2,1)} %get-tuple-element.19), channel_id=1, source_target_pairs={{0,1},{1,2},{2,3},{3,4},{4,5},{5,6},{6,7},{7,0},{8,9},{9,10},{10,1... | collective-permute-start | bytes 1376264 | tf_op jit(solution)/shard_map/ppermute | solution.py:63
  53.6 1.8 %bitcast_dynamic-update-slice_fusion.7 = bf16[8,2,128,896]{3,2,1,0:T(8,128)(2,1)} fusion(bf16[2,128,7168]{2,1,0:T(8,128)(2,1)} %param.8, s32[]{:T(128)S(6)} %select_n.103), kind=kLoop, calls=%fused_computation.18 | loop fusion | bytes 917508
  55.4 22.3 %collective-permute-done = bf16[2,128,896]{2,1,0:T(8,128)(2,1)} collective-permute-done((bf16[2,128,896]{2,1,0:T(8,128)(2,1)}, bf16[2,128,896]{2,1,0:T(8,128)(2,1)}, u32[]{:S(2)}, u32[]{:S(2)}) %collective-permute-start) | collective-permute-done | bytes 458784 | tf_op jit(solution)/shard_map/ppermute | solution.py:63
  77.8 5.8 %collective-permute-start.2 = (bf16[2,128,896]{2,1,0:T(8,128)(2,1)}, bf16[2,128,896]{2,1,0:T(8,128)(2,1)S(1)}, u32[]{:S(2)}, u32[]{:S(2)}) collective-permute-start(bf16[2,128,896]{2,1,0:T(8,128)(2,1)} %get-tuple-element.17), channel_id=1, source_target_pairs={{0,3},{1,4},{2,5},{3,6},{4,7},{5,0},{6,1},{7,2},{8,11},{9,12},{10,... | collective-permute-start | bytes 1376264 | tf_op jit(solution)/shard_map/ppermute | solution.py:63
  83.6 1.8 %bitcast_dynamic-update-slice_fusion.6 = bf16[8,2,128,896]{3,2,1,0:T(8,128)(2,1)} fusion(bf16[8,2,128,896]{3,2,1,0:T(8,128)(2,1)} %bitcast_dynamic-update-slice_fusion.7, bf16[2,128,896]{2,1,0:T(8,128)(2,1)} %collective-permute-done), kind=kLoop, calls=%fused_computation.17 | loop fusion | bytes 917504
  85.4 3.0 %collective-permute-start.5 = (bf16[2,128,896]{2,1,0:T(8,128)(2,1)}, bf16[2,128,896]{2,1,0:T(8,128)(2,1)S(1)}, u32[]{:S(2)}, u32[]{:S(2)}) collective-permute-start(bf16[2,128,896]{2,1,0:T(8,128)(2,1)} %get-tuple-element.20), channel_id=1, source_target_pairs={{0,6},{1,7},{2,0},{3,1},{4,2},{5,3},{6,4},{7,5},{8,14},{9,15},{10,... | collective-permute-start | bytes 1376264 | tf_op jit(solution)/shard_map/ppermute | solution.py:63
  88.4 0.8 bitcast_dynamic-update-slice_fusion.5
  89.3 3.9 %collective-permute-done.2 = bf16[2,128,896]{2,1,0:T(8,128)(2,1)S(1)} collective-permute-done((bf16[2,128,896]{2,1,0:T(8,128)(2,1)}, bf16[2,128,896]{2,1,0:T(8,128)(2,1)S(1)}, u32[]{:S(2)}, u32[]{:S(2)}) %collective-permute-start.2) | collective-permute-done | bytes 458784 | tf_op jit(solution)/shard_map/ppermute | solution.py:63
  93.2 0.8 bitcast_dynamic-update-slice_fusion.4
  94.0 0.8 bitcast_dynamic-update-slice_fusion.3
  94.8 0.8 bitcast_dynamic-update-slice_fusion.2
  95.6 3.6 %collective-permute-done.5 = bf16[2,128,896]{2,1,0:T(8,128)(2,1)S(1)} collective-permute-done((bf16[2,128,896]{2,1,0:T(8,128)(2,1)}, bf16[2,128,896]{2,1,0:T(8,128)(2,1)S(1)}, u32[]{:S(2)}, u32[]{:S(2)}) %collective-permute-start.5) | collective-permute-done | bytes 458784 | tf_op jit(solution)/shard_map/ppermute | solution.py:63
  99.3 0.8 bitcast_dynamic-update-slice_fusion.1
  100.1 0.8 bitcast_dynamic-update-slice_fusion
  100.9 4.9 %gather_fusion = bf16[8,2,128,896]{3,2,1,0:T(8,128)(2,1)} fusion(bf16[8,2,128,896]{3,2,1,0:T(8,128)(2,1)} %bitcast_dynamic-update-slice_fusion, s32[1024]{0:T(1024)S(1)} %pad_clamp_fusion), kind=kCustom, calls=%fused_computation | custom fusion | bytes 7340064 | tf_op jit(solution)/shard_map/jit(_take)/gather | solution.py:67
  105.8 2.5 %select_bitcast_fusion = bf16[2,8,128,896]{3,2,0,1:T(8,128)(2,1)S(1)} fusion(bf16[8,2,128,896]{3,2,1,0:T(8,128)(2,1)} %gather_fusion, pred[8]{0:T(512)(128)(4,1)S(1)} %compare_and_fusion), kind=kLoop, calls=%fused_computation.2 | loop fusion | flops 1835008 | bytes 7340040 | tf_op jit(solution)/shard_map/jit(_take)/select_n | solution.py:67
  108.2 2.2 %copy.86 = bf16[2,8,128,896]{3,2,1,0:T(8,128)(2,1)} copy(bf16[2,8,128,896]{3,2,0,1:T(8,128)(2,1)S(1)} %select_bitcast_fusion) | data formatting | bytes 7340032 | tf_op jit(solution)/shard_map/jit(_take)/select_n | solution.py:67
  110.5 0.9 slice.11
  111.4 1.8 reshape.110
  113.2 9.6 %multiply_reduce_fusion = (f32[2,768]{1,0:T(2,128)S(1)}, f32[2,768,1024]{1,2,0:T(8,128)}) fusion(bf16[2,768,1024]{1,2,0:T(8,128)(2,1)} %all-gather.2.cloned.1.call-done, bf16[2,1024,896]{2,1,0:T(8,128)(2,1)} %bitcast.42, bf16[768,896,1]{1,0,2:T(8,128)(2,1)} %reshape.110), kind=kOutput, calls=%fused_computation.1 | convolution fusion | flops 2823289344 | bytes 14489600 | tf_op jit(solution)/shard_map/rd,ehd->erh/dot_general | solution.py:69
  122.8 0.0 reduce-scatter.2.cloned.1.call-update
  122.8 0.1 all_gather_reshape.3
  122.9 0.1 copy.88
  123.0 12.5 %all_gather.7 = f32[8,64,12,2]{1,3,2,0:T(2,128)S(1)} all-gather(f32[1,64,12,2]{1,3,2,0:T(2,128)S(1)} %copy.88), channel_id=1, replica_groups=mesh['node'=64,'local'=8] {'local'}, dimensions={0}, use_global_device_ids=true | all-gather | bytes 55296 | tf_op jit(solution)/shard_map/all_gather | solution.py:78
  135.5 0.1 reduce_sum.29
  135.5 0.7 copy.90
  136.3 15.0 %all-to-all-start.1 = ((f32[64,12,2]{1,2,0:T(2,128)}), f32[64,12,2]{1,2,0:T(2,128)S(1)}, u32[]{:S(2)}, u32[]{:S(2)}) async-start(f32[64,12,2]{1,2,0:T(2,128)} %copy.90), calls=%async_computation.2 | async-start | bytes 131072 | tf_op jit(solution)/shard_map/all_to_all | solution.py:82
  151.3 0.2 reshape.100
  151.6 0.1 copy.85
  151.7 13.8 %all-to-all-done.1 = f32[64,12,2]{1,2,0:T(2,128)S(1)} async-done(((f32[64,12,2]{1,2,0:T(2,128)}), f32[64,12,2]{1,2,0:T(2,128)S(1)}, u32[]{:S(2)}, u32[]{:S(2)}) %all-to-all-start.1) | async-done | bytes 6176 | tf_op jit(solution)/shard_map/all_to_all | solution.py:82
  165.5 0.4 convolution_bitcast_fusion.1
  165.9 0.1 copy.91
  166.0 0.6 fusion.2
  166.7 0.7 copy.92
  167.4 5.6 %reduce-scatter.2.cloned.1.call-done = f32[2,768,128]{1,2,0:T(8,128)} async-done(((f32[2,768,1024]{1,2,0:T(8,128)}), f32[2,768,128]{1,2,0:T(8,128)}) %reduce-scatter.2.cloned.1.call-update) | async-done | bytes 786448 | tf_op jit(solution)/shard_map/reduce_scatter | solution.py:79
  172.9 1.2 multiply_convert_fusion
  174.1 0.9 copy.93
  (18 shorter events, 0.1 us)
Async XLA Ops:
  7.2 5.7 %copy-start = (bf16[128,896]{1,0:T(8,128)(2,1)S(1)}, bf16[128,896]{1,0:T(8,128)(2,1)}, u32[]{:S(2)}) copy-start(bf16[128,896]{1,0:T(8,128)(2,1)} %param.5) | copy-start | bytes 688132
  7.2 106.0 %all-gather.2.cloned.1.call-start = ((), (), s32[]{:S(2)}) async-start(), calls=%async_computation.4 | async-start | bytes 3538944 | tf_op jit(solution)/shard_map/all_gather | solution.py:75
  10.6 2.1 %copy-start.1 = (s32[128,64]{0,1:T(8,128)}, s32[128,64]{0,1:T(8,128)S(1)}, u32[]{:S(2)}) copy-start(s32[128,64]{0,1:T(8,128)S(1)} %copy.77) | copy-start | bytes 98308
  17.4 93.1 %all-to-all-start = ((bf16[64,2,5388]{2,1,0:T(2,128)(2,1)}), bf16[64,2,5388]{2,1,0:T(2,128)(2,1)S(1)}, u32[]{:S(2)}, u32[]{:S(2)}) async-start(bf16[64,2,5388]{2,1,0:T(2,128)(2,1)} %pad_maximum_fusion), calls=%async_computation | async-start | bytes 2818048 | tf_op jit(solution)/shard_map/all_to_all | solution.py:52
  36.5 136.4 %reduce-scatter.2.cloned.1.call-start = ((), (), s32[]{:S(2)}) async-start(), calls=%async_computation.3 | async-start | bytes 7077888 | tf_op jit(solution)/shard_map/reduce_scatter | solution.py:79
  40.4 59.7 %collective-permute-start.6 = (bf16[2,128,896]{2,1,0:T(8,128)(2,1)}, bf16[2,128,896]{2,1,0:T(8,128)(2,1)S(1)}, u32[]{:S(2)}, u32[]{:S(2)}) collective-permute-start(bf16[2,128,896]{2,1,0:T(8,128)(2,1)} %get-tuple-element.14), channel_id=1, source_target_pairs={{0,7},{1,0},{2,1},{3,2},{4,3},{5,4},{6,5},{7,6},{8,15},{9,8},{10,9... | collective-permute-start | bytes 1376264 | tf_op jit(solution)/shard_map/ppermute | solution.py:63
  41.3 53.5 %collective-permute-start.4 = (bf16[2,128,896]{2,1,0:T(8,128)(2,1)}, bf16[2,128,896]{2,1,0:T(8,128)(2,1)S(1)}, u32[]{:S(2)}, u32[]{:S(2)}) collective-permute-start(bf16[2,128,896]{2,1,0:T(8,128)(2,1)} %get-tuple-element.15), channel_id=1, source_target_pairs={{0,5},{1,6},{2,7},{3,0},{4,1},{5,2},{6,3},{7,4},{8,13},{9,14},{10,... | collective-permute-start | bytes 1376264 | tf_op jit(solution)/shard_map/ppermute | solution.py:63
  45.9 48.1 %collective-permute-start.3 = (bf16[2,128,896]{2,1,0:T(8,128)(2,1)}, bf16[2,128,896]{2,1,0:T(8,128)(2,1)S(1)}, u32[]{:S(2)}, u32[]{:S(2)}) collective-permute-start(bf16[2,128,896]{2,1,0:T(8,128)(2,1)} %get-tuple-element.16), channel_id=1, source_target_pairs={{0,4},{1,5},{2,6},{3,7},{4,0},{5,1},{6,2},{7,3},{8,12},{9,13},{10,... | collective-permute-start | bytes 1376264 | tf_op jit(solution)/shard_map/ppermute | solution.py:63
  48.2 37.3 %collective-permute-start.1 = (bf16[2,128,896]{2,1,0:T(8,128)(2,1)}, bf16[2,128,896]{2,1,0:T(8,128)(2,1)S(1)}, u32[]{:S(2)}, u32[]{:S(2)}) collective-permute-start(bf16[2,128,896]{2,1,0:T(8,128)(2,1)} %get-tuple-element.18), channel_id=1, source_target_pairs={{0,2},{1,3},{2,4},{3,5},{4,6},{5,7},{6,0},{7,1},{8,10},{9,11},{10,... | collective-permute-start | bytes 1376264 | tf_op jit(solution)/shard_map/ppermute | solution.py:63
  50.8 27.0 %collective-permute-start = (bf16[2,128,896]{2,1,0:T(8,128)(2,1)}, bf16[2,128,896]{2,1,0:T(8,128)(2,1)}, u32[]{:S(2)}, u32[]{:S(2)}) collective-permute-start(bf16[2,128,896]{2,1,0:T(8,128)(2,1)} %get-tuple-element.19), channel_id=1, source_target_pairs={{0,1},{1,2},{2,3},{3,4},{4,5},{5,6},{6,7},{7,0},{8,9},{9,10},{10,1... | collective-permute-start | bytes 1376264 | tf_op jit(solution)/shard_map/ppermute | solution.py:63
  77.8 15.4 %collective-permute-start.2 = (bf16[2,128,896]{2,1,0:T(8,128)(2,1)}, bf16[2,128,896]{2,1,0:T(8,128)(2,1)S(1)}, u32[]{:S(2)}, u32[]{:S(2)}) collective-permute-start(bf16[2,128,896]{2,1,0:T(8,128)(2,1)} %get-tuple-element.17), channel_id=1, source_target_pairs={{0,3},{1,4},{2,5},{3,6},{4,7},{5,0},{6,1},{7,2},{8,11},{9,12},{10,... | collective-permute-start | bytes 1376264 | tf_op jit(solution)/shard_map/ppermute | solution.py:63
  85.4 13.8 %collective-permute-start.5 = (bf16[2,128,896]{2,1,0:T(8,128)(2,1)}, bf16[2,128,896]{2,1,0:T(8,128)(2,1)S(1)}, u32[]{:S(2)}, u32[]{:S(2)}) collective-permute-start(bf16[2,128,896]{2,1,0:T(8,128)(2,1)} %get-tuple-element.20), channel_id=1, source_target_pairs={{0,6},{1,7},{2,0},{3,1},{4,2},{5,3},{6,4},{7,5},{8,14},{9,15},{10,... | collective-permute-start | bytes 1376264 | tf_op jit(solution)/shard_map/ppermute | solution.py:63
  122.8 42.7 %copy-start.2 = (s32[128,64]{0,1:T(8,128)S(1)}, s32[128,64]{0,1:T(8,128)}, u32[]{:S(2)}) copy-start(s32[128,64]{0,1:T(8,128)} %copy-done.1) | copy-start | bytes 98308
  136.3 29.2 %all-to-all-start.1 = ((f32[64,12,2]{1,2,0:T(2,128)}), f32[64,12,2]{1,2,0:T(2,128)S(1)}, u32[]{:S(2)}, u32[]{:S(2)}) async-start(f32[64,12,2]{1,2,0:T(2,128)} %copy.90), calls=%async_computation.2 | async-start | bytes 131072 | tf_op jit(solution)/shard_map/all_to_all | solution.py:82
Sparse Core Ops, SparseCore 0:
  10.7 43.9 all-gather.1
  122.9 49.9 reduce-scatter.1

commit v14 on v13

--- a/solution.py
+++ b/solution.py
@@ -54,18 +54,17 @@
     prob_in = payload_in[:, :, per_half * width :]
     local_count = lax.axis_size("local")
     local_index = lax.axis_index("local")
-    pieces = []
+    hidden_local = weight_down.shape[1]
+    weight_buffer = jnp.zeros((expert_count, local_count, hidden_local, width), weight_down.dtype)
     for step in range(local_count):
         target = (local_index + step) % local_count
         piece = lax.dynamic_slice_in_dim(weight_down, target * width, width, axis=2)
         if step:
             pairs = [(j, (j + step) % local_count) for j in range(local_count)]
             piece = lax.ppermute(piece, "local", perm=pairs)
-        pieces.append(piece)
-    stacked = jnp.stack(pieces, axis=0)
-    block_order = (local_index - jnp.arange(local_count, dtype=jnp.int32)) % local_count
-    weight_blocks = jnp.take(stacked, block_order, axis=0)
-    weight_cols = jnp.transpose(weight_blocks, (1, 0, 2, 3)).reshape(expert_count, -1, width)
+        block = (local_index - step) % local_count
+        weight_buffer = lax.dynamic_update_slice(weight_buffer, piece[:, None], (0, block, 0, 0))
+    weight_cols = weight_buffer.reshape(expert_count, -1, width)
     partial_grads = jnp.einsum(
         "rd,ehd->erh",
         rows_in,

time: 183 us -> 171 us (0.934)
  starting transfers between devices: 56.2 us -> 44.4 us
  local copies, waits for them, and re-layouts: 30.8 us -> 22.5 us
  waiting for transfers between devices: 49.2 us -> 54.7 us
  blocking collectives: 12.5 us -> 17.8 us
  other arithmetic: 6.72 us -> 4.23 us
    all_to_all x1, starting transfers between devices: 15 us -> 5.54 us  [on_device(): lax.all_to_all(summed, 'node', split_axis=0, concat_axis=0, tiled=True)]
    unnamed x16 -> x13, local copies, waits for them, and re-layouts: 11.5 us -> 3.71 us
    all_to_all x1, waiting for transfers between devices: 0.01 us -> 7.09 us  [on_device(): lax.all_to_all(payload, 'node', split_axis=0, concat_axis=0, tiled=True)]
    dynamic_update_slice x0 -> x9, local copies, waits for them, and re-layouts: none -> 7.02 us  [on_device(): lax.dynamic_update_slice(weight_buffer, piece[:, None], (0, block, 0, 0))]
    all_gather x1, blocking collectives: 12.5 us -> 17.8 us  [on_device(): lax.all_gather(partial_value, 'local', axis=0, tiled=False)]
    gather x1 -> x0, local copies, waits for them, and re-layouts: 4.87 us -> none  [on_device(): weight_blocks = jnp.take(stacked, block_order, axis=0)]
    select_n x2 -> x0, other arithmetic: 2.48 us -> none  [on_device(): weight_blocks = jnp.take(stacked, block_order, axis=0)]
    ppermute x7, starting transfers between devices: 22 us -> 19.7 us  [on_device(): piece = lax.ppermute(piece, 'local', perm=pairs)]
  transfers between devices with their start and end apart: 11 -> 11, of which waited for: 5 -> 7; matrix products, arithmetic and copies ran while one was open for 20% -> 15% of each run, Pallas kernels for 0% -> 0%
where the time goes in v14:
time: 171 us; the launch traced here: 170 us
  waiting for transfers between devices  54.7 us (32%)
  starting transfers between devices  44.4 us (26%)
  local copies, waits for them, and re-layouts  22.5 us (13%)
  blocking collectives  17.8 us (10%)
  between operations  14.6 us (9%)
  matrix products  12 us (7%)
  other arithmetic  4.23 us (2%)
    ppermute x7, waiting for transfers between devices, on_device(): piece = lax.ppermute(piece, 'local', perm=pairs)  28.6 us
    ppermute x7, starting transfers between devices, on_device(): piece = lax.ppermute(piece, 'local', perm=pairs)  19.7 us
    all_to_all x1, starting transfers between devices, on_device(): lax.all_to_all(payload, 'node', split_axis=0, concat_axis=0, tiled=True)  19.1 us
    all_gather x1, blocking collectives, on_device(): lax.all_gather(partial_value, 'local', axis=0, tiled=False)  17.8 us
    all_to_all x1, waiting for transfers between devices, on_device(): lax.all_to_all(summed, 'node', split_axis=0, concat_axis=0, tiled=True)  13.8 us
    dot_general x1, matrix products, on_device(): jnp.einsum('rd,ehd->erh', rows_in, weight_cols, preferred_element_type=jn...  9.56 us
    all_to_all x1, waiting for transfers between devices, on_device(): lax.all_to_all(payload, 'node', split_axis=0, concat_axis=0, tiled=True)  7.09 us
    dynamic_update_slice x9, local copies, waits for them, and re-layouts, on_device(): lax.dynamic_update_slice(weight_buffer, piece[:, None], (0, block, 0, 0))  7.02 us
  transfers between devices with their start and end apart: 11, of which 7 were waited for; matrix products, arithmetic and copies ran while one was open for 15% of the time, Pallas kernels for 0%

profile of v14, /device:TPU:1, one launch (start us, length us, event | category | flops | bytes accessed | tf_op | source)
XLA Modules:
  0.0 170.3 jit_solution(16850399592990489366)
XLA Ops:
  7.2 0.0 all-gather.2.cloned.1.call-start
  7.2 2.0 %copy.89 = bf16[2,768,128]{1,2,0:T(8,128)(2,1)} copy(bf16[2,768,128]{2,1,0:T(8,128)(2,1)} %param.9) | data formatting | bytes 786432 | tf_op args[4]
  9.2 0.0 all-gather.2.cloned.1.call-update
  9.2 0.8 copy.75
  10.0 0.3 convert_reduce_fusion
  10.3 0.1 copy.77
  10.4 0.2 reduce_window_sum.11
  10.6 0.1 copy.76
  10.6 0.0 copy-start.3
  10.6 0.8 copy.80
  11.5 0.3 fusion.3
  11.8 0.1 copy.81
  11.9 0.1 fusion
  12.1 0.5 convolution_convert_fusion.1
  12.6 0.1 copy.82
  12.7 0.1 copy.83
  12.9 0.5 convolution_convert_fusion
  13.4 0.8 copy.79
  14.2 0.8 reshape.40
  15.0 2.4 %pad_maximum_fusion = bf16[64,2,5388]{2,1,0:T(2,128)(2,1)} fusion(bf16[64,2,12]{2,1,0:T(2,128)(2,1)S(1)} %copy.83, bf16[64,2,5376]{2,1,0:T(2,128)(2,1)S(1)} %reshape.40), kind=kLoop, calls=%fused_computation.3 | loop fusion | flops 2758656 | bytes 2758656 | tf_op jit(solution)/shard_map/concatenate | solution.py:45
  17.4 19.1 %all-to-all-start = ((bf16[64,2,5388]{2,1,0:T(2,128)(2,1)}), bf16[64,2,5388]{2,1,0:T(2,128)(2,1)S(1)}, u32[]{:S(2)}, u32[]{:S(2)}) async-start(bf16[64,2,5388]{2,1,0:T(2,128)(2,1)} %pad_maximum_fusion), calls=%async_computation | async-start | bytes 2818048 | tf_op jit(solution)/shard_map/all_to_all | solution.py:52
  36.5 0.0 reduce-scatter.2.cloned.1.call-start
  36.7 3.6 %constant_dynamic-slice_fusion = (bf16[2,128,896]{2,1,0:T(8,128)(2,1)}, bf16[2,128,896]{2,1,0:T(8,128)(2,1)}, bf16[2,128,896]{2,1,0:T(8,128)(2,1)}, bf16[2,128,8...) fusion(bf16[2,128,7168]{2,1,0:T(8,128)(2,1)} %param.8, ...), kind=kLoop, calls=%fused_computation.27 | loop fusion | bytes 6422556 | tf_op jit(solution)/shard_map/dynamic_slice | solution.py:61
  40.3 2.2 %collective-permute-start = (bf16[2,128,896]{2,1,0:T(8,128)(2,1)}, bf16[2,128,896]{2,1,0:T(8,128)(2,1)}, u32[]{:S(2)}, u32[]{:S(2)}) collective-permute-start(bf16[2,128,896]{2,1,0:T(8,128)(2,1)} %get-tuple-element.17), channel_id=1, source_target_pairs={{0,1},{1,2},{2,3},{3,4},{4,5},{5,6},{6,7},{7,0},{8,9},{9,10},{10,1... | collective-permute-start | bytes 1376264 | tf_op jit(solution)/shard_map/ppermute | solution.py:64
  42.5 3.2 %collective-permute-start.1 = (bf16[2,128,896]{2,1,0:T(8,128)(2,1)}, bf16[2,128,896]{2,1,0:T(8,128)(2,1)S(1)}, u32[]{:S(2)}, u32[]{:S(2)}) collective-permute-start(bf16[2,128,896]{2,1,0:T(8,128)(2,1)} %get-tuple-element.16), channel_id=1, source_target_pairs={{0,2},{1,3},{2,4},{3,5},{4,6},{5,7},{6,0},{7,1},{8,10},{9,11},{10,... | collective-permute-start | bytes 1376264 | tf_op jit(solution)/shard_map/ppermute | solution.py:64
  45.7 0.0 collective-permute-start.6
  45.7 3.8 %collective-permute-start.4 = (bf16[2,128,896]{2,1,0:T(8,128)(2,1)}, bf16[2,128,896]{2,1,0:T(8,128)(2,1)S(1)}, u32[]{:S(2)}, u32[]{:S(2)}) collective-permute-start(bf16[2,128,896]{2,1,0:T(8,128)(2,1)} %get-tuple-element.13), channel_id=1, source_target_pairs={{0,5},{1,6},{2,7},{3,0},{4,1},{5,2},{6,3},{7,4},{8,13},{9,14},{10,... | collective-permute-start | bytes 1376264 | tf_op jit(solution)/shard_map/ppermute | solution.py:64
  49.5 3.6 %collective-permute-start.3 = (bf16[2,128,896]{2,1,0:T(8,128)(2,1)}, bf16[2,128,896]{2,1,0:T(8,128)(2,1)S(1)}, u32[]{:S(2)}, u32[]{:S(2)}) collective-permute-start(bf16[2,128,896]{2,1,0:T(8,128)(2,1)} %get-tuple-element.14), channel_id=1, source_target_pairs={{0,4},{1,5},{2,6},{3,7},{4,0},{5,1},{6,2},{7,3},{8,12},{9,13},{10,... | collective-permute-start | bytes 1376264 | tf_op jit(solution)/shard_map/ppermute | solution.py:64
  53.3 0.5 broadcast_in_dim.32
  53.8 1.1 bitcast_dynamic-update-slice_fusion.7
  54.8 2.3 %collective-permute-done = bf16[2,128,896]{2,1,0:T(8,128)(2,1)} collective-permute-done((bf16[2,128,896]{2,1,0:T(8,128)(2,1)}, bf16[2,128,896]{2,1,0:T(8,128)(2,1)}, u32[]{:S(2)}, u32[]{:S(2)}) %collective-permute-start) | collective-permute-done | bytes 458784 | tf_op jit(solution)/shard_map/ppermute | solution.py:64
  57.2 4.8 %collective-permute-start.2 = (bf16[2,128,896]{2,1,0:T(8,128)(2,1)S(1)}, bf16[2,128,896]{2,1,0:T(8,128)(2,1)S(1)}, u32[]{:S(2)}, u32[]{:S(2)}) collective-permute-start(bf16[2,128,896]{2,1,0:T(8,128)(2,1)S(1)} %copy-done.2), channel_id=1, source_target_pairs={{0,3},{1,4},{2,5},{3,6},{4,7},{5,0},{6,1},{7,2},{8,11},{9,12},{10,... | collective-permute-start | bytes 1376264 | tf_op jit(solution)/shard_map/ppermute | solution.py:64
  62.0 1.1 bitcast_dynamic-update-slice_fusion.6
  63.0 22.2 %collective-permute-done.1 = bf16[2,128,896]{2,1,0:T(8,128)(2,1)S(1)} collective-permute-done((bf16[2,128,896]{2,1,0:T(8,128)(2,1)}, bf16[2,128,896]{2,1,0:T(8,128)(2,1)S(1)}, u32[]{:S(2)}, u32[]{:S(2)}) %collective-permute-start.1) | collective-permute-done | bytes 458784 | tf_op jit(solution)/shard_map/ppermute | solution.py:64
  85.2 2.1 %collective-permute-start.5 = (bf16[2,128,896]{2,1,0:T(8,128)(2,1)S(1)}, bf16[2,128,896]{2,1,0:T(8,128)(2,1)S(1)}, u32[]{:S(2)}, u32[]{:S(2)}) collective-permute-start(bf16[2,128,896]{2,1,0:T(8,128)(2,1)S(1)} %copy-done.1), channel_id=1, source_target_pairs={{0,6},{1,7},{2,0},{3,1},{4,2},{5,3},{6,4},{7,5},{8,14},{9,15},{10,... | collective-permute-start | bytes 1376264 | tf_op jit(solution)/shard_map/ppermute | solution.py:64
  87.3 0.1 bitcast_dynamic-update-slice_fusion.5
  87.4 2.1 %collective-permute-done.2 = bf16[2,128,896]{2,1,0:T(8,128)(2,1)S(1)} collective-permute-done((bf16[2,128,896]{2,1,0:T(8,128)(2,1)S(1)}, bf16[2,128,896]{2,1,0:T(8,128)(2,1)S(1)}, u32[]{:S(2)}, u32[]{:S(2)}) %collective-permute-start.2) | collective-permute-done | bytes 458784 | tf_op jit(solution)/shard_map/ppermute | solution.py:64
  89.6 0.1 bitcast_dynamic-update-slice_fusion.3
  89.6 2.2 %copy.85 = bf16[2,8,128,896]{3,2,1,0:T(8,128)(2,1)} copy(bf16[2,8,128,896]{3,2,0,1:T(8,128)(2,1)S(1)} %bitcast_dynamic-update-slice_fusion.3) | data formatting | bytes 7340032 | tf_op jit(solution)/shard_map/dynamic_update_slice | solution.py:66
  91.8 0.8 bitcast_dynamic-update-slice_fusion.2
  92.7 2.0 %collective-permute-done.5 = bf16[2,128,896]{2,1,0:T(8,128)(2,1)S(1)} collective-permute-done((bf16[2,128,896]{2,1,0:T(8,128)(2,1)S(1)}, bf16[2,128,896]{2,1,0:T(8,128)(2,1)S(1)}, u32[]{:S(2)}, u32[]{:S(2)}) %collective-permute-start.5) | collective-permute-done | bytes 458784 | tf_op jit(solution)/shard_map/ppermute | solution.py:64
  94.7 0.8 bitcast_dynamic-update-slice_fusion.1
  95.5 0.9 bitcast_dynamic-update-slice_fusion
  96.4 7.1 %all-to-all-done = bf16[64,2,5388]{2,1,0:T(2,128)(2,1)S(1)} async-done(((bf16[64,2,5388]{2,1,0:T(2,128)(2,1)}), bf16[64,2,5388]{2,1,0:T(2,128)(2,1)S(1)}, u32[]{:S(2)}, u32[]{:S(2)}) %all-to-all-start) | async-done | bytes 1379360 | tf_op jit(solution)/shard_map/all_to_all | solution.py:52
  103.5 0.9 slice.9
  104.4 1.8 %reshape.48 = bf16[768,896,1]{1,0,2:T(8,128)(2,1)} reshape(bf16[64,2,5376]{2,1,0:T(2,128)(2,1)S(1)} %slice.9) | data formatting | bytes 2752512 | tf_op jit(solution)/shard_map/reshape | solution.py:53
  106.2 9.6 %multiply_reduce_fusion = (f32[2,768]{1,0:T(2,128)S(1)}, f32[2,768,1024]{1,2,0:T(8,128)}) fusion(bf16[2,768,1024]{1,2,0:T(8,128)(2,1)} %all-gather.2.cloned.1.call-done, bf16[2,1024,896]{2,1,0:T(8,128)(2,1)} %bitcast.14, bf16[768,896,1]{1,0,2:T(8,128)(2,1)} %reshape.48), kind=kOutput, calls=%fused_computation | convolution fusion | flops 2823289344 | bytes 14489600 | tf_op jit(solution)/shard_map/rd,ehd->erh/dot_general | solution.py:68
  115.7 0.0 reduce-scatter.2.cloned.1.call-update
  115.8 0.1 all_gather_reshape.3
  115.9 0.1 copy.90
  116.0 17.8 %all_gather.7 = f32[8,64,12,2]{1,3,2,0:T(2,128)S(1)} all-gather(f32[1,64,12,2]{1,3,2,0:T(2,128)S(1)} %copy.90), channel_id=1, replica_groups=mesh['node'=64,'local'=8] {'local'}, dimensions={0}, use_global_device_ids=true | all-gather | bytes 55296 | tf_op jit(solution)/shard_map/all_gather | solution.py:77
  133.8 0.1 reduce_sum.29
  133.8 0.7 copy.92
  134.6 5.5 %all-to-all-start.1 = ((f32[64,12,2]{1,2,0:T(2,128)}), f32[64,12,2]{1,2,0:T(2,128)S(1)}, u32[]{:S(2)}, u32[]{:S(2)}) async-start(f32[64,12,2]{1,2,0:T(2,128)} %copy.92), calls=%async_computation.2 | async-start | bytes 131072 | tf_op jit(solution)/shard_map/all_to_all | solution.py:81
  140.2 0.2 reshape.46
  140.4 0.1 copy.84
  140.5 13.8 %all-to-all-done.1 = f32[64,12,2]{1,2,0:T(2,128)S(1)} async-done(((f32[64,12,2]{1,2,0:T(2,128)}), f32[64,12,2]{1,2,0:T(2,128)S(1)}, u32[]{:S(2)}, u32[]{:S(2)}) %all-to-all-start.1) | async-done | bytes 6176 | tf_op jit(solution)/shard_map/all_to_all | solution.py:81
  154.3 0.4 convolution_bitcast_fusion.1
  154.7 0.1 copy.93
  154.8 0.6 fusion.2
  155.5 0.7 copy.94
  156.2 5.2 %reduce-scatter.2.cloned.1.call-done = f32[2,768,128]{1,2,0:T(8,128)} async-done(((f32[2,768,1024]{1,2,0:T(8,128)}), f32[2,768,128]{1,2,0:T(8,128)}) %reduce-scatter.2.cloned.1.call-update) | async-done | bytes 786448 | tf_op jit(solution)/shard_map/reduce_scatter | solution.py:78
  161.4 1.2 multiply_convert_fusion
  162.6 0.9 copy.95
  (18 shorter events, 0.2 us)
Async XLA Ops:
  7.2 5.7 %copy-start = (bf16[128,896]{1,0:T(8,128)(2,1)S(1)}, bf16[128,896]{1,0:T(8,128)(2,1)}, u32[]{:S(2)}) copy-start(bf16[128,896]{1,0:T(8,128)(2,1)} %param.5) | copy-start | bytes 688132
  7.2 99.0 %all-gather.2.cloned.1.call-start = ((), (), s32[]{:S(2)}) async-start(), calls=%async_computation.4 | async-start | bytes 3538944 | tf_op jit(solution)/shard_map/all_gather | solution.py:74
  10.6 2.1 %copy-start.3 = (s32[128,64]{0,1:T(8,128)}, s32[128,64]{0,1:T(8,128)S(1)}, u32[]{:S(2)}) copy-start(s32[128,64]{0,1:T(8,128)S(1)} %copy.76) | copy-start | bytes 98308
  17.4 86.1 %all-to-all-start = ((bf16[64,2,5388]{2,1,0:T(2,128)(2,1)}), bf16[64,2,5388]{2,1,0:T(2,128)(2,1)S(1)}, u32[]{:S(2)}, u32[]{:S(2)}) async-start(bf16[64,2,5388]{2,1,0:T(2,128)(2,1)} %pad_maximum_fusion), calls=%async_computation | async-start | bytes 2818048 | tf_op jit(solution)/shard_map/all_to_all | solution.py:52
  36.5 124.9 %reduce-scatter.2.cloned.1.call-start = ((), (), s32[]{:S(2)}) async-start(), calls=%async_computation.3 | async-start | bytes 7077888 | tf_op jit(solution)/shard_map/reduce_scatter | solution.py:78
  40.3 16.9 %collective-permute-start = (bf16[2,128,896]{2,1,0:T(8,128)(2,1)}, bf16[2,128,896]{2,1,0:T(8,128)(2,1)}, u32[]{:S(2)}, u32[]{:S(2)}) collective-permute-start(bf16[2,128,896]{2,1,0:T(8,128)(2,1)} %get-tuple-element.17), channel_id=1, source_target_pairs={{0,1},{1,2},{2,3},{3,4},{4,5},{5,6},{6,7},{7,0},{8,9},{9,10},{10,1... | collective-permute-start | bytes 1376264 | tf_op jit(solution)/shard_map/ppermute | solution.py:64
  42.5 42.7 %collective-permute-start.1 = (bf16[2,128,896]{2,1,0:T(8,128)(2,1)}, bf16[2,128,896]{2,1,0:T(8,128)(2,1)S(1)}, u32[]{:S(2)}, u32[]{:S(2)}) collective-permute-start(bf16[2,128,896]{2,1,0:T(8,128)(2,1)} %get-tuple-element.16), channel_id=1, source_target_pairs={{0,2},{1,3},{2,4},{3,5},{4,6},{5,7},{6,0},{7,1},{8,10},{9,11},{10,... | collective-permute-start | bytes 1376264 | tf_op jit(solution)/shard_map/ppermute | solution.py:64
  45.7 49.8 %collective-permute-start.6 = (bf16[2,128,896]{2,1,0:T(8,128)(2,1)}, bf16[2,128,896]{2,1,0:T(8,128)(2,1)S(1)}, u32[]{:S(2)}, u32[]{:S(2)}) collective-permute-start(bf16[2,128,896]{2,1,0:T(8,128)(2,1)} %get-tuple-element.12), channel_id=1, source_target_pairs={{0,7},{1,0},{2,1},{3,2},{4,3},{5,4},{6,5},{7,6},{8,15},{9,8},{10,9... | collective-permute-start | bytes 1376264 | tf_op jit(solution)/shard_map/ppermute | solution.py:64
  45.7 46.1 %collective-permute-start.4 = (bf16[2,128,896]{2,1,0:T(8,128)(2,1)}, bf16[2,128,896]{2,1,0:T(8,128)(2,1)S(1)}, u32[]{:S(2)}, u32[]{:S(2)}) collective-permute-start(bf16[2,128,896]{2,1,0:T(8,128)(2,1)} %get-tuple-element.13), channel_id=1, source_target_pairs={{0,5},{1,6},{2,7},{3,0},{4,1},{5,2},{6,3},{7,4},{8,13},{9,14},{10,... | collective-permute-start | bytes 1376264 | tf_op jit(solution)/shard_map/ppermute | solution.py:64
  49.5 40.0 %collective-permute-start.3 = (bf16[2,128,896]{2,1,0:T(8,128)(2,1)}, bf16[2,128,896]{2,1,0:T(8,128)(2,1)S(1)}, u32[]{:S(2)}, u32[]{:S(2)}) collective-permute-start(bf16[2,128,896]{2,1,0:T(8,128)(2,1)} %get-tuple-element.14), channel_id=1, source_target_pairs={{0,4},{1,5},{2,6},{3,7},{4,0},{5,1},{6,2},{7,3},{8,12},{9,13},{10,... | collective-permute-start | bytes 1376264 | tf_op jit(solution)/shard_map/ppermute | solution.py:64
  53.2 3.9 %copy-start.2 = (bf16[2,128,896]{2,1,0:T(8,128)(2,1)S(1)}, bf16[2,128,896]{2,1,0:T(8,128)(2,1)}, u32[]{:S(2)}) copy-start(bf16[2,128,896]{2,1,0:T(8,128)(2,1)} %get-tuple-element.15) | copy-start | bytes 1376260
  53.2 32.0 %copy-start.1 = (bf16[2,128,896]{2,1,0:T(8,128)(2,1)S(1)}, bf16[2,128,896]{2,1,0:T(8,128)(2,1)}, u32[]{:S(2)}) copy-start(bf16[2,128,896]{2,1,0:T(8,128)(2,1)} %get-tuple-element.18) | copy-start | bytes 1376260
  57.2 32.3 %collective-permute-start.2 = (bf16[2,128,896]{2,1,0:T(8,128)(2,1)S(1)}, bf16[2,128,896]{2,1,0:T(8,128)(2,1)S(1)}, u32[]{:S(2)}, u32[]{:S(2)}) collective-permute-start(bf16[2,128,896]{2,1,0:T(8,128)(2,1)S(1)} %copy-done.2), channel_id=1, source_target_pairs={{0,3},{1,4},{2,5},{3,6},{4,7},{5,0},{6,1},{7,2},{8,11},{9,12},{10,... | collective-permute-start | bytes 1376264 | tf_op jit(solution)/shard_map/ppermute | solution.py:64
  85.2 9.5 %collective-permute-start.5 = (bf16[2,128,896]{2,1,0:T(8,128)(2,1)S(1)}, bf16[2,128,896]{2,1,0:T(8,128)(2,1)S(1)}, u32[]{:S(2)}, u32[]{:S(2)}) collective-permute-start(bf16[2,128,896]{2,1,0:T(8,128)(2,1)S(1)} %copy-done.1), channel_id=1, source_target_pairs={{0,6},{1,7},{2,0},{3,1},{4,2},{5,3},{6,4},{7,5},{8,14},{9,15},{10,... | collective-permute-start | bytes 1376264 | tf_op jit(solution)/shard_map/ppermute | solution.py:64
  115.7 38.6 %copy-start.4 = (s32[128,64]{0,1:T(8,128)S(1)}, s32[128,64]{0,1:T(8,128)}, u32[]{:S(2)}) copy-start(s32[128,64]{0,1:T(8,128)} %copy-done.3) | copy-start | bytes 98308
  134.6 19.7 %all-to-all-start.1 = ((f32[64,12,2]{1,2,0:T(2,128)}), f32[64,12,2]{1,2,0:T(2,128)S(1)}, u32[]{:S(2)}, u32[]{:S(2)}) async-start(f32[64,12,2]{1,2,0:T(2,128)} %copy.92), calls=%async_computation.2 | async-start | bytes 131072 | tf_op jit(solution)/shard_map/all_to_all | solution.py:81
Sparse Core Ops, SparseCore 0:
  10.7 45.5 all-gather.1
  115.9 45.4 reduce-scatter.1

commit v15 on v14

--- a/solution.py
+++ b/solution.py
@@ -62,6 +62,8 @@
         if step:
             pairs = [(j, (j + step) % local_count) for j in range(local_count)]
             piece = lax.ppermute(piece, "local", perm=pairs)
+            if step == 1:
+                piece, saved_late = lax.optimization_barrier((piece, saved_hidden))
         block = (local_index - step) % local_count
         weight_buffer = lax.dynamic_update_slice(weight_buffer, piece[:, None], (0, block, 0, 0))
     weight_cols = weight_buffer.reshape(expert_count, -1, width)
@@ -71,7 +73,7 @@
         weight_cols,
         preferred_element_type=jnp.float32,
     )
-    saved_full = lax.all_gather(saved_hidden, "local", axis=2, tiled=True)
+    saved_full = lax.all_gather(saved_late, "local", axis=2, tiled=True)
     partial_scores = jnp.sum(saved_full.astype(jnp.float32) * partial_grads, axis=2)
     partial_value = jnp.transpose(partial_scores).reshape(node_count, capacity, expert_count)
     summed = jnp.sum(lax.all_gather(partial_value, "local", axis=0, tiled=False), axis=0)

time: 171 us -> 182 us (1.064)
  starting transfers between devices: 44.4 us -> 56 us
  blocking collectives: 17.8 us -> 13.1 us
  other arithmetic: 4.23 us -> 8.6 us
    ppermute x7, waiting for transfers between devices: 28.6 us -> 40.6 us  [on_device(): piece = lax.ppermute(piece, 'local', perm=pairs)]
    all_to_all x1, starting transfers between devices: 5.54 us -> 14.8 us  [on_device(): lax.all_to_all(summed, 'node', split_axis=0, concat_axis=0, tiled=True)]
    all_to_all x1, waiting for transfers between devices: 7.09 us -> 0.01 us  [on_device(): lax.all_to_all(payload, 'node', split_axis=0, concat_axis=0, tiled=True)]
    all_gather x1, blocking collectives: 17.8 us -> 13.1 us  [on_device(): lax.all_gather(partial_value, 'local', axis=0, tiled=False)]
    reduce_sum x0 -> x1, other arithmetic: none -> 4.36 us  [on_device(): jnp.sum(saved_full.astype(jnp.float32) * partial_grads, axis=2)]
    reduce_scatter x1, waiting for transfers between devices: 5.22 us -> 0.97 us  [on_device(): lax.psum_scatter(partial_grads, 'local', scatter_dimension=2, tiled=True)]
    ppermute x7, starting transfers between devices: 19.7 us -> 22 us  [on_device(): piece = lax.ppermute(piece, 'local', perm=pairs)]
    unnamed x13 -> x12, local copies, waits for them, and re-layouts: 3.71 us -> 1.79 us
  transfers between devices with their start and end apart: 11 -> 11, of which waited for: 7 -> 7; matrix products, arithmetic and copies ran while one was open for 15% -> 18% of each run, Pallas kernels for 0% -> 0%
where the time goes in v15:
time: 182 us; the launch traced here: 181 us
  starting transfers between devices  56 us (31%)
  waiting for transfers between devices  55.4 us (30%)
  local copies, waits for them, and re-layouts  22.4 us (12%)
  between operations  14.6 us (8%)
  blocking collectives  13.1 us (7%)
  matrix products  11 us (6%)
  other arithmetic  8.6 us (5%)
    ppermute x7, waiting for transfers between devices, on_device(): piece = lax.ppermute(piece, 'local', perm=pairs)  40.6 us
    ppermute x7, starting transfers between devices, on_device(): piece = lax.ppermute(piece, 'local', perm=pairs)  22 us
    all_to_all x1, starting transfers between devices, on_device(): lax.all_to_all(payload, 'node', split_axis=0, concat_axis=0, tiled=True)  19.1 us
    all_to_all x1, starting transfers between devices, on_device(): lax.all_to_all(summed, 'node', split_axis=0, concat_axis=0, tiled=True)  14.8 us
    all_to_all x1, waiting for transfers between devices, on_device(): lax.all_to_all(summed, 'node', split_axis=0, concat_axis=0, tiled=True)  13.8 us
    all_gather x1, blocking collectives, on_device(): lax.all_gather(partial_value, 'local', axis=0, tiled=False)  13.1 us
    dot_general x1, matrix products, on_device(): jnp.einsum('rd,ehd->erh', rows_in, weight_cols, preferred_element_type=jn...  8.57 us
    dynamic_update_slice x9, local copies, waits for them, and re-layouts, on_device(): lax.dynamic_update_slice(weight_buffer, piece[:, None], (0, block, 0, 0))  8.09 us
  transfers between devices with their start and end apart: 11, of which 7 were waited for; matrix products, arithmetic and copies ran while one was open for 18% of the time, Pallas kernels for 0%

profile of v15, /device:TPU:1, one launch (start us, length us, event | category | flops | bytes accessed | tf_op | source)
XLA Modules:
  0.0 181.1 jit_solution(7089695748764850234)
XLA Ops:
  7.2 0.8 copy.75
  8.0 0.3 convert_reduce_fusion
  8.3 0.1 copy.77
  8.3 0.2 reduce_window_sum.11
  8.5 0.1 copy.76
  8.6 0.8 copy.80
  9.5 0.3 fusion.3
  9.8 0.1 copy.81
  9.9 0.1 fusion
  10.0 0.5 convolution_convert_fusion.1
  10.6 0.1 copy.82
  10.7 0.1 copy.83
  10.9 0.5 convolution_convert_fusion
  11.4 0.8 copy.79
  12.2 0.8 reshape.40
  13.0 2.4 %pad_maximum_fusion = bf16[64,2,5388]{2,1,0:T(2,128)(2,1)} fusion(bf16[64,2,12]{2,1,0:T(2,128)(2,1)S(1)} %copy.83, bf16[64,2,5376]{2,1,0:T(2,128)(2,1)S(1)} %reshape.40), kind=kLoop, calls=%fused_computation.3 | loop fusion | flops 2758656 | bytes 2758656 | tf_op jit(solution)/shard_map/concatenate | solution.py:45
  15.4 19.1 %all-to-all-start = ((bf16[64,2,5388]{2,1,0:T(2,128)(2,1)}), bf16[64,2,5388]{2,1,0:T(2,128)(2,1)S(1)}, u32[]{:S(2)}, u32[]{:S(2)}) async-start(bf16[64,2,5388]{2,1,0:T(2,128)(2,1)} %pad_maximum_fusion), calls=%async_computation | async-start | bytes 2818048 | tf_op jit(solution)/shard_map/all_to_all | solution.py:52
  34.5 0.0 all-gather.2.cloned.1.call-start
  34.7 3.4 %constant_dynamic-slice_fusion = (bf16[2,128,896]{2,1,0:T(8,128)(2,1)}, bf16[2,128,896]{2,1,0:T(8,128)(2,1)}, bf16[2,128,896]{2,1,0:T(8,128)(2,1)}, bf16[2,128,8...) fusion(bf16[2,128,7168]{2,1,0:T(8,128)(2,1)} %param.8, ...), kind=kLoop, calls=%fused_computation.27 | loop fusion | bytes 6422556 | tf_op jit(solution)/shard_map/dynamic_slice | solution.py:61
  38.1 2.1 %collective-permute-start = (bf16[2,128,896]{2,1,0:T(8,128)(2,1)S(1)}, bf16[2,128,896]{2,1,0:T(8,128)(2,1)S(1)}, u32[]{:S(2)}, u32[]{:S(2)}) collective-permute-start(bf16[2,128,896]{2,1,0:T(8,128)(2,1)S(1)} %get-tuple-element.21), channel_id=1, source_target_pairs={{0,1},{1,2},{2,3},{3,4},{4,5},{5,6},{6,7},{7,0},{8,9},{9,10},{10,1... | collective-permute-start | bytes 1376264 | tf_op jit(solution)/shard_map/ppermute | solution.py:64
  40.3 5.4 %collective-permute-done = bf16[2,128,896]{2,1,0:T(8,128)(2,1)S(1)} collective-permute-done((bf16[2,128,896]{2,1,0:T(8,128)(2,1)S(1)}, bf16[2,128,896]{2,1,0:T(8,128)(2,1)S(1)}, u32[]{:S(2)}, u32[]{:S(2)}) %collective-permute-start) | collective-permute-done | bytes 458784 | tf_op jit(solution)/shard_map/ppermute | solution.py:64
  45.7 0.9 copy.89
  46.6 0.0 all-gather.2.cloned.1.call-update
  46.6 0.0 reduce-scatter.2.cloned.1.call-start
  46.7 3.2 %collective-permute-start.1 = (bf16[2,128,896]{2,1,0:T(8,128)(2,1)}, bf16[2,128,896]{2,1,0:T(8,128)(2,1)}, u32[]{:S(2)}, u32[]{:S(2)}) collective-permute-start(bf16[2,128,896]{2,1,0:T(8,128)(2,1)} %get-tuple-element.20), channel_id=1, source_target_pairs={{0,2},{1,3},{2,4},{3,5},{4,6},{5,7},{6,0},{7,1},{8,10},{9,11},{10,... | collective-permute-start | bytes 1376264 | tf_op jit(solution)/shard_map/ppermute | solution.py:64
  49.9 6.0 %collective-permute-start.2 = (bf16[2,128,896]{2,1,0:T(8,128)(2,1)}, bf16[2,128,896]{2,1,0:T(8,128)(2,1)}, u32[]{:S(2)}, u32[]{:S(2)}) collective-permute-start(bf16[2,128,896]{2,1,0:T(8,128)(2,1)} %get-tuple-element.19), channel_id=1, source_target_pairs={{0,3},{1,4},{2,5},{3,6},{4,7},{5,0},{6,1},{7,2},{8,11},{9,12},{10,... | collective-permute-start | bytes 1376264 | tf_op jit(solution)/shard_map/ppermute | solution.py:64
  55.9 2.3 %collective-permute-start.3 = (bf16[2,128,896]{2,1,0:T(8,128)(2,1)}, bf16[2,128,896]{2,1,0:T(8,128)(2,1)S(1)}, u32[]{:S(2)}, u32[]{:S(2)}) collective-permute-start(bf16[2,128,896]{2,1,0:T(8,128)(2,1)} %get-tuple-element.18), channel_id=1, source_target_pairs={{0,4},{1,5},{2,6},{3,7},{4,0},{5,1},{6,2},{7,3},{8,12},{9,13},{10,... | collective-permute-start | bytes 1376264 | tf_op jit(solution)/shard_map/ppermute | solution.py:64
  58.2 2.9 %collective-permute-start.4 = (bf16[2,128,896]{2,1,0:T(8,128)(2,1)}, bf16[2,128,896]{2,1,0:T(8,128)(2,1)S(1)}, u32[]{:S(2)}, u32[]{:S(2)}) collective-permute-start(bf16[2,128,896]{2,1,0:T(8,128)(2,1)} %get-tuple-element.17), channel_id=1, source_target_pairs={{0,5},{1,6},{2,7},{3,0},{4,1},{5,2},{6,3},{7,4},{8,13},{9,14},{10,... | collective-permute-start | bytes 1376264 | tf_op jit(solution)/shard_map/ppermute | solution.py:64
  61.1 3.7 %collective-permute-start.5 = (bf16[2,128,896]{2,1,0:T(8,128)(2,1)}, bf16[2,128,896]{2,1,0:T(8,128)(2,1)S(1)}, u32[]{:S(2)}, u32[]{:S(2)}) collective-permute-start(bf16[2,128,896]{2,1,0:T(8,128)(2,1)} %get-tuple-element.22), channel_id=1, source_target_pairs={{0,6},{1,7},{2,0},{3,1},{4,2},{5,3},{6,4},{7,5},{8,14},{9,15},{10,... | collective-permute-start | bytes 1376264 | tf_op jit(solution)/shard_map/ppermute | solution.py:64
  64.9 0.5 broadcast_in_dim.32
  65.4 1.1 bitcast_dynamic-update-slice_fusion.7
  66.6 0.1 bitcast_dynamic-update-slice_fusion.6
  66.6 1.8 collective-permute-start.6
  68.4 1.1 bitcast_dynamic-update-slice_fusion.5
  69.5 12.0 %collective-permute-done.2 = bf16[2,128,896]{2,1,0:T(8,128)(2,1)} collective-permute-done((bf16[2,128,896]{2,1,0:T(8,128)(2,1)}, bf16[2,128,896]{2,1,0:T(8,128)(2,1)}, u32[]{:S(2)}, u32[]{:S(2)}) %collective-permute-start.2) | collective-permute-done | bytes 458784 | tf_op jit(solution)/shard_map/ppermute | solution.py:64
  81.5 1.1 bitcast_dynamic-update-slice_fusion.4
  82.5 7.0 %collective-permute-done.3 = bf16[2,128,896]{2,1,0:T(8,128)(2,1)S(1)} collective-permute-done((bf16[2,128,896]{2,1,0:T(8,128)(2,1)}, bf16[2,128,896]{2,1,0:T(8,128)(2,1)S(1)}, u32[]{:S(2)}, u32[]{:S(2)}) %collective-permute-start.3) | collective-permute-done | bytes 458784 | tf_op jit(solution)/shard_map/ppermute | solution.py:64
  89.6 2.2 %copy.85 = bf16[2,8,128,896]{3,2,1,0:T(8,128)(2,1)} copy(bf16[2,8,128,896]{3,2,0,1:T(8,128)(2,1)S(1)} %bitcast_dynamic-update-slice_fusion.3) | data formatting | bytes 7340032 | tf_op jit(solution)/shard_map/dynamic_update_slice | solution.py:68
  91.8 7.9 %collective-permute-done.4 = bf16[2,128,896]{2,1,0:T(8,128)(2,1)S(1)} collective-permute-done((bf16[2,128,896]{2,1,0:T(8,128)(2,1)}, bf16[2,128,896]{2,1,0:T(8,128)(2,1)S(1)}, u32[]{:S(2)}, u32[]{:S(2)}) %collective-permute-start.4) | collective-permute-done | bytes 458784 | tf_op jit(solution)/shard_map/ppermute | solution.py:64
  99.7 0.9 bitcast_dynamic-update-slice_fusion.2
  100.6 8.3 %collective-permute-done.5 = bf16[2,128,896]{2,1,0:T(8,128)(2,1)S(1)} collective-permute-done((bf16[2,128,896]{2,1,0:T(8,128)(2,1)}, bf16[2,128,896]{2,1,0:T(8,128)(2,1)S(1)}, u32[]{:S(2)}, u32[]{:S(2)}) %collective-permute-start.5) | collective-permute-done | bytes 458784 | tf_op jit(solution)/shard_map/ppermute | solution.py:64
  108.8 0.8 bitcast_dynamic-update-slice_fusion.1
  109.6 0.9 bitcast_dynamic-update-slice_fusion
  110.5 0.9 slice.9
  111.4 1.8 reshape.48
  113.2 8.6 %convolution_bitcast_fusion = f32[2,768,1024]{1,2,0:T(8,128)} fusion(bf16[2,1024,896]{2,1,0:T(8,128)(2,1)} %bitcast.14, bf16[768,896,1]{1,0,2:T(8,128)(2,1)} %reshape.48), kind=kOutput, calls=%fused_computation.1 | convolution fusion | flops 2818572288 | bytes 11337728 | tf_op jit(solution)/shard_map/rd,ehd->erh/dot_general | solution.py:70
  121.8 0.0 all-gather.2.cloned.1.call-done
  121.8 4.4 %multiply_reduce_fusion = f32[2,768]{1,0:T(2,128)S(1)} fusion(f32[2,768,1024]{1,2,0:T(8,128)} %convolution_bitcast_fusion, bf16[2,768,1024]{1,2,0:T(8,128)(2,1)} %all-gather.2.cloned.1.call-done), kind=kLoop, calls=%fused_computation | loop fusion | flops 4717056 | bytes 9443328 | tf_op jit(solution)/shard_map/reduce_sum | solution.py:77
  126.2 0.1 all_gather_reshape.3
  126.3 0.1 copy.90
  126.4 13.1 %all_gather.7 = f32[8,64,12,2]{1,3,2,0:T(2,128)S(1)} all-gather(f32[1,64,12,2]{1,3,2,0:T(2,128)S(1)} %copy.90), channel_id=1, replica_groups=mesh['node'=64,'local'=8] {'local'}, dimensions={0}, use_global_device_ids=true | all-gather | bytes 55296 | tf_op jit(solution)/shard_map/all_gather | solution.py:79
  139.6 0.1 reduce_sum.29
  139.6 0.7 copy.92
  140.3 14.8 %all-to-all-start.1 = ((f32[64,12,2]{1,2,0:T(2,128)}), f32[64,12,2]{1,2,0:T(2,128)S(1)}, u32[]{:S(2)}, u32[]{:S(2)}) async-start(f32[64,12,2]{1,2,0:T(2,128)} %copy.92), calls=%async_computation.2 | async-start | bytes 131072 | tf_op jit(solution)/shard_map/all_to_all | solution.py:83
  155.2 0.2 reshape.46
  155.4 0.1 copy.84
  155.5 13.8 %all-to-all-done.1 = f32[64,12,2]{1,2,0:T(2,128)S(1)} async-done(((f32[64,12,2]{1,2,0:T(2,128)}), f32[64,12,2]{1,2,0:T(2,128)S(1)}, u32[]{:S(2)}, u32[]{:S(2)}) %all-to-all-start.1) | async-done | bytes 6176 | tf_op jit(solution)/shard_map/all_to_all | solution.py:83
  169.3 0.4 convolution_bitcast_fusion.1
  169.8 0.1 copy.93
  169.9 0.6 fusion.2
  170.5 0.7 copy.94
  171.2 1.0 reduce-scatter.2.cloned.1.call-done
  172.2 1.2 multiply_convert_fusion
  173.4 0.9 copy.95
  (19 shorter events, 0.2 us)
Async XLA Ops:
  7.2 3.7 %copy-start = (bf16[128,896]{1,0:T(8,128)(2,1)S(1)}, bf16[128,896]{1,0:T(8,128)(2,1)}, u32[]{:S(2)}) copy-start(bf16[128,896]{1,0:T(8,128)(2,1)} %param.5) | copy-start | bytes 688132
  8.6 2.1 %copy-start.3 = (s32[128,64]{0,1:T(8,128)}, s32[128,64]{0,1:T(8,128)S(1)}, u32[]{:S(2)}) copy-start(s32[128,64]{0,1:T(8,128)S(1)} %copy.76) | copy-start | bytes 98308
  15.4 95.1 %all-to-all-start = ((bf16[64,2,5388]{2,1,0:T(2,128)(2,1)}), bf16[64,2,5388]{2,1,0:T(2,128)(2,1)S(1)}, u32[]{:S(2)}, u32[]{:S(2)}) async-start(bf16[64,2,5388]{2,1,0:T(2,128)(2,1)} %pad_maximum_fusion), calls=%async_computation | async-start | bytes 2818048 | tf_op jit(solution)/shard_map/all_to_all | solution.py:52
  34.5 11.2 %copy-start.2 = (bf16[2,768,128]{2,1,0:T(8,128)(2,1)S(1)}, bf16[2,768,128]{2,1,0:T(8,128)(2,1)}, u32[]{:S(2)}) copy-start(bf16[2,768,128]{2,1,0:T(8,128)(2,1)} %param.9) | copy-start | bytes 1179652
  34.5 87.3 %all-gather.2.cloned.1.call-start = ((), (), s32[]{:S(2)}) async-start(), calls=%async_computation.4 | async-start | bytes 3538944 | tf_op jit(solution)/shard_map/all_gather | solution.py:76
  38.1 7.6 %collective-permute-start = (bf16[2,128,896]{2,1,0:T(8,128)(2,1)S(1)}, bf16[2,128,896]{2,1,0:T(8,128)(2,1)S(1)}, u32[]{:S(2)}, u32[]{:S(2)}) collective-permute-start(bf16[2,128,896]{2,1,0:T(8,128)(2,1)S(1)} %get-tuple-element.21), channel_id=1, source_target_pairs={{0,1},{1,2},{2,3},{3,4},{4,5},{5,6},{6,7},{7,0},{8,9},{9,10},{10,1... | collective-permute-start | bytes 1376264 | tf_op jit(solution)/shard_map/ppermute | solution.py:64
  46.6 125.5 %reduce-scatter.2.cloned.1.call-start = ((), (), s32[]{:S(2)}) async-start(), calls=%async_computation.3 | async-start | bytes 7077888 | tf_op jit(solution)/shard_map/reduce_scatter | solution.py:80
  46.7 19.9 %collective-permute-start.1 = (bf16[2,128,896]{2,1,0:T(8,128)(2,1)}, bf16[2,128,896]{2,1,0:T(8,128)(2,1)}, u32[]{:S(2)}, u32[]{:S(2)}) collective-permute-start(bf16[2,128,896]{2,1,0:T(8,128)(2,1)} %get-tuple-element.20), channel_id=1, source_target_pairs={{0,2},{1,3},{2,4},{3,5},{4,6},{5,7},{6,0},{7,1},{8,10},{9,11},{10,... | collective-permute-start | bytes 1376264 | tf_op jit(solution)/shard_map/ppermute | solution.py:64
  49.9 31.6 %collective-permute-start.2 = (bf16[2,128,896]{2,1,0:T(8,128)(2,1)}, bf16[2,128,896]{2,1,0:T(8,128)(2,1)}, u32[]{:S(2)}, u32[]{:S(2)}) collective-permute-start(bf16[2,128,896]{2,1,0:T(8,128)(2,1)} %get-tuple-element.19), channel_id=1, source_target_pairs={{0,3},{1,4},{2,5},{3,6},{4,7},{5,0},{6,1},{7,2},{8,11},{9,12},{10,... | collective-permute-start | bytes 1376264 | tf_op jit(solution)/shard_map/ppermute | solution.py:64
  55.9 33.7 %collective-permute-start.3 = (bf16[2,128,896]{2,1,0:T(8,128)(2,1)}, bf16[2,128,896]{2,1,0:T(8,128)(2,1)S(1)}, u32[]{:S(2)}, u32[]{:S(2)}) collective-permute-start(bf16[2,128,896]{2,1,0:T(8,128)(2,1)} %get-tuple-element.18), channel_id=1, source_target_pairs={{0,4},{1,5},{2,6},{3,7},{4,0},{5,1},{6,2},{7,3},{8,12},{9,13},{10,... | collective-permute-start | bytes 1376264 | tf_op jit(solution)/shard_map/ppermute | solution.py:64
  58.2 41.5 %collective-permute-start.4 = (bf16[2,128,896]{2,1,0:T(8,128)(2,1)}, bf16[2,128,896]{2,1,0:T(8,128)(2,1)S(1)}, u32[]{:S(2)}, u32[]{:S(2)}) collective-permute-start(bf16[2,128,896]{2,1,0:T(8,128)(2,1)} %get-tuple-element.17), channel_id=1, source_target_pairs={{0,5},{1,6},{2,7},{3,0},{4,1},{5,2},{6,3},{7,4},{8,13},{9,14},{10,... | collective-permute-start | bytes 1376264 | tf_op jit(solution)/shard_map/ppermute | solution.py:64
  61.1 47.7 %collective-permute-start.5 = (bf16[2,128,896]{2,1,0:T(8,128)(2,1)}, bf16[2,128,896]{2,1,0:T(8,128)(2,1)S(1)}, u32[]{:S(2)}, u32[]{:S(2)}) collective-permute-start(bf16[2,128,896]{2,1,0:T(8,128)(2,1)} %get-tuple-element.22), channel_id=1, source_target_pairs={{0,6},{1,7},{2,0},{3,1},{4,2},{5,3},{6,4},{7,5},{8,14},{9,15},{10,... | collective-permute-start | bytes 1376264 | tf_op jit(solution)/shard_map/ppermute | solution.py:64
  64.9 1.7 copy-start.1
  66.6 43.0 %collective-permute-start.6 = (bf16[2,128,896]{2,1,0:T(8,128)(2,1)S(1)}, bf16[2,128,896]{2,1,0:T(8,128)(2,1)S(1)}, u32[]{:S(2)}, u32[]{:S(2)}) collective-permute-start(bf16[2,128,896]{2,1,0:T(8,128)(2,1)S(1)} %copy-done.1), channel_id=1, source_target_pairs={{0,7},{1,0},{2,1},{3,2},{4,3},{5,4},{6,5},{7,6},{8,15},{9,8},{10,9... | collective-permute-start | bytes 1376264 | tf_op jit(solution)/shard_map/ppermute | solution.py:64
  121.8 47.5 %copy-start.4 = (s32[128,64]{0,1:T(8,128)S(1)}, s32[128,64]{0,1:T(8,128)}, u32[]{:S(2)}) copy-start(s32[128,64]{0,1:T(8,128)} %copy-done.3) | copy-start | bytes 98308
  140.3 29.0 %all-to-all-start.1 = ((f32[64,12,2]{1,2,0:T(2,128)}), f32[64,12,2]{1,2,0:T(2,128)S(1)}, u32[]{:S(2)}, u32[]{:S(2)}) async-start(f32[64,12,2]{1,2,0:T(2,128)} %copy.92), calls=%async_computation.2 | async-start | bytes 131072 | tf_op jit(solution)/shard_map/all_to_all | solution.py:83
Sparse Core Ops, SparseCore 0:
  46.8 56.8 all-gather.1
  121.9 50.1 reduce-scatter.1
